TPU v7x, 32 devices: a whole 2x2x4 slice. The times are simulated.
32 devices in a mesh: arrays: 2 (over y), elem: 4 (over z), gate: 2 (over x), pol: 2 (over core).
Axes of the slice: x: 2, y: 2, z: 4, core: 2. Of those that a mesh axis runs over, the one named last changes fastest.
Arguments:
- signal: bfloat16 [4, 2, 16384, 1024], P('arrays', 'pol', 'elem', 'gate'), parts along dimension 0, may hold values from -170 to 170
- weights: bfloat16 [4, 2, 1024, 16384], P('arrays', 'pol', None, 'elem'), parts along dimension 0, may hold values from -0.0625 to 0.0625
Outputs:
- moments: float32 [4, 4, 1024, 16], P(None, ('arrays', 'pol'), 'elem', 'gate'), parts along dimension 1
- polar: float32 [2, 2048, 16], P('pol', ('arrays', 'elem'), 'gate'), parts along dimension 1
There are 2 independent parts, one for each index of `arrays`. A program takes and returns all parts, laid end to end along the dimension named above; each array names one. Nothing has to cross between parts.
All inputs are finite; a program needn't handle non-finite values.
Results may differ from a plain program's by a relative error of at most 0.0003.
Values sent between devices are 32-bit elements; how exact they have to be, the bound alone decides.
No kernel may reach another device: no remote copies, remote signals or barrier semaphores. Data moves between devices by JAX's collectives and lax.ppermute only.
A program may use at most 128 MiB of HBM per device.

v0:
```python
import jax
import jax.numpy as jnp
from jax import lax
from jax.sharding import PartitionSpec as P

PULSES = 64


def swapped(value, axis, bit):
    mask = 2**bit
    pairs = [(source, source ^ mask) for source in range(lax.axis_size(axis))]
    return lax.ppermute(value, axis, pairs)


def with_halo(block, sides, width):
    for axis, dim in sides:
        count = lax.axis_size(axis)
        forward = [(i, i + 1) for i in range(count - 1)]
        backward = [(target, source) for source, target in forward]
        low = lax.ppermute(
            lax.slice_in_dim(block, block.shape[dim] - width, None, axis=dim), axis, forward
        )
        high = lax.ppermute(lax.slice_in_dim(block, 0, width, axis=dim), axis, backward)
        block = jnp.concatenate([low, block, high], axis=dim)
    return block


def project(stacked_w, columns, count):
    block = stacked_w.shape[2]
    chosen = stacked_w.reshape(2 * count, block)
    product = jnp.dot(chosen, columns, preferred_element_type=jnp.float32)
    width = columns.shape[1] // 2
    real = product[:count, :width] + product[count:, width:]
    imag = product[:count, width:] - product[count:, :width]
    return jnp.concatenate([real, imag], axis=1)


def lag_stats(real, imag):
    zero_lag = jnp.mean(real * real + imag * imag, axis=-1)
    lag_re = jnp.sum(real[..., :-1] * real[..., 1:] + imag[..., :-1] * imag[..., 1:], axis=-1) / (
        PULSES - 1
    )
    lag_im = jnp.sum(real[..., :-1] * imag[..., 1:] - imag[..., :-1] * real[..., 1:], axis=-1) / (
        PULSES - 1
    )
    return (zero_lag, lag_re, lag_im)


def pair_stats(first, second):
    power_h = jnp.mean(first[0] * first[0] + first[1] * first[1], axis=-1)
    power_v = jnp.mean(second[0] * second[0] + second[1] * second[1], axis=-1)
    cross_re = jnp.mean(first[0] * second[0] + first[1] * second[1], axis=-1)
    cross_im = jnp.mean(first[0] * second[1] - first[1] * second[0], axis=-1)
    return (power_h, power_v, cross_re, cross_im)


def on_device(signal, weights):
    n_elem = lax.axis_size("elem")
    samples = signal.shape[3]
    gates = samples // PULSES
    local = weights.shape[2] // n_elem
    stacked_w = weights[:, 0]
    columns = jnp.concatenate([signal[0, 0], signal[1, 0]], axis=1)
    summed = lax.psum_scatter(
        project(stacked_w, columns, lax.axis_size("elem") * local),
        "elem",
        scatter_dimension=0,
        tiled=True,
    )
    real = summed[:, :samples].reshape(local, gates, PULSES)
    imag = summed[:, samples:].reshape(local, gates, PULSES)
    zero_lag, lag_re, lag_im = lag_stats(real, imag)
    series = jnp.stack([real, imag])
    pol_index = lax.axis_index("pol")
    other = swapped(series, "pol", 0)
    first = jnp.where(pol_index == 0, series, other)
    second = jnp.where(pol_index == 0, other, series)
    pair = jnp.stack(pair_stats(first, second))
    stats = jnp.concatenate([jnp.stack([zero_lag, lag_re, lag_im]), pair], axis=0)
    padded = with_halo(stats, (("gate", 2),), 1)
    smoothed = (padded[..., :-2] + 2.0 * padded[..., 1:-1] + padded[..., 2:]) * 0.25
    power = smoothed[0]
    magnitude = jnp.sqrt(smoothed[1] * smoothed[1] + smoothed[2] * smoothed[2])
    floor_mag = jnp.maximum(magnitude, 0.25 * power)
    moments = jnp.stack(
        [
            10.0 * jnp.log10(power + 1e-06),
            smoothed[1] / floor_mag,
            smoothed[2] / floor_mag,
            jnp.log(power / floor_mag),
        ]
    )
    zdr = 10.0 * jnp.log10((smoothed[3] + 1e-06) / (smoothed[4] + 1e-06))
    corr = jnp.sqrt(smoothed[5] * smoothed[5] + smoothed[6] * smoothed[6]) / jnp.sqrt(
        smoothed[3] * smoothed[4]
    )
    polar = jnp.where(pol_index == 0, zdr, corr)
    return (moments[:, None], polar[None])


def solution(mesh):
    return jax.shard_map(
        on_device,
        mesh=mesh,
        in_specs=(P("arrays", "pol", "elem", "gate"), P("arrays", "pol", None, "elem")),
        out_specs=(
            P(None, ("arrays", "pol"), "elem", "gate"),
            P("pol", ("arrays", "elem"), "gate"),
        ),
        check_vma=False,
    )
```

profile of v0, /device:TPU:0, one launch (start us, length us, event | category | flops | bytes accessed | tf_op | source)
XLA Modules:
  0.0 139.8 jit_solution(7181890280487918561)
XLA Ops:
  7.2 0.0 reduce-scatter.2.cloned.1.call-start
  7.2 5.0 %slice_bitcast_fusion.1 = (bf16[4096,512]{1,0:T(8,128)(2,1)S(1)}, bf16[4096,512]{1,0:T(8,128)(2,1)}) fusion(bf16[2,1,4096,512]{3,2,1,0:T(8,128)(2,1)} %param.2), kind=kLoop, calls=%fused_computation.7 | loop fusion | bytes 16777216 | tf_op jit(solution)/shard_map/squeeze | solution.py:63
  12.3 21.7 %fusion.4 = f32[2048,1024]{0,1:T(8,128)S(1)} fusion(bf16[2048,4096]{1,0:T(8,128)(2,1)} %bitcast.36, bf16[4096,512]{1,0:T(8,128)(2,1)} %get-tuple-element.13, bf16[4096,512]{1,0:T(8,128)(2,1)S(1)} %get-tuple-element.12), kind=kOutput, calls=%fused_computation.4 | convolution fusion | flops 17196646400 | bytes 33554432 | tf_op jit(solution)/shard_map/dot_general | solution.py:31
  33.9 0.9 slice_add_fusion
  34.9 2.2 %pad_maximum_fusion = f32[1024,1024]{0,1:T(8,128)} fusion(f32[1024,512]{0,1:T(8,128)S(1)} %get-tuple-element.11, f32[1024,512]{0,1:T(8,128)S(1)} %get-tuple-element.10), kind=kLoop, calls=%fused_computation.5 | loop fusion | flops 1048576 | bytes 8388608 | tf_op jit(solution)/shard_map/concatenate | solution.py:35
  37.1 0.0 reduce-scatter.2.cloned.1.call-update
  37.1 79.7 %reduce-scatter.2.cloned.1.call-done = f32[256,1024]{0,1:T(8,128)} async-done(((f32[1024,1024]{0,1:T(8,128)}), f32[256,1024]{0,1:T(8,128)}) %reduce-scatter.2.cloned.1.call-update) | async-done | bytes 1048592 | tf_op jit(solution)/shard_map/reduce_scatter | solution.py:64
  116.8 0.0 copy-start
  116.8 1.4 fusion.15
  118.2 1.1 pad_maximum_fusion.1
  119.3 0.0 collective-permute-start
  119.3 0.0 copy-done
  119.3 0.1 add_reduce_fusion.4
  119.4 0.2 subtract_reduce_fusion.1
  119.6 2.5 %collective-permute-done = f32[2,256,8,64]{1,3,2,0:T(8,128)S(1)} collective-permute-done((f32[2,256,8,64]{1,3,2,0:T(8,128)}, f32[2,256,8,64]{1,3,2,0:T(8,128)S(1)}, u32[]{:S(2)}, u32[]{:S(2)}) %collective-permute-start) | collective-permute-done | bytes 1048608 | tf_op jit(solution)/shard_map/ppermute | solution.py:12
  122.1 0.2 broadcast_select_fusion.1
  122.3 0.3 subtract_reduce_fusion
  122.7 3.4 %collective-permute-start.1 = (f32[7,256,1]{1,2,0:T(1,128)S(1)}, f32[7,256,1]{1,2,0:T(1,128)S(1)}, u32[]{:S(2)}, u32[]{:S(2)}) collective-permute-start(f32[7,256,1]{1,2,0:T(1,128)S(1)} %get-tuple-element.22), channel_id=1, source_target_pairs={{0,2},{1,3},{4,6},{5,7},{8,10},{9,11},{12,14},{13,15},{16,18},{17,... | collective-permute-start | bytes 21512 | tf_op jit(solution)/shard_map/ppermute | solution.py:20
  126.1 1.3 collective-permute-start.2
  127.4 0.0 collective-permute-done.1
  127.4 4.2 %collective-permute-done.2 = f32[7,256,1]{1,2,0:T(1,128)S(1)} collective-permute-done((f32[7,256,1]{1,2,0:T(1,128)S(1)}, f32[7,256,1]{1,2,0:T(1,128)S(1)}, u32[]{:S(2)}, u32[]{:S(2)}) %collective-permute-start.2) | collective-permute-done | bytes 7200 | tf_op jit(solution)/shard_map/ppermute | solution.py:23
  131.7 0.6 slice_divide_fusion
  132.3 0.6 maximum_bitcast_fusion
  (10 shorter events, 0.1 us)
Async XLA Ops:
  7.2 109.6 %reduce-scatter.2.cloned.1.call-start = ((), (), s32[]{:S(2)}) async-start(), calls=%async_computation.1 | async-start | bytes 5242880 | tf_op jit(solution)/shard_map/reduce_scatter | solution.py:64
  116.8 2.5 %copy-start = (f32[256,1024]{0,1:T(8,128)S(1)}, f32[256,1024]{0,1:T(8,128)}, u32[]{:S(2)}) copy-start(f32[256,1024]{0,1:T(8,128)} %reduce-scatter.2.cloned.1.call-done) | copy-start | bytes 3145732
  119.3 2.9 %collective-permute-start = (f32[2,256,8,64]{1,3,2,0:T(8,128)}, f32[2,256,8,64]{1,3,2,0:T(8,128)S(1)}, u32[]{:S(2)}, u32[]{:S(2)}) collective-permute-start(f32[2,256,8,64]{1,3,2,0:T(8,128)} %pad_maximum_fusion.1), channel_id=1, source_target_pairs={{0,1},{1,0},{2,3},{3,2},{4,5},{5,4},{6,7},{7,6},{8,9},{9,8},{10,11... | collective-permute-start | bytes 3145736 | tf_op jit(solution)/shard_map/ppermute | solution.py:12
  122.7 4.7 %collective-permute-start.1 = (f32[7,256,1]{1,2,0:T(1,128)S(1)}, f32[7,256,1]{1,2,0:T(1,128)S(1)}, u32[]{:S(2)}, u32[]{:S(2)}) collective-permute-start(f32[7,256,1]{1,2,0:T(1,128)S(1)} %get-tuple-element.22), channel_id=1, source_target_pairs={{0,2},{1,3},{4,6},{5,7},{8,10},{9,11},{12,14},{13,15},{16,18},{17,... | collective-permute-start | bytes 21512 | tf_op jit(solution)/shard_map/ppermute | solution.py:20
  126.1 5.5 %collective-permute-start.2 = (f32[7,256,1]{1,2,0:T(1,128)S(1)}, f32[7,256,1]{1,2,0:T(1,128)S(1)}, u32[]{:S(2)}, u32[]{:S(2)}) collective-permute-start(f32[7,256,1]{1,2,0:T(1,128)S(1)} %get-tuple-element.23), channel_id=1, source_target_pairs={{2,0},{3,1},{6,4},{7,5},{10,8},{11,9},{14,12},{15,13},{18,16},{19,... | collective-permute-start | bytes 21512 | tf_op jit(solution)/shard_map/ppermute | solution.py:23
Sparse Core Ops, SparseCore 0:
  37.3 79.5 reduce-scatter.1
where the time goes:
time: 140 us
  waiting for transfers between devices  86.4 us (62%)
  matrix products  21.7 us (16%)
  between operations  14.2 us (10%)
  local copies, waits for them, and re-layouts  6.42 us (5%)
  other arithmetic  6.39 us (5%)
  starting transfers between devices  4.7 us (3%)
    reduce_scatter x1, waiting for transfers between devices, on_device(): lax.psum_scatter(project(stacked_w, columns, lax.axis_size('elem') * loca...  79.7 us
    dot_general x1, matrix products, project(): product = jnp.dot(chosen, columns, preferred_element_type=jnp.float32)  21.7 us
    squeeze x1, local copies, waits for them, and re-layouts, on_device(): columns = jnp.concatenate([signal[0, 0], signal[1, 0]], axis=1)  5.04 us
    ppermute x1, waiting for transfers between devices, with_halo(): lax.ppermute(lax.slice_in_dim(block, 0, width, axis=dim), axis, backward)  4.19 us
    ppermute x1, starting transfers between devices, with_halo(): lax.ppermute(lax.slice_in_dim(block, block.shape[dim] - width, None, axis...  3.36 us
  transfers between devices with their start and end apart: 4, of which 3 were waited for; matrix products, arithmetic and copies ran while one was open for 0% of the time, Pallas kernels for 0%

commit v1 on v0

v1 whole, which is shorter than its diff:
```python
import jax
import jax.numpy as jnp
from jax import lax
from jax.sharding import PartitionSpec as P

PULSES = 64
CHUNKS = 4


def swapped(value, axis, bit):
    mask = 2**bit
    pairs = [(source, source ^ mask) for source in range(lax.axis_size(axis))]
    return lax.ppermute(value, axis, pairs)


def with_halo(block, axis, dim):
    count = lax.axis_size(axis)
    first = lax.slice_in_dim(block, 0, 1, axis=dim)
    last = lax.slice_in_dim(block, block.shape[dim] - 1, None, axis=dim)
    index = lax.axis_index(axis)
    if count == 2:
        sent = jnp.where(index == 0, last, first)
        got = lax.ppermute(sent, axis, [(0, 1), (1, 0)])
        zero = jnp.zeros_like(got)
        low = jnp.where(index == 0, zero, got)
        high = jnp.where(index == 0, got, zero)
    else:
        forward = [(i, i + 1) for i in range(count - 1)]
        backward = [(target, source) for source, target in forward]
        low = lax.ppermute(last, axis, forward)
        high = lax.ppermute(first, axis, backward)
    return jnp.concatenate([low, block, high], axis=dim)


def lag_stats(real, imag):
    zero_lag = jnp.mean(real * real + imag * imag, axis=-1)
    lag_re = jnp.sum(real[..., :-1] * real[..., 1:] + imag[..., :-1] * imag[..., 1:], axis=-1) / (
        PULSES - 1
    )
    lag_im = jnp.sum(real[..., :-1] * imag[..., 1:] - imag[..., :-1] * real[..., 1:], axis=-1) / (
        PULSES - 1
    )
    return (zero_lag, lag_re, lag_im)


def pair_stats(first, second):
    power_h = jnp.mean(first[0] * first[0] + first[1] * first[1], axis=-1)
    power_v = jnp.mean(second[0] * second[0] + second[1] * second[1], axis=-1)
    cross_re = jnp.mean(first[0] * second[0] + first[1] * second[1], axis=-1)
    cross_im = jnp.mean(first[0] * second[1] - first[1] * second[0], axis=-1)
    return (power_h, power_v, cross_re, cross_im)


def chunk_stats(summed, gates):
    count = summed.shape[1]
    real = summed[0].reshape(count, gates, PULSES)
    imag = summed[1].reshape(count, gates, PULSES)
    zero_lag, lag_re, lag_im = lag_stats(real, imag)
    series = jnp.stack([real, imag])
    pol_index = lax.axis_index("pol")
    other = swapped(series, "pol", 0)
    first = jnp.where(pol_index == 0, series, other)
    second = jnp.where(pol_index == 0, other, series)
    pair = jnp.stack(pair_stats(first, second))
    return jnp.concatenate([jnp.stack([zero_lag, lag_re, lag_im]), pair], axis=0)


def on_device(signal, weights):
    n_elem = lax.axis_size("elem")
    samples = signal.shape[3]
    gates = samples // PULSES
    beams = weights.shape[2]
    elems = weights.shape[3]
    local = beams // n_elem
    chunks = CHUNKS
    while chunks > 1 and local % (chunks * 8):
        chunks //= 2
    per = local // chunks
    w = weights[:, 0].reshape(2, n_elem, chunks, per, elems)
    x_re = signal[0, 0]
    x_im = signal[1, 0]
    parts = []
    for j in range(chunks):
        rows = w[:, :, j].reshape(2 * n_elem * per, elems)
        p_re = jnp.dot(rows, x_re, preferred_element_type=jnp.float32).reshape(2, n_elem * per, samples)
        p_im = jnp.dot(rows, x_im, preferred_element_type=jnp.float32).reshape(2, n_elem * per, samples)
        combined = jnp.stack([p_re[0] + p_im[1], p_im[0] - p_re[1]])
        summed = lax.psum_scatter(combined, "elem", scatter_dimension=1, tiled=True)
        parts.append(chunk_stats(summed, gates))
    stats = jnp.concatenate(parts, axis=1)
    padded = with_halo(stats, "gate", 2)
    smoothed = (padded[..., :-2] + 2.0 * padded[..., 1:-1] + padded[..., 2:]) * 0.25
    power = smoothed[0]
    magnitude = jnp.sqrt(smoothed[1] * smoothed[1] + smoothed[2] * smoothed[2])
    floor_mag = jnp.maximum(magnitude, 0.25 * power)
    moments = jnp.stack(
        [
            10.0 * jnp.log10(power + 1e-06),
            smoothed[1] / floor_mag,
            smoothed[2] / floor_mag,
            jnp.log(power / floor_mag),
        ]
    )
    zdr = 10.0 * jnp.log10((smoothed[3] + 1e-06) / (smoothed[4] + 1e-06))
    corr = jnp.sqrt(smoothed[5] * smoothed[5] + smoothed[6] * smoothed[6]) / jnp.sqrt(
        smoothed[3] * smoothed[4]
    )
    pol_index = lax.axis_index("pol")
    polar = jnp.where(pol_index == 0, zdr, corr)
    return (moments[:, None], polar[None])


def solution(mesh):
    return jax.shard_map(
        on_device,
        mesh=mesh,
        in_specs=(P("arrays", "pol", "elem", "gate"), P("arrays", "pol", None, "elem")),
        out_specs=(
            P(None, ("arrays", "pol"), "elem", "gate"),
            P("pol", ("arrays", "elem"), "gate"),
        ),
        check_vma=False,
    )
```

time: 140 us -> 162 us (1.16)
  matrix products: 21.7 us -> 36.1 us
  local copies, waits for them, and re-layouts: 6.42 us -> 20.4 us
  waiting for transfers between devices: 86.4 us -> 75.3 us
  other arithmetic: 6.39 us -> 11.9 us
    dot_general x1 -> x8, matrix products: 21.7 us -> 36.1 us  [the longest x4 18.7 us: on_device(): jnp.dot(rows, x_re, preferred_element_type=jnp.float32)]
    slice x2 -> x5, local copies, waits for them, and re-layouts: 1.37 us -> 15.5 us  [the longest x1 11.6 us: on_device(): rows = w[:, :, j].reshape(2 * n_elem * per, elems)]
    reduce_scatter x1 -> x4, waiting for transfers between devices: 79.7 us -> 72.6 us  [on_device(): summed = lax.psum_scatter(combined, 'elem', scatter_dimension=1, tiled=True)]
    squeeze x1 -> x0, local copies, waits for them, and re-layouts: 5.04 us -> none  [on_device(): columns = jnp.concatenate([signal[0, 0], signal[1, 0]], axis=1)]
    another operation x1 -> x4, other arithmetic: 1.09 us -> 4.35 us  [on_device(): combined = jnp.stack([p_re[0] + p_im[1], p_im[0] - p_re[1]])]
    ppermute x2 -> x1, starting transfers between devices: 4.66 us -> 1.55 us  [with_halo(): got = lax.ppermute(sent, axis, [(0, 1), (1, 0)])]
    concatenate x2 -> x1, other arithmetic: 2.24 us -> 0.09 us  [on_device(): stats = jnp.concatenate(parts, axis=1)]
    ppermute x2 -> x1, waiting for transfers between devices: 4.23 us -> 2.15 us  [with_halo(): got = lax.ppermute(sent, axis, [(0, 1), (1, 0)])]
  transfers between devices with their start and end apart: 4 -> 9, of which waited for: 3 -> 5; matrix products, arithmetic and copies ran while one was open for 0% -> 28% of each run, Pallas kernels for 0% -> 0%
where the time goes in v1:
time: 162 us; the launch traced here: 161 us
  waiting for transfers between devices  75.3 us (46%)
  matrix products  36.1 us (22%)
  local copies, waits for them, and re-layouts  20.4 us (13%)
  between operations  14.4 us (9%)
  other arithmetic  11.9 us (7%)
  starting transfers between devices  3.16 us (2%)
    reduce_scatter x4, waiting for transfers between devices, on_device(): summed = lax.psum_scatter(combined, 'elem', scatter_dimension=1, tiled=True)  72.6 us
    dot_general x4, matrix products, on_device(): jnp.dot(rows, x_re, preferred_element_type=jnp.float32)  18.7 us
    dot_general x4, matrix products, on_device(): jnp.dot(rows, x_im, preferred_element_type=jnp.float32)  17.4 us
    slice x1, local copies, waits for them, and re-layouts, on_device(): rows = w[:, :, j].reshape(2 * n_elem * per, elems)  11.6 us
    another operation x4, other arithmetic, on_device(): combined = jnp.stack([p_re[0] + p_im[1], p_im[0] - p_re[1]])  4.35 us
    slice x4, local copies, waits for them, and re-layouts, chunk_stats(): real = summed[0].reshape(count, gates, PULSES)  3.96 us
  transfers between devices with their start and end apart: 9, of which 5 were waited for; matrix products, arithmetic and copies ran while one was open for 28% of the time, Pallas kernels for 0%

profile of v1, /device:TPU:0, one launch (start us, length us, event | category | flops | bytes accessed | tf_op | source)
XLA Modules:
  0.0 161.3 jit_solution(14544279651131181252)
XLA Ops:
  7.2 11.6 %fusion.39 = (bf16[2,4,1,64,4096]{4,3,2,1,0:T(8,128)(2,1)S(1)}, bf16[2,4,1,64,4096]{4,3,2,1,0:T(8,128)(2,1)}, bf16[2,4,1,64,4096]{4,3,2,1,0:T(8,128)(2,1)}, bf16[2,4,1,64,4096]{4,3,2,1,0:T(8,128)(2,1)}) fusion(bf16[2,4,4,64,4096]{4,3,2,1,0:T(8,128)(2,1)} %bitcast.107), kind=kLoop, calls=%fused_computation.171 | loop fusion | bytes 33554432 | tf_op jit(solution)/shard_map/slice | solution.py:84
  18.8 1.1 copy-done.3
  19.9 2.3 %fusion.14 = f32[512,512]{1,0:T(8,128)S(1)} fusion(bf16[512,4096]{1,0:T(8,128)(2,1)S(1)} %bitcast.114, bf16[2,1,4096,512]{3,2,1,0:T(8,128)(2,1)S(1)} %copy-done.3), kind=kOutput, calls=%fused_computation.14 | convolution fusion | flops 2147483648 | bytes 9437184 | tf_op jit(solution)/shard_map/dot_general | solution.py:85
  22.2 2.3 %fusion.6 = f32[512,512]{1,0:T(8,128)S(1)} fusion(bf16[512,4096]{1,0:T(8,128)(2,1)S(1)} %bitcast.115, bf16[2,1,4096,512]{3,2,1,0:T(8,128)(2,1)S(1)} %copy-done.3), kind=kOutput, calls=%fused_computation.6 | convolution fusion | flops 2147483648 | bytes 9437184 | tf_op jit(solution)/shard_map/dot_general | solution.py:86
  24.7 1.1 pad_maximum_fusion
  25.9 5.9 %fusion.12 = f32[512,512]{1,0:T(8,128)S(1)} fusion(bf16[512,4096]{1,0:T(8,128)(2,1)} %bitcast.112, bf16[2,1,4096,512]{3,2,1,0:T(8,128)(2,1)} %param.2), kind=kOutput, calls=%fused_computation.12 | convolution fusion | flops 2147483648 | bytes 9437184 | tf_op jit(solution)/shard_map/dot_general | solution.py:85
  31.9 4.5 %fusion.4 = f32[512,512]{1,0:T(8,128)S(1)} fusion(bf16[512,4096]{1,0:T(8,128)(2,1)S(1)} %bitcast.113, bf16[2,1,4096,512]{3,2,1,0:T(8,128)(2,1)} %param.2), kind=kOutput, calls=%fused_computation.4 | convolution fusion | flops 2147483648 | bytes 9437184 | tf_op jit(solution)/shard_map/dot_general | solution.py:86
  36.6 1.1 pad_maximum_fusion.1
  37.9 5.9 %fusion.10 = f32[512,512]{1,0:T(8,128)S(1)} fusion(bf16[512,4096]{1,0:T(8,128)(2,1)} %bitcast.110, bf16[2,1,4096,512]{3,2,1,0:T(8,128)(2,1)} %param.2), kind=kOutput, calls=%fused_computation.10 | convolution fusion | flops 2147483648 | bytes 9437184 | tf_op jit(solution)/shard_map/dot_general | solution.py:85
  43.8 4.6 %fusion.2 = f32[512,512]{1,0:T(8,128)S(1)} fusion(bf16[512,4096]{1,0:T(8,128)(2,1)S(1)} %bitcast.111, bf16[2,1,4096,512]{3,2,1,0:T(8,128)(2,1)} %param.2), kind=kOutput, calls=%fused_computation.2 | convolution fusion | flops 2147483648 | bytes 9437184 | tf_op jit(solution)/shard_map/dot_general | solution.py:86
  48.6 1.0 pad_maximum_fusion.2
  49.9 6.0 %fusion = f32[512,512]{1,0:T(8,128)S(1)} fusion(bf16[512,4096]{1,0:T(8,128)(2,1)} %bitcast.108, bf16[2,1,4096,512]{3,2,1,0:T(8,128)(2,1)} %param.2), kind=kOutput, calls=%fused_computation | convolution fusion | flops 2147483648 | bytes 9437184 | tf_op jit(solution)/shard_map/dot_general | solution.py:86
  55.9 4.5 %fusion.8 = f32[512,512]{1,0:T(8,128)S(1)} fusion(bf16[512,4096]{1,0:T(8,128)(2,1)S(1)} %bitcast.109, bf16[2,1,4096,512]{3,2,1,0:T(8,128)(2,1)} %param.2), kind=kOutput, calls=%fused_computation.8 | convolution fusion | flops 2147483648 | bytes 9437184 | tf_op jit(solution)/shard_map/dot_general | solution.py:85
  60.7 1.0 pad_maximum_fusion.3
  61.8 1.0 fusion.40
  63.2 21.0 %reduce-scatter.7.cloned.1.call-done = f32[2,64,512]{2,1,0:T(8,128)} async-done(((f32[2,256,512]{2,1,0:T(8,128)}), f32[2,64,512]{2,1,0:T(8,128)}) %reduce-scatter.7.cloned.1.call-update) | async-done | bytes 262160 | tf_op jit(solution)/shard_map/reduce_scatter | solution.py:88
  84.2 1.0 fusion.41
  85.6 26.7 %reduce-scatter.9.cloned.1.call-done = f32[2,64,512]{2,1,0:T(8,128)} async-done(((f32[2,256,512]{2,1,0:T(8,128)}), f32[2,64,512]{2,1,0:T(8,128)}) %reduce-scatter.9.cloned.1.call-update) | async-done | bytes 262160 | tf_op jit(solution)/shard_map/reduce_scatter | solution.py:88
  112.3 1.0 fusion.42
  115.3 24.9 %reduce-scatter.11.cloned.1.call-done = f32[2,64,512]{2,1,0:T(8,128)} async-done(((f32[2,256,512]{2,1,0:T(8,128)}), f32[2,64,512]{2,1,0:T(8,128)}) %reduce-scatter.11.cloned.1.call-update) | async-done | bytes 262160 | tf_op jit(solution)/shard_map/reduce_scatter | solution.py:88
  140.2 1.0 fusion.43
  145.1 1.3 broadcast_select_fusion.5
  149.6 1.6 collective-permute-start.4
  151.1 2.2 %collective-permute-done.4 = f32[7,256,1]{1,2,0:T(1,128)S(1)} collective-permute-done((f32[7,256,1]{1,2,0:T(1,128)S(1)}, f32[7,256,1]{1,2,0:T(1,128)S(1)}, u32[]{:S(2)}, u32[]{:S(2)}) %collective-permute-start.4) | collective-permute-done | bytes 7200 | tf_op jit(solution)/shard_map/ppermute | solution.py:23
  (152 shorter events, 12.2 us)
Async XLA Ops:
  7.2 54.6 %reduce-scatter.5.cloned.1.call-start = ((), (), s32[]{:S(2)}) async-start(), calls=%async_computation.4 | async-start | bytes 1310720 | tf_op jit(solution)/shard_map/reduce_scatter | solution.py:88
  7.2 12.7 %copy-start.3 = (bf16[2,1,4096,512]{3,2,1,0:T(8,128)(2,1)S(1)}, bf16[2,1,4096,512]{3,2,1,0:T(8,128)(2,1)}, u32[]{:S(2)}) copy-start(bf16[2,1,4096,512]{3,2,1,0:T(8,128)(2,1)} %param.2) | copy-start | bytes 25165828
  25.9 58.3 %reduce-scatter.7.cloned.1.call-start = ((), (), s32[]{:S(2)}) async-start(), calls=%async_computation.5 | async-start | bytes 1310720 | tf_op jit(solution)/shard_map/reduce_scatter | solution.py:88
  25.9 5.9 %copy-start.2 = (bf16[2,4,1,64,4096]{4,3,2,1,0:T(8,128)(2,1)S(1)}, bf16[2,4,1,64,4096]{4,3,2,1,0:T(8,128)(2,1)}, u32[]{:S(2)}) copy-start(bf16[2,4,1,64,4096]{4,3,2,1,0:T(8,128)(2,1)} %get-tuple-element.37) | copy-start | bytes 12582916
  37.8 74.5 %reduce-scatter.9.cloned.1.call-start = ((), (), s32[]{:S(2)}) async-start(), calls=%async_computation.6 | async-start | bytes 1310720 | tf_op jit(solution)/shard_map/reduce_scatter | solution.py:88
  37.9 6.0 %copy-start.1 = (bf16[2,4,1,64,4096]{4,3,2,1,0:T(8,128)(2,1)S(1)}, bf16[2,4,1,64,4096]{4,3,2,1,0:T(8,128)(2,1)}, u32[]{:S(2)}) copy-start(bf16[2,4,1,64,4096]{4,3,2,1,0:T(8,128)(2,1)} %get-tuple-element.36) | copy-start | bytes 12582916
  49.7 90.5 %reduce-scatter.11.cloned.1.call-start = ((), (), s32[]{:S(2)}) async-start(), calls=%async_computation.7 | async-start | bytes 1310720 | tf_op jit(solution)/shard_map/reduce_scatter | solution.py:88
  49.9 6.0 %copy-start = (bf16[2,4,1,64,4096]{4,3,2,1,0:T(8,128)(2,1)S(1)}, bf16[2,4,1,64,4096]{4,3,2,1,0:T(8,128)(2,1)}, u32[]{:S(2)}) copy-start(bf16[2,4,1,64,4096]{4,3,2,1,0:T(8,128)(2,1)} %get-tuple-element.35) | copy-start | bytes 12582916
  142.2 2.4 %collective-permute-start = (f32[2,64,8,64]{3,2,1,0:T(8,128)S(1)}, f32[2,64,8,64]{3,2,1,0:T(8,128)}, u32[]{:S(2)}, u32[]{:S(2)}) collective-permute-start(f32[2,64,8,64]{3,2,1,0:T(8,128)S(1)} %constant_dynamic-update-slice_fusion), channel_id=1, source_target_pairs={{0,1},{1,0},{2,3},{3,2},{4,5},{5,4},{6,7},{7,6},{8,9},{9,8},{10,11... | collective-permute-start | bytes 786440 | tf_op jit(solution)/shard_map/ppermute | solution.py:13
  142.4 2.7 %collective-permute-start.1 = (f32[2,64,8,64]{3,2,1,0:T(8,128)S(1)}, f32[2,64,8,64]{3,2,1,0:T(8,128)}, u32[]{:S(2)}, u32[]{:S(2)}) collective-permute-start(f32[2,64,8,64]{3,2,1,0:T(8,128)S(1)} %constant_dynamic-update-slice_fusion.9), channel_id=1, source_target_pairs={{0,1},{1,0},{2,3},{3,2},{4,5},{5,4},{6,7},{7,6},{8,9},{9,8},{10,11... | collective-permute-start | bytes 786440 | tf_op jit(solution)/shard_map/ppermute | solution.py:13
  143.4 4.4 %collective-permute-start.2 = (f32[2,64,8,64]{3,2,1,0:T(8,128)S(1)}, f32[2,64,8,64]{3,2,1,0:T(8,128)S(1)}, u32[]{:S(2)}, u32[]{:S(2)}) collective-permute-start(f32[2,64,8,64]{3,2,1,0:T(8,128)S(1)} %constant_dynamic-update-slice_fusion.18), channel_id=1, source_target_pairs={{0,1},{1,0},{2,3},{3,2},{4,5},{5,4},{6,7},{7,6},{8,9},{9,8},{10,11... | collective-permute-start | bytes 786440 | tf_op jit(solution)/shard_map/ppermute | solution.py:13
  143.6 4.2 %collective-permute-start.3 = (f32[2,64,8,64]{3,2,1,0:T(8,128)S(1)}, f32[2,64,8,64]{3,2,1,0:T(8,128)S(1)}, u32[]{:S(2)}, u32[]{:S(2)}) collective-permute-start(f32[2,64,8,64]{3,2,1,0:T(8,128)S(1)} %constant_dynamic-update-slice_fusion.27), channel_id=1, source_target_pairs={{0,1},{1,0},{2,3},{3,2},{4,5},{5,4},{6,7},{7,6},{8,9},{9,8},{10,11... | collective-permute-start | bytes 786440 | tf_op jit(solution)/shard_map/ppermute | solution.py:13
  149.6 3.7 %collective-permute-start.4 = (f32[7,256,1]{1,2,0:T(1,128)S(1)}, f32[7,256,1]{1,2,0:T(1,128)S(1)}, u32[]{:S(2)}, u32[]{:S(2)}) collective-permute-start(f32[7,256,1]{1,2,0:T(1,128)S(1)} %broadcast_select_fusion.10), channel_id=1, source_target_pairs={{0,2},{2,0},{1,3},{3,1},{4,6},{6,4},{5,7},{7,5},{8,10},{10,8},{9,1... | collective-permute-start | bytes 21512 | tf_op jit(solution)/shard_map/ppermute | solution.py:23
Sparse Core Ops, SparseCore 0:
  26.0 30.0 reduce-scatter.4
  58.4 25.7 reduce-scatter.6
  86.5 25.7 reduce-scatter.8
  114.4 25.7 reduce-scatter.10

commit v2 on v1

--- a/solution.py
+++ b/solution.py
@@ -1,10 +1,13 @@
 import jax
 import jax.numpy as jnp
 from jax import lax
+from jax.experimental import pallas as pl
+from jax.experimental.pallas import tpu as pltpu
 from jax.sharding import PartitionSpec as P
 
 PULSES = 64
-CHUNKS = 4
+BEAM_TILE = 512
+ELEM_TILE = 1024
 
 
 def swapped(value, axis, bit):
@@ -51,7 +54,7 @@
     return (power_h, power_v, cross_re, cross_im)
 
 
-def chunk_stats(summed, gates):
+def beam_stats(summed, gates):
     count = summed.shape[1]
     real = summed[0].reshape(count, gates, PULSES)
     imag = summed[1].reshape(count, gates, PULSES)
@@ -65,29 +68,60 @@
     return jnp.concatenate([jnp.stack([zero_lag, lag_re, lag_im]), pair], axis=0)
 
 
+def complex_kernel(w_ref, x_ref, o_ref):
+    bt = w_ref.shape[1]
+    rows = w_ref[...].reshape(2 * bt, w_ref.shape[2])
+    with_re = jnp.dot(rows, x_ref[0], preferred_element_type=jnp.float32)
+    with_im = jnp.dot(rows, x_ref[1], preferred_element_type=jnp.float32)
+    real = with_re[:bt] + with_im[bt:]
+    imag = with_im[:bt] - with_re[bt:]
+
+    @pl.when(pl.program_id(1) == 0)
+    def _():
+        o_ref[0] = real
+        o_ref[1] = imag
+
+    @pl.when(pl.program_id(1) > 0)
+    def _():
+        o_ref[0] += real
+        o_ref[1] += imag
+
+
+def partials(signal, weights):
+    w = weights[:, 0]
+    x = signal[:, 0]
+    beams, elems = w.shape[1], w.shape[2]
+    samples = x.shape[2]
+    bt = min(BEAM_TILE, beams)
+    tk = min(ELEM_TILE, elems)
+    return pl.pallas_call(
+        complex_kernel,
+        out_shape=jax.ShapeDtypeStruct((2, beams, samples), jnp.float32),
+        grid=(beams // bt, elems // tk),
+        in_specs=[
+            pl.BlockSpec((2, bt, tk), lambda i, k: (0, i, k)),
+            pl.BlockSpec((2, tk, samples), lambda i, k: (0, k, 0)),
+        ],
+        out_specs=pl.BlockSpec((2, bt, samples), lambda i, k: (0, i, 0)),
+        compiler_params=pltpu.CompilerParams(
+            dimension_semantics=("arbitrary", "arbitrary"), vmem_limit_bytes=48 * 1024 * 1024
+        ),
+        cost_estimate=pl.CostEstimate(
+            flops=8 * beams * elems * samples,
+            transcendentals=0,
+            bytes_accessed=4 * beams * elems + 4 * elems * samples * (beams // bt) + 8 * beams * samples,
+        ),
+    )(w, x)
+
+
 def on_device(signal, weights):
     n_elem = lax.axis_size("elem")
     samples = signal.shape[3]
     gates = samples // PULSES
     beams = weights.shape[2]
-    elems = weights.shape[3]
-    local = beams // n_elem
-    chunks = CHUNKS
-    while chunks > 1 and local % (chunks * 8):
-        chunks //= 2
-    per = local // chunks
-    w = weights[:, 0].reshape(2, n_elem, chunks, per, elems)
-    x_re = signal[0, 0]
-    x_im = signal[1, 0]
-    parts = []
-    for j in range(chunks):
-        rows = w[:, :, j].reshape(2 * n_elem * per, elems)
-        p_re = jnp.dot(rows, x_re, preferred_element_type=jnp.float32).reshape(2, n_elem * per, samples)
-        p_im = jnp.dot(rows, x_im, preferred_element_type=jnp.float32).reshape(2, n_elem * per, samples)
-        combined = jnp.stack([p_re[0] + p_im[1], p_im[0] - p_re[1]])
-        summed = lax.psum_scatter(combined, "elem", scatter_dimension=1, tiled=True)
-        parts.append(chunk_stats(summed, gates))
-    stats = jnp.concatenate(parts, axis=1)
+    part = partials(signal, weights)
+    summed = lax.psum_scatter(part, "elem", scatter_dimension=1, tiled=True)
+    stats = beam_stats(summed, gates)
     padded = with_halo(stats, "gate", 2)
     smoothed = (padded[..., :-2] + 2.0 * padded[..., 1:-1] + padded[..., 2:]) * 0.25
     power = smoothed[0]

time: 162 us -> 129 us (0.80)
  matrix products: 36.1 us -> 0 us
  Pallas kernels: 0 us -> 22.8 us
  local copies, waits for them, and re-layouts: 20.4 us -> 3.58 us
  other arithmetic: 11.9 us -> 2.25 us
  waiting for transfers between devices: 75.3 us -> 84.1 us
    dot_general x8 -> x0, matrix products: 36.1 us -> none  [the longest x4 18.7 us: on_device(): jnp.dot(rows, x_re, preferred_element_type=jnp.float32)]
    pallas_call x0 -> x1, Pallas kernels: none -> 22.8 us  [partials(): pl.pallas_call(complex_kernel, out_shape=jax.ShapeDtypeStruct((2, beams,...]
    slice x5 -> x3, local copies, waits for them, and re-layouts: 15.5 us -> 1.66 us  [the longest x2 1.46 us: beam_stats(): real = summed[0].reshape(count, gates, PULSES)]
    reduce_scatter x4 -> x1, waiting for transfers between devices: 72.6 us -> 79.7 us  [on_device(): summed = lax.psum_scatter(part, 'elem', scatter_dimension=1, tiled=True)]
    another operation x4 -> x1, other arithmetic: 4.35 us -> 0.09 us  [beam_stats(): series = jnp.stack([real, imag])]
    div x28 -> x0, local copies, waits for them, and re-layouts: 1.84 us -> none  [the longest x4 0.31 us: pair_stats(): cross_im = jnp.mean(first[0] * second[1] - first[1] * second[0], axis=-1)]
    ppermute x4 -> x1, waiting for transfers between devices: 0.48 us -> 2.26 us  [swapped(): return lax.ppermute(value, axis, pairs)]
    another operation x20 -> x0, local copies, waits for them, and re-layouts: 1.72 us -> none  [the longest x12 0.9 us: chunk_stats(): series = jnp.stack([real, imag])]
  transfers between devices with their start and end apart: 9 -> 3, of which waited for: 5 -> 3; matrix products, arithmetic and copies ran while one was open for 28% -> 0% of each run, Pallas kernels for 0% -> 0%
where the time goes in v2:
time: 129 us
  waiting for transfers between devices  84.1 us (65%)
  Pallas kernels  22.8 us (18%)
  between operations  14.2 us (11%)
  local copies, waits for them, and re-layouts  3.58 us (3%)
  other arithmetic  2.25 us (2%)
  starting transfers between devices  1.64 us (1%)
    reduce_scatter x1, waiting for transfers between devices, on_device(): summed = lax.psum_scatter(part, 'elem', scatter_dimension=1, tiled=True)  79.7 us
    pallas_call x1, Pallas kernels, partials(): pl.pallas_call(complex_kernel, out_shape=jax.ShapeDtypeStruct((2, beams,...  22.8 us
  transfers between devices with their start and end apart: 3, of which 3 were waited for; matrix products, arithmetic and copies ran while one was open for 0% of the time, Pallas kernels for 0%

profile of v2, /device:TPU:0, one launch (start us, length us, event | category | flops | bytes accessed | tf_op | source)
XLA Modules:
  0.0 128.6 jit_solution(4787494789803754526)
XLA Ops:
  7.2 0.0 reduce-scatter.2.cloned.1.call-start
  7.2 22.8 %shard_map.41 = f32[2,1024,512]{2,1,0:T(8,128)S(1)} custom-call(bf16[2,1024,4096]{2,1,0:T(8,128)(2,1)} %bitcast.30, bf16[2,4096,512]{2,1,0:T(8,128)(2,1)} %bitcast.31), custom_call_target="tpu_custom_call" | custom-call | flops 17179869184 | bytes 37748736 | tf_op jit(solution)/shard_map/pallas_call | solution.py:97
  30.1 0.0 copy-start
  30.1 1.9 %copy-done = f32[2,1024,512]{2,1,0:T(8,128)} copy-done((f32[2,1024,512]{2,1,0:T(8,128)}, f32[2,1024,512]{2,1,0:T(8,128)S(1)}, u32[]{:S(2)}) %copy-start) | copy-done | bytes 4194328
  32.0 0.0 reduce-scatter.2.cloned.1.call-update
  32.0 79.7 %reduce-scatter.2.cloned.1.call-done = f32[2,256,512]{2,1,0:T(8,128)} async-done(((f32[2,1024,512]{2,1,0:T(8,128)}), f32[2,256,512]{2,1,0:T(8,128)}) %reduce-scatter.2.cloned.1.call-update) | async-done | bytes 1048592 | tf_op jit(solution)/shard_map/reduce_scatter | solution.py:123
  111.7 1.3 fusion.7
  113.0 0.2 copy.4
  113.2 0.2 copy.5
  113.4 0.1 pad_maximum_fusion
  113.5 0.1 collective-permute-start
  113.6 0.1 add_reduce_fusion.4
  113.6 0.2 subtract_reduce_fusion.1
  113.9 2.3 %collective-permute-done = f32[2,256,8,64]{1,3,2,0:T(8,128)S(1)} collective-permute-done((f32[2,256,8,64]{1,3,2,0:T(8,128)S(1)}, f32[2,256,8,64]{1,3,2,0:T(8,128)S(1)}, u32[]{:S(2)}, u32[]{:S(2)}) %collective-permute-start) | collective-permute-done | bytes 1048608 | tf_op jit(solution)/shard_map/ppermute | solution.py:16
  116.2 0.2 broadcast_select_fusion.1
  116.4 0.3 subtract_reduce_fusion
  116.8 1.5 %collective-permute-start.1 = (f32[7,256,1]{1,2,0:T(1,128)S(1)}, f32[7,256,1]{1,2,0:T(1,128)S(1)}, u32[]{:S(2)}, u32[]{:S(2)}) collective-permute-start(f32[7,256,1]{1,2,0:T(1,128)S(1)} %broadcast_select_fusion.4), channel_id=1, source_target_pairs={{0,2},{2,0},{1,3},{3,1},{4,6},{6,4},{5,7},{7,5},{8,10},{10,8},{9,1... | collective-permute-start | bytes 21512 | tf_op jit(solution)/shard_map/ppermute | solution.py:26
  118.3 2.2 %collective-permute-done.1 = f32[7,256,1]{1,2,0:T(1,128)S(1)} collective-permute-done((f32[7,256,1]{1,2,0:T(1,128)S(1)}, f32[7,256,1]{1,2,0:T(1,128)S(1)}, u32[]{:S(2)}, u32[]{:S(2)}) %collective-permute-start.1) | collective-permute-done | bytes 7200 | tf_op jit(solution)/shard_map/ppermute | solution.py:26
  120.6 0.6 slice_divide_fusion
  121.2 0.6 maximum_bitcast_fusion
  (11 shorter events, 0.1 us)
Async XLA Ops:
  7.2 104.5 %reduce-scatter.2.cloned.1.call-start = ((), (), s32[]{:S(2)}) async-start(), calls=%async_computation.1 | async-start | bytes 5242880 | tf_op jit(solution)/shard_map/reduce_scatter | solution.py:123
  30.1 1.9 %copy-start = (f32[2,1024,512]{2,1,0:T(8,128)}, f32[2,1024,512]{2,1,0:T(8,128)S(1)}, u32[]{:S(2)}) copy-start(f32[2,1024,512]{2,1,0:T(8,128)S(1)} %shard_map.41) | copy-start | bytes 12582916
  113.5 2.7 %collective-permute-start = (f32[2,256,8,64]{1,3,2,0:T(8,128)S(1)}, f32[2,256,8,64]{1,3,2,0:T(8,128)S(1)}, u32[]{:S(2)}, u32[]{:S(2)}) collective-permute-start(f32[2,256,8,64]{1,3,2,0:T(8,128)S(1)} %pad_maximum_fusion), channel_id=1, source_target_pairs={{0,1},{1,0},{2,3},{3,2},{4,5},{5,4},{6,7},{7,6},{8,9},{9,8},{10,11... | collective-permute-start | bytes 3145736 | tf_op jit(solution)/shard_map/ppermute | solution.py:16
  116.8 3.7 %collective-permute-start.1 = (f32[7,256,1]{1,2,0:T(1,128)S(1)}, f32[7,256,1]{1,2,0:T(1,128)S(1)}, u32[]{:S(2)}, u32[]{:S(2)}) collective-permute-start(f32[7,256,1]{1,2,0:T(1,128)S(1)} %broadcast_select_fusion.4), channel_id=1, source_target_pairs={{0,2},{2,0},{1,3},{3,1},{4,6},{6,4},{5,7},{7,5},{8,10},{10,8},{9,1... | collective-permute-start | bytes 21512 | tf_op jit(solution)/shard_map/ppermute | solution.py:26
Sparse Core Ops, SparseCore 0:
  32.1 79.5 reduce-scatter.1

commit v3 on v2

--- a/solution.py
+++ b/solution.py
@@ -114,13 +114,35 @@
     )(w, x)
 
 
+def line_scatter(part, n_elem):
+    me = lax.axis_index("elem")
+    blocks = part.reshape(2, n_elem, part.shape[1] // n_elem, part.shape[2])
+    got_right = None
+    got_left = None
+    for step in range(1, n_elem):
+        to_right = lax.dynamic_index_in_dim(blocks, jnp.clip(me + n_elem - step, 0, n_elem - 1), 1, False)
+        to_left = lax.dynamic_index_in_dim(blocks, jnp.clip(me - n_elem + step, 0, n_elem - 1), 1, False)
+        if got_right is not None:
+            to_right = to_right + got_right
+            to_left = to_left + got_left
+        got_right = lax.ppermute(to_right, "elem", [(c, c + 1) for c in range(step)])
+        got_left = lax.ppermute(to_left, "elem", [(c, c - 1) for c in range(n_elem - step, n_elem)])
+    own = lax.dynamic_index_in_dim(blocks, me, 1, False)
+    if got_right is None:
+        return own
+    return own + got_right + got_left
+
+
 def on_device(signal, weights):
     n_elem = lax.axis_size("elem")
     samples = signal.shape[3]
     gates = samples // PULSES
     beams = weights.shape[2]
     part = partials(signal, weights)
-    summed = lax.psum_scatter(part, "elem", scatter_dimension=1, tiled=True)
+    if n_elem <= 8:
+        summed = line_scatter(part, n_elem)
+    else:
+        summed = lax.psum_scatter(part, "elem", scatter_dimension=1, tiled=True)
     stats = beam_stats(summed, gates)
     padded = with_halo(stats, "gate", 2)
     smoothed = (padded[..., :-2] + 2.0 * padded[..., 1:-1] + padded[..., 2:]) * 0.25

time: 129 us -> 131 us (1.016)
  waiting for transfers between devices: 84.1 us -> 55.1 us
  starting transfers between devices: 1.64 us -> 22.9 us
  between operations: 14.2 us -> 0.84 us
  other arithmetic: 2.25 us -> 14 us
  local copies, waits for them, and re-layouts: 3.58 us -> 15.1 us
    reduce_scatter x1 -> x0, waiting for transfers between devices: 79.7 us -> none  [on_device(): summed = lax.psum_scatter(part, 'elem', scatter_dimension=1, tiled=True)]
    ppermute x0 -> x6, waiting for transfers between devices: none -> 50.7 us  [the longest x3 43.3 us: line_scatter(): lax.ppermute(to_right, 'elem', [(c, c + 1) for c in range(step)])]
    ppermute x0 -> x6, starting transfers between devices: none -> 21.3 us  [the longest x3 16.7 us: line_scatter(): lax.ppermute(to_right, 'elem', [(c, c + 1) for c in range(step)])]
    dynamic_slice x0 -> x8, local copies, waits for them, and re-layouts: none -> 15 us  [the longest x3 6.42 us: line_scatter(): lax.dynamic_index_in_dim(blocks, jnp.clip(me + n_elem - step, 0, n_elem -...]
    add x0 -> x5, other arithmetic: none -> 11.8 us  [the longest x2 5.33 us: line_scatter(): to_right = to_right + got_right]
    unnamed x2 -> x0, local copies, waits for them, and re-layouts: 1.92 us -> none
    slice x2 -> x1, local copies, waits for them, and re-layouts: 1.46 us -> 0.07 us  [beam_stats(): real = summed[0].reshape(count, gates, PULSES)]
  transfers between devices with their start and end apart: 3 -> 8, of which waited for: 3 -> 6; matrix products, arithmetic and copies ran while one was open for 0% -> 16% of each run, Pallas kernels for 0% -> 0%
where the time goes in v3:
time: 131 us
  waiting for transfers between devices  55.1 us (42%)
  Pallas kernels  22.9 us (17%)
  starting transfers between devices  22.9 us (17%)
  local copies, waits for them, and re-layouts  15.1 us (12%)
  other arithmetic  14 us (11%)
    ppermute x3, waiting for transfers between devices, line_scatter(): lax.ppermute(to_right, 'elem', [(c, c + 1) for c in range(step)])  43.3 us
    pallas_call x1, Pallas kernels, partials(): pl.pallas_call(complex_kernel, out_shape=jax.ShapeDtypeStruct((2, beams,...  22.9 us
    ppermute x3, starting transfers between devices, line_scatter(): lax.ppermute(to_right, 'elem', [(c, c + 1) for c in range(step)])  16.7 us
    ppermute x3, waiting for transfers between devices, line_scatter(): lax.ppermute(to_left, 'elem', [(c, c - 1) for c in range(n_elem - step, n...  7.38 us
    dynamic_slice x3, local copies, waits for them, and re-layouts, line_scatter(): lax.dynamic_index_in_dim(blocks, jnp.clip(me + n_elem - step, 0, n_elem -...  6.42 us
    dynamic_slice x3, local copies, waits for them, and re-layouts, line_scatter(): lax.dynamic_index_in_dim(blocks, jnp.clip(me - n_elem + step, 0, n_elem -...  5.5 us
    add x2, other arithmetic, line_scatter(): to_right = to_right + got_right  5.33 us
    add x2, other arithmetic, line_scatter(): to_left = to_left + got_left  5.03 us
  transfers between devices with their start and end apart: 8, of which 6 were waited for; matrix products, arithmetic and copies ran while one was open for 16% of the time, Pallas kernels for 0%

profile of v3, /device:TPU:0, one launch (start us, length us, event | category | flops | bytes accessed | tf_op | source)
XLA Modules:
  0.0 130.8 jit_solution(15736551088654076035)
XLA Ops:
  0.7 22.9 %shard_map.41 = f32[2,1024,512]{2,1,0:T(8,128)S(1)} custom-call(bf16[2,1024,4096]{2,1,0:T(8,128)(2,1)} %bitcast.48, bf16[2,4096,512]{2,1,0:T(8,128)(2,1)} %bitcast.49), custom_call_target="tpu_custom_call" | custom-call | flops 17179869184 | bytes 37748736 | tf_op jit(solution)/shard_map/pallas_call | solution.py:97
  23.5 2.7 %constant_dynamic-slice_fusion.6 = (f32[2,1,256,512]{3,2,1,0:T(8,128)S(1)}, f32[2,1,256,512]{3,2,1,0:T(8,128)}, f32[2,1,256,512]{3,2,1,0:T(8,128)}, f32[2,1,256,...) fusion(f32[2,4,256,512]{3,2,1,0:T(8,128)S(1)} %bitcast.37, ...), kind=kLoop, calls=%fused_computation.49 | loop fusion | bytes 14680092 | tf_op jit(solution)/shard_map/jit(dynamic_index_in_dim)/dynamic_slice | solution.py:130
  26.3 2.5 %copy.7 = f32[2,1,256,512]{2,3,0,1:T(8,128)} copy(f32[2,1,256,512]{3,2,1,0:T(8,128)} %get-tuple-element.14) | data formatting | bytes 2097152 | tf_op jit(solution)/shard_map/jit(dynamic_index_in_dim)/dynamic_slice | solution.py:123
  28.8 5.9 %collective-permute-start = (f32[2,256,512]{1,2,0:T(8,128)}, f32[2,256,512]{1,2,0:T(8,128)}, u32[]{:S(2)}, u32[]{:S(2)}) collective-permute-start(f32[2,256,512]{1,2,0:T(8,128)} %bitcast.47), channel_id=1, source_target_pairs={{0,4},{1,5},{2,6},{3,7},{16,20},{17,21},{18,22},{19,23}} | collective-permute-start | bytes 3145736 | tf_op jit(solution)/shard_map/ppermute | solution.py:128
  34.7 2.6 %copy.10 = f32[2,1,256,512]{2,3,0,1:T(8,128)} copy(f32[2,1,256,512]{3,2,1,0:T(8,128)} %get-tuple-element.11) | data formatting | bytes 2097152 | tf_op jit(solution)/shard_map/jit(dynamic_index_in_dim)/dynamic_slice | solution.py:124
  37.3 1.6 %collective-permute-start.3 = (f32[2,256,512]{1,2,0:T(8,128)}, f32[2,256,512]{1,2,0:T(8,128)}, u32[]{:S(2)}, u32[]{:S(2)}) collective-permute-start(f32[2,256,512]{1,2,0:T(8,128)} %bitcast.46), channel_id=1, source_target_pairs={{12,8},{13,9},{14,10},{15,11},{28,24},{29,25},{30,26},{31,27}} | collective-permute-start | bytes 3145736 | tf_op jit(solution)/shard_map/ppermute | solution.py:129
  39.0 2.6 %copy.6 = f32[2,1,256,512]{2,3,0,1:T(8,128)} copy(f32[2,1,256,512]{3,2,1,0:T(8,128)} %get-tuple-element.15) | data formatting | bytes 2097152 | tf_op jit(solution)/shard_map/jit(dynamic_index_in_dim)/dynamic_slice | solution.py:123
  41.5 2.6 %copy.9 = f32[2,1,256,512]{2,3,0,1:T(8,128)} copy(f32[2,1,256,512]{3,2,1,0:T(8,128)} %get-tuple-element.12) | data formatting | bytes 2097152 | tf_op jit(solution)/shard_map/jit(dynamic_index_in_dim)/dynamic_slice | solution.py:124
  44.1 12.4 %collective-permute-done = f32[2,256,512]{1,2,0:T(8,128)} collective-permute-done((f32[2,256,512]{1,2,0:T(8,128)}, f32[2,256,512]{1,2,0:T(8,128)}, u32[]{:S(2)}, u32[]{:S(2)}) %collective-permute-start) | collective-permute-done | bytes 1048608 | tf_op jit(solution)/shard_map/ppermute | solution.py:128
  56.5 2.7 %bitcast_add_fusion.2 = f32[2,256,512]{1,2,0:T(8,128)} fusion(f32[2,256,512]{1,2,0:T(8,128)} %collective-permute-done, f32[2,1,256,512]{2,3,0,1:T(8,128)} %copy.6), kind=kLoop, calls=%fused_computation.3 | loop fusion | flops 262144 | bytes 3145728 | tf_op jit(solution)/shard_map/add | solution.py:126
  59.2 5.4 %collective-permute-start.1 = (f32[2,256,512]{1,2,0:T(8,128)}, f32[2,256,512]{1,2,0:T(8,128)}, u32[]{:S(2)}, u32[]{:S(2)}) collective-permute-start(f32[2,256,512]{1,2,0:T(8,128)} %bitcast_add_fusion.2), channel_id=1, source_target_pairs={{0,4},{4,8},{1,5},{5,9},{2,6},{6,10},{3,7},{7,11},{16,20},{20,24},... | collective-permute-start | bytes 3145736 | tf_op jit(solution)/shard_map/ppermute | solution.py:128
  64.5 2.7 %bitcast_add_fusion = f32[2,256,512]{1,2,0:T(8,128)} fusion(f32[2,256,512]{1,2,0:T(8,128)} %collective-permute-done.3, f32[2,1,256,512]{2,3,0,1:T(8,128)} %copy.9), kind=kLoop, calls=%fused_computation.1 | loop fusion | flops 262144 | bytes 3145728 | tf_op jit(solution)/shard_map/add | solution.py:127
  67.2 1.6 %collective-permute-start.4 = (f32[2,256,512]{1,2,0:T(8,128)}, f32[2,256,512]{1,2,0:T(8,128)}, u32[]{:S(2)}, u32[]{:S(2)}) collective-permute-start(f32[2,256,512]{1,2,0:T(8,128)} %bitcast_add_fusion), channel_id=1, source_target_pairs={{8,4},{12,8},{9,5},{13,9},{10,6},{14,10},{11,7},{15,11},{24,20},{2... | collective-permute-start | bytes 3145736 | tf_op jit(solution)/shard_map/ppermute | solution.py:129
  68.9 1.3 %copy.5 = f32[2,1,256,512]{2,3,0,1:T(8,128)} copy(f32[2,1,256,512]{3,2,1,0:T(8,128)S(1)} %get-tuple-element.16) | data formatting | bytes 2097152 | tf_op jit(solution)/shard_map/jit(dynamic_index_in_dim)/dynamic_slice | solution.py:123
  70.5 14.9 %collective-permute-done.1 = f32[2,256,512]{1,2,0:T(8,128)} collective-permute-done((f32[2,256,512]{1,2,0:T(8,128)}, f32[2,256,512]{1,2,0:T(8,128)}, u32[]{:S(2)}, u32[]{:S(2)}) %collective-permute-start.1) | collective-permute-done | bytes 1048608 | tf_op jit(solution)/shard_map/ppermute | solution.py:128
  85.4 2.7 %bitcast_add_fusion.3 = f32[2,256,512]{1,2,0:T(8,128)} fusion(f32[2,256,512]{1,2,0:T(8,128)} %collective-permute-done.1, f32[2,1,256,512]{2,3,0,1:T(8,128)} %copy.5), kind=kLoop, calls=%fused_computation.4 | loop fusion | flops 262144 | bytes 3145728 | tf_op jit(solution)/shard_map/add | solution.py:126
  88.1 5.4 %collective-permute-start.2 = (f32[2,256,512]{1,2,0:T(8,128)}, f32[2,256,512]{1,2,0:T(8,128)}, u32[]{:S(2)}, u32[]{:S(2)}) collective-permute-start(f32[2,256,512]{1,2,0:T(8,128)} %bitcast_add_fusion.3), channel_id=1, source_target_pairs={{0,4},{4,8},{8,12},{1,5},{5,9},{9,13},{2,6},{6,10},{10,14},{3,7},{... | collective-permute-start | bytes 3145736 | tf_op jit(solution)/shard_map/ppermute | solution.py:128
  93.5 2.3 %bitcast_add_fusion.1 = f32[2,256,512]{1,2,0:T(8,128)} fusion(f32[2,256,512]{1,2,0:T(8,128)} %collective-permute-done.4, f32[2,1,256,512]{2,3,0,1:T(8,128)S(1)} %copy.8), kind=kLoop, calls=%fused_computation.2 | loop fusion | flops 262144 | bytes 3145728 | tf_op jit(solution)/shard_map/add | solution.py:127
  97.5 16.0 %collective-permute-done.2 = f32[2,256,512]{1,2,0:T(8,128)} collective-permute-done((f32[2,256,512]{1,2,0:T(8,128)}, f32[2,256,512]{1,2,0:T(8,128)}, u32[]{:S(2)}, u32[]{:S(2)}) %collective-permute-start.2) | collective-permute-done | bytes 1048608 | tf_op jit(solution)/shard_map/ppermute | solution.py:128
  113.5 7.4 %collective-permute-done.5 = f32[2,256,512]{1,2,0:T(8,128)S(1)} collective-permute-done((f32[2,256,512]{1,2,0:T(8,128)}, f32[2,256,512]{1,2,0:T(8,128)S(1)}, u32[]{:S(2)}, u32[]{:S(2)}) %collective-permute-start.5) | collective-permute-done | bytes 1048608 | tf_op jit(solution)/shard_map/ppermute | solution.py:129
  120.8 1.4 %fusion = f32[2,256,512]{1,2,0:T(8,128)S(1)} fusion(f32[2,256,512]{1,2,0:T(8,128)S(1)} %collective-permute-done.5, f32[2,256,512]{1,2,0:T(8,128)} %collective-permute-done.2, f32[2,1,256,512]{2,3,0,1:T(8,128)S(1)} %copy.4), kind=kLoop, calls=%fused_computation.6 | loop fusion | flops 524288 | bytes 4194304 | tf_op jit(solution)/shard_map/add | solution.py:133
  122.9 2.3 %collective-permute-done.6 = f32[2,256,8,64]{1,3,2,0:T(8,128)S(1)} collective-permute-done((f32[2,256,8,64]{1,3,2,0:T(8,128)S(1)}, f32[2,256,8,64]{1,3,2,0:T(8,128)S(1)}, u32[]{:S(2)}, u32[]{:S(2)}) %collective-permute-start.6) | collective-permute-done | bytes 1048608 | tf_op jit(solution)/shard_map/ppermute | solution.py:16
  125.8 1.5 %collective-permute-start.7 = (f32[7,256,1]{1,2,0:T(1,128)S(1)}, f32[7,256,1]{1,2,0:T(1,128)S(1)}, u32[]{:S(2)}, u32[]{:S(2)}) collective-permute-start(f32[7,256,1]{1,2,0:T(1,128)S(1)} %broadcast_select_fusion.4), channel_id=1, source_target_pairs={{0,2},{2,0},{1,3},{3,1},{4,6},{6,4},{5,7},{7,5},{8,10},{10,8},{9,1... | collective-permute-start | bytes 21512 | tf_op jit(solution)/shard_map/ppermute | solution.py:26
  127.3 2.2 %collective-permute-done.7 = f32[7,256,1]{1,2,0:T(1,128)S(1)} collective-permute-done((f32[7,256,1]{1,2,0:T(1,128)S(1)}, f32[7,256,1]{1,2,0:T(1,128)S(1)}, u32[]{:S(2)}, u32[]{:S(2)}) %collective-permute-start.7) | collective-permute-done | bytes 7200 | tf_op jit(solution)/shard_map/ppermute | solution.py:26
  (25 shorter events, 4.3 us)
Async XLA Ops:
  28.8 27.7 %collective-permute-start = (f32[2,256,512]{1,2,0:T(8,128)}, f32[2,256,512]{1,2,0:T(8,128)}, u32[]{:S(2)}, u32[]{:S(2)}) collective-permute-start(f32[2,256,512]{1,2,0:T(8,128)} %bitcast.47), channel_id=1, source_target_pairs={{0,4},{1,5},{2,6},{3,7},{16,20},{17,21},{18,22},{19,23}} | collective-permute-start | bytes 3145736 | tf_op jit(solution)/shard_map/ppermute | solution.py:128
  37.3 27.2 %collective-permute-start.3 = (f32[2,256,512]{1,2,0:T(8,128)}, f32[2,256,512]{1,2,0:T(8,128)}, u32[]{:S(2)}, u32[]{:S(2)}) collective-permute-start(f32[2,256,512]{1,2,0:T(8,128)} %bitcast.46), channel_id=1, source_target_pairs={{12,8},{13,9},{14,10},{15,11},{28,24},{29,25},{30,26},{31,27}} | collective-permute-start | bytes 3145736 | tf_op jit(solution)/shard_map/ppermute | solution.py:129
  59.2 26.3 %collective-permute-start.1 = (f32[2,256,512]{1,2,0:T(8,128)}, f32[2,256,512]{1,2,0:T(8,128)}, u32[]{:S(2)}, u32[]{:S(2)}) collective-permute-start(f32[2,256,512]{1,2,0:T(8,128)} %bitcast_add_fusion.2), channel_id=1, source_target_pairs={{0,4},{4,8},{1,5},{5,9},{2,6},{6,10},{3,7},{7,11},{16,20},{20,24},... | collective-permute-start | bytes 3145736 | tf_op jit(solution)/shard_map/ppermute | solution.py:128
  67.2 26.3 %collective-permute-start.4 = (f32[2,256,512]{1,2,0:T(8,128)}, f32[2,256,512]{1,2,0:T(8,128)}, u32[]{:S(2)}, u32[]{:S(2)}) collective-permute-start(f32[2,256,512]{1,2,0:T(8,128)} %bitcast_add_fusion), channel_id=1, source_target_pairs={{8,4},{12,8},{9,5},{13,9},{10,6},{14,10},{11,7},{15,11},{24,20},{2... | collective-permute-start | bytes 3145736 | tf_op jit(solution)/shard_map/ppermute | solution.py:129
  88.1 25.4 %collective-permute-start.2 = (f32[2,256,512]{1,2,0:T(8,128)}, f32[2,256,512]{1,2,0:T(8,128)}, u32[]{:S(2)}, u32[]{:S(2)}) collective-permute-start(f32[2,256,512]{1,2,0:T(8,128)} %bitcast_add_fusion.3), channel_id=1, source_target_pairs={{0,4},{4,8},{8,12},{1,5},{5,9},{9,13},{2,6},{6,10},{10,14},{3,7},{... | collective-permute-start | bytes 3145736 | tf_op jit(solution)/shard_map/ppermute | solution.py:128
  95.8 25.0 %collective-permute-start.5 = (f32[2,256,512]{1,2,0:T(8,128)}, f32[2,256,512]{1,2,0:T(8,128)S(1)}, u32[]{:S(2)}, u32[]{:S(2)}) collective-permute-start(f32[2,256,512]{1,2,0:T(8,128)} %bitcast_add_fusion.1), channel_id=1, source_target_pairs={{4,0},{8,4},{12,8},{5,1},{9,5},{13,9},{6,2},{10,6},{14,10},{7,3},{... | collective-permute-start | bytes 3145736 | tf_op jit(solution)/shard_map/ppermute | solution.py:129
  122.5 2.7 %collective-permute-start.6 = (f32[2,256,8,64]{1,3,2,0:T(8,128)S(1)}, f32[2,256,8,64]{1,3,2,0:T(8,128)S(1)}, u32[]{:S(2)}, u32[]{:S(2)}) collective-permute-start(f32[2,256,8,64]{1,3,2,0:T(8,128)S(1)} %pad_maximum_fusion), channel_id=1, source_target_pairs={{0,1},{1,0},{2,3},{3,2},{4,5},{5,4},{6,7},{7,6},{8,9},{9,8},{10,11... | collective-permute-start | bytes 3145736 | tf_op jit(solution)/shard_map/ppermute | solution.py:16
  125.8 3.7 %collective-permute-start.7 = (f32[7,256,1]{1,2,0:T(1,128)S(1)}, f32[7,256,1]{1,2,0:T(1,128)S(1)}, u32[]{:S(2)}, u32[]{:S(2)}) collective-permute-start(f32[7,256,1]{1,2,0:T(1,128)S(1)} %broadcast_select_fusion.4), channel_id=1, source_target_pairs={{0,2},{2,0},{1,3},{3,1},{4,6},{6,4},{5,7},{7,5},{8,10},{10,8},{9,1... | collective-permute-start | bytes 21512 | tf_op jit(solution)/shard_map/ppermute | solution.py:26

commit v4 on v3

--- a/solution.py
+++ b/solution.py
@@ -3,9 +3,11 @@
 from jax import lax
 from jax.experimental import pallas as pl
 from jax.experimental.pallas import tpu as pltpu
+from jax.experimental.layout import Layout, with_layout_constraint
 from jax.sharding import PartitionSpec as P
 
 PULSES = 64
+ROW_MAJOR = Layout(major_to_minor=(0, 1, 2))
 BEAM_TILE = 512
 ELEM_TILE = 1024
 
@@ -125,6 +127,8 @@
         if got_right is not None:
             to_right = to_right + got_right
             to_left = to_left + got_left
+        to_right = with_layout_constraint(to_right, ROW_MAJOR)
+        to_left = with_layout_constraint(to_left, ROW_MAJOR)
         got_right = lax.ppermute(to_right, "elem", [(c, c + 1) for c in range(step)])
         got_left = lax.ppermute(to_left, "elem", [(c, c - 1) for c in range(n_elem - step, n_elem)])
     own = lax.dynamic_index_in_dim(blocks, me, 1, False)

time: 131 us -> 147 us (1.12)
  waiting for transfers between devices: 55.1 us -> 89.7 us
  local copies, waits for them, and re-layouts: 15.1 us -> 2.55 us
  other arithmetic: 14 us -> 10.4 us
  starting transfers between devices: 22.9 us -> 19.8 us
    ppermute x3, waiting for transfers between devices: 7.38 us -> 25 us  [line_scatter(): lax.ppermute(to_left, 'elem', [(c, c - 1) for c in range(n_elem - step, n...]
    ppermute x3, waiting for transfers between devices: 43.3 us -> 60.3 us  [line_scatter(): lax.ppermute(to_right, 'elem', [(c, c + 1) for c in range(step)])]
    dynamic_slice x8 -> x0, local copies, waits for them, and re-layouts: 15 us -> none  [the longest x3 6.42 us: line_scatter(): lax.dynamic_index_in_dim(blocks, jnp.clip(me + n_elem - step, 0, n_elem -...]
    add x2 -> x1, other arithmetic: 5.03 us -> 1.44 us  [line_scatter(): to_left = to_left + got_left]
    ppermute x3, starting transfers between devices: 16.7 us -> 14.5 us  [line_scatter(): lax.ppermute(to_right, 'elem', [(c, c + 1) for c in range(step)])]
    unnamed x0 -> x2, local copies, waits for them, and re-layouts: none -> 1.92 us
  transfers between devices with their start and end apart: 8 -> 8, of which waited for: 6 -> 6; matrix products, arithmetic and copies ran while one was open for 16% -> 2% of each run, Pallas kernels for 0% -> 0%
where the time goes in v4:
time: 147 us; the launch traced here: 146 us
  waiting for transfers between devices  89.7 us (61%)
  Pallas kernels  22.8 us (16%)
  starting transfers between devices  19.8 us (13%)
  other arithmetic  10.4 us (7%)
  local copies, waits for them, and re-layouts  2.55 us (2%)
    ppermute x3, waiting for transfers between devices, line_scatter(): lax.ppermute(to_right, 'elem', [(c, c + 1) for c in range(step)])  60.3 us
    ppermute x3, waiting for transfers between devices, line_scatter(): lax.ppermute(to_left, 'elem', [(c, c - 1) for c in range(n_elem - step, n...  25 us
    pallas_call x1, Pallas kernels, partials(): pl.pallas_call(complex_kernel, out_shape=jax.ShapeDtypeStruct((2, beams,...  22.8 us
    ppermute x3, starting transfers between devices, line_scatter(): lax.ppermute(to_right, 'elem', [(c, c + 1) for c in range(step)])  14.5 us
    add x2, other arithmetic, line_scatter(): to_right = to_right + got_right  5.13 us
    ppermute x3, starting transfers between devices, line_scatter(): lax.ppermute(to_left, 'elem', [(c, c - 1) for c in range(n_elem - step, n...  3.65 us
  transfers between devices with their start and end apart: 8, of which 6 were waited for; matrix products, arithmetic and copies ran while one was open for 2% of the time, Pallas kernels for 0%

profile of v4, /device:TPU:0, one launch (start us, length us, event | category | flops | bytes accessed | tf_op | source)
XLA Modules:
  0.0 146.2 jit_solution(8933982064862211629)
XLA Ops:
  0.6 22.8 %shard_map.41 = f32[2,1024,512]{2,1,0:T(8,128)S(1)} custom-call(bf16[2,1024,4096]{2,1,0:T(8,128)(2,1)} %bitcast.66, bf16[2,4096,512]{2,1,0:T(8,128)(2,1)} %bitcast.67), custom_call_target="tpu_custom_call" | custom-call | flops 17179869184 | bytes 37748736 | tf_op jit(solution)/shard_map/pallas_call | solution.py:99
  23.5 1.9 %copy-done = f32[2,1024,512]{2,1,0:T(8,128)} copy-done((f32[2,1024,512]{2,1,0:T(8,128)}, f32[2,1024,512]{2,1,0:T(8,128)S(1)}, u32[]{:S(2)}) %copy-start) | copy-done | bytes 4194328
  25.6 5.0 %collective-permute-start = (f32[2,256,512]{2,1,0:T(8,128)S(1)}, f32[2,256,512]{2,1,0:T(8,128)S(1)}, u32[]{:S(2)}, u32[]{:S(2)}) collective-permute-start(f32[2,256,512]{2,1,0:T(8,128)S(1)} %get-tuple-element.12), channel_id=1, source_target_pairs={{0,4},{1,5},{2,6},{3,7},{16,20},{17,21},{18,22},{19,23}} | collective-permute-start | bytes 3145736 | tf_op jit(solution)/shard_map/ppermute | solution.py:132
  30.6 1.6 %collective-permute-start.3 = (f32[2,256,512]{2,1,0:T(8,128)S(1)}, f32[2,256,512]{2,1,0:T(8,128)}, u32[]{:S(2)}, u32[]{:S(2)}) collective-permute-start(f32[2,256,512]{2,1,0:T(8,128)S(1)} %get-tuple-element.13), channel_id=1, source_target_pairs={{12,8},{13,9},{14,10},{15,11},{28,24},{29,25},{30,26},{31,27}} | collective-permute-start | bytes 3145736 | tf_op jit(solution)/shard_map/ppermute | solution.py:133
  32.3 20.7 %collective-permute-done = f32[2,256,512]{2,1,0:T(8,128)S(1)} collective-permute-done((f32[2,256,512]{2,1,0:T(8,128)S(1)}, f32[2,256,512]{2,1,0:T(8,128)S(1)}, u32[]{:S(2)}, u32[]{:S(2)}) %collective-permute-start) | collective-permute-done | bytes 1048608 | tf_op jit(solution)/shard_map/ppermute | solution.py:132
  53.0 1.4 bitcast_add_fusion.2
  54.4 4.5 %collective-permute-start.1 = (f32[2,256,512]{2,1,0:T(8,128)S(1)}, f32[2,256,512]{2,1,0:T(8,128)S(1)}, u32[]{:S(2)}, u32[]{:S(2)}) collective-permute-start(f32[2,256,512]{2,1,0:T(8,128)S(1)} %bitcast_add_fusion.2), channel_id=1, source_target_pairs={{0,4},{4,8},{1,5},{5,9},{2,6},{6,10},{3,7},{7,11},{16,20},{20,24},... | collective-permute-start | bytes 3145736 | tf_op jit(solution)/shard_map/ppermute | solution.py:132
  58.9 21.5 %collective-permute-done.1 = f32[2,256,512]{2,1,0:T(8,128)S(1)} collective-permute-done((f32[2,256,512]{2,1,0:T(8,128)S(1)}, f32[2,256,512]{2,1,0:T(8,128)S(1)}, u32[]{:S(2)}, u32[]{:S(2)}) %collective-permute-start.1) | collective-permute-done | bytes 1048608 | tf_op jit(solution)/shard_map/ppermute | solution.py:132
  80.3 3.7 %bitcast_add_fusion.3 = (f32[2,256,512]{2,1,0:T(8,128)}, f32[2,256,512]{2,1,0:T(8,128)}) fusion(f32[2,256,512]{2,1,0:T(8,128)S(1)} %collective-permute-done.1, f32[2,4,256,512]{3,2,1,0:T(8,128)} %bitcast.55, s32[]{:T(128)S(6)} %min.19, f32[2,256,512]{2,1,0:T(8,128)} %collective-permute-done.3, s32[]{:T(128)S(6)} %min.23), kind=kLoop, calls=%fused_computation.4 | loop fusion | flops 524288 | bytes 6291464 | tf_op jit(solution)/shard_map/add | solution.py:128
  84.0 0.7 collective-permute-start.4
  84.8 5.0 %collective-permute-start.2 = (f32[2,256,512]{2,1,0:T(8,128)}, f32[2,256,512]{2,1,0:T(8,128)S(1)}, u32[]{:S(2)}, u32[]{:S(2)}) collective-permute-start(f32[2,256,512]{2,1,0:T(8,128)} %get-tuple-element.10), channel_id=1, source_target_pairs={{0,4},{4,8},{8,12},{1,5},{5,9},{9,13},{2,6},{6,10},{10,14},{3,7},{... | collective-permute-start | bytes 3145736 | tf_op jit(solution)/shard_map/ppermute | solution.py:132
  89.8 1.4 bitcast_add_fusion.1
  91.2 1.3 collective-permute-start.5
  92.5 18.2 %collective-permute-done.2 = f32[2,256,512]{2,1,0:T(8,128)S(1)} collective-permute-done((f32[2,256,512]{2,1,0:T(8,128)}, f32[2,256,512]{2,1,0:T(8,128)S(1)}, u32[]{:S(2)}, u32[]{:S(2)}) %collective-permute-start.2) | collective-permute-done | bytes 1048608 | tf_op jit(solution)/shard_map/ppermute | solution.py:132
  110.7 25.0 %collective-permute-done.5 = f32[2,256,512]{2,1,0:T(8,128)S(1)} collective-permute-done((f32[2,256,512]{2,1,0:T(8,128)S(1)}, f32[2,256,512]{2,1,0:T(8,128)S(1)}, u32[]{:S(2)}, u32[]{:S(2)}) %collective-permute-start.5) | collective-permute-done | bytes 1048608 | tf_op jit(solution)/shard_map/ppermute | solution.py:133
  135.7 1.6 %fusion = f32[2,256,512]{2,1,0:T(8,128)S(1)} fusion(f32[2,256,512]{2,1,0:T(8,128)S(1)} %collective-permute-done.5, f32[2,256,512]{2,1,0:T(8,128)S(1)} %collective-permute-done.2, f32[2,4,256,512]{3,2,1,0:T(8,128)} %bitcast.57, s32[]{:T(128)S(6)} %select_n.48), kind=kLoop, calls=%fused_computation.6 | loop fusion | flops 524288 | bytes 4194308 | tf_op jit(solution)/shard_map/add | solution.py:137
  137.4 0.2 copy.18
  138.1 0.2 subtract_reduce_fusion.1
  138.4 2.3 %collective-permute-done.6 = f32[2,256,8,64]{1,3,2,0:T(8,128)S(1)} collective-permute-done((f32[2,256,8,64]{1,3,2,0:T(8,128)S(1)}, f32[2,256,8,64]{1,3,2,0:T(8,128)S(1)}, u32[]{:S(2)}, u32[]{:S(2)}) %collective-permute-start.6) | collective-permute-done | bytes 1048608 | tf_op jit(solution)/shard_map/ppermute | solution.py:18
  140.8 0.3 subtract_reduce_fusion
  141.2 1.6 %collective-permute-start.7 = (f32[7,256,1]{1,2,0:T(1,128)S(1)}, f32[7,256,1]{1,2,0:T(1,128)S(1)}, u32[]{:S(2)}, u32[]{:S(2)}) collective-permute-start(f32[7,256,1]{1,2,0:T(1,128)S(1)} %broadcast_select_fusion.4), channel_id=1, source_target_pairs={{0,2},{2,0},{1,3},{3,1},{4,6},{6,4},{5,7},{7,5},{8,10},{10,8},{9,1... | collective-permute-start | bytes 21512 | tf_op jit(solution)/shard_map/ppermute | solution.py:28
  142.8 2.1 %collective-permute-done.7 = f32[7,256,1]{1,2,0:T(1,128)S(1)} collective-permute-done((f32[7,256,1]{1,2,0:T(1,128)S(1)}, f32[7,256,1]{1,2,0:T(1,128)S(1)}, u32[]{:S(2)}, u32[]{:S(2)}) %collective-permute-start.7) | collective-permute-done | bytes 7200 | tf_op jit(solution)/shard_map/ppermute | solution.py:28
  145.0 0.6 slice_divide_fusion
  145.6 0.6 maximum_bitcast_fusion
  (21 shorter events, 1.0 us)
Async XLA Ops:
  23.5 1.9 %copy-start = (f32[2,1024,512]{2,1,0:T(8,128)}, f32[2,1024,512]{2,1,0:T(8,128)S(1)}, u32[]{:S(2)}) copy-start(f32[2,1024,512]{2,1,0:T(8,128)S(1)} %shard_map.41) | copy-start | bytes 12582916
  25.6 27.4 %collective-permute-start = (f32[2,256,512]{2,1,0:T(8,128)S(1)}, f32[2,256,512]{2,1,0:T(8,128)S(1)}, u32[]{:S(2)}, u32[]{:S(2)}) collective-permute-start(f32[2,256,512]{2,1,0:T(8,128)S(1)} %get-tuple-element.12), channel_id=1, source_target_pairs={{0,4},{1,5},{2,6},{3,7},{16,20},{17,21},{18,22},{19,23}} | collective-permute-start | bytes 3145736 | tf_op jit(solution)/shard_map/ppermute | solution.py:132
  30.6 28.2 %collective-permute-start.3 = (f32[2,256,512]{2,1,0:T(8,128)S(1)}, f32[2,256,512]{2,1,0:T(8,128)}, u32[]{:S(2)}, u32[]{:S(2)}) collective-permute-start(f32[2,256,512]{2,1,0:T(8,128)S(1)} %get-tuple-element.13), channel_id=1, source_target_pairs={{12,8},{13,9},{14,10},{15,11},{28,24},{29,25},{30,26},{31,27}} | collective-permute-start | bytes 3145736 | tf_op jit(solution)/shard_map/ppermute | solution.py:133
  54.4 25.9 %collective-permute-start.1 = (f32[2,256,512]{2,1,0:T(8,128)S(1)}, f32[2,256,512]{2,1,0:T(8,128)S(1)}, u32[]{:S(2)}, u32[]{:S(2)}) collective-permute-start(f32[2,256,512]{2,1,0:T(8,128)S(1)} %bitcast_add_fusion.2), channel_id=1, source_target_pairs={{0,4},{4,8},{1,5},{5,9},{2,6},{6,10},{3,7},{7,11},{16,20},{20,24},... | collective-permute-start | bytes 3145736 | tf_op jit(solution)/shard_map/ppermute | solution.py:132
  84.0 5.8 %collective-permute-start.4 = (f32[2,256,512]{2,1,0:T(8,128)}, f32[2,256,512]{2,1,0:T(8,128)S(1)}, u32[]{:S(2)}, u32[]{:S(2)}) collective-permute-start(f32[2,256,512]{2,1,0:T(8,128)} %get-tuple-element.11), channel_id=1, source_target_pairs={{8,4},{12,8},{9,5},{13,9},{10,6},{14,10},{11,7},{15,11},{24,20},{2... | collective-permute-start | bytes 3145736 | tf_op jit(solution)/shard_map/ppermute | solution.py:133
  84.8 26.0 %collective-permute-start.2 = (f32[2,256,512]{2,1,0:T(8,128)}, f32[2,256,512]{2,1,0:T(8,128)S(1)}, u32[]{:S(2)}, u32[]{:S(2)}) collective-permute-start(f32[2,256,512]{2,1,0:T(8,128)} %get-tuple-element.10), channel_id=1, source_target_pairs={{0,4},{4,8},{8,12},{1,5},{5,9},{9,13},{2,6},{6,10},{10,14},{3,7},{... | collective-permute-start | bytes 3145736 | tf_op jit(solution)/shard_map/ppermute | solution.py:132
  91.2 44.5 %collective-permute-start.5 = (f32[2,256,512]{2,1,0:T(8,128)S(1)}, f32[2,256,512]{2,1,0:T(8,128)S(1)}, u32[]{:S(2)}, u32[]{:S(2)}) collective-permute-start(f32[2,256,512]{2,1,0:T(8,128)S(1)} %bitcast_add_fusion.1), channel_id=1, source_target_pairs={{4,0},{8,4},{12,8},{5,1},{9,5},{13,9},{6,2},{10,6},{14,10},{7,3},{... | collective-permute-start | bytes 3145736 | tf_op jit(solution)/shard_map/ppermute | solution.py:133
  137.9 2.7 %collective-permute-start.6 = (f32[2,256,8,64]{1,3,2,0:T(8,128)S(1)}, f32[2,256,8,64]{1,3,2,0:T(8,128)S(1)}, u32[]{:S(2)}, u32[]{:S(2)}) collective-permute-start(f32[2,256,8,64]{1,3,2,0:T(8,128)S(1)} %pad_maximum_fusion), channel_id=1, source_target_pairs={{0,1},{1,0},{2,3},{3,2},{4,5},{5,4},{6,7},{7,6},{8,9},{9,8},{10,11... | collective-permute-start | bytes 3145736 | tf_op jit(solution)/shard_map/ppermute | solution.py:18
  141.2 3.7 %collective-permute-start.7 = (f32[7,256,1]{1,2,0:T(1,128)S(1)}, f32[7,256,1]{1,2,0:T(1,128)S(1)}, u32[]{:S(2)}, u32[]{:S(2)}) collective-permute-start(f32[7,256,1]{1,2,0:T(1,128)S(1)} %broadcast_select_fusion.4), channel_id=1, source_target_pairs={{0,2},{2,0},{1,3},{3,1},{4,6},{6,4},{5,7},{7,5},{8,10},{10,8},{9,1... | collective-permute-start | bytes 21512 | tf_op jit(solution)/shard_map/ppermute | solution.py:28

commit v5 on v3

--- a/solution.py
+++ b/solution.py
@@ -68,7 +68,7 @@
     return jnp.concatenate([jnp.stack([zero_lag, lag_re, lag_im]), pair], axis=0)
 
 
-def complex_kernel(w_ref, x_ref, o_ref):
+def complex_kernel(half_ref, w_ref, x_ref, o_ref):
     bt = w_ref.shape[1]
     rows = w_ref[...].reshape(2 * bt, w_ref.shape[2])
     with_re = jnp.dot(rows, x_ref[0], preferred_element_type=jnp.float32)
@@ -87,49 +87,71 @@
         o_ref[1] += imag
 
 
-def partials(signal, weights):
+def partials(signal, weights, half=None):
     w = weights[:, 0]
     x = signal[:, 0]
     beams, elems = w.shape[1], w.shape[2]
     samples = x.shape[2]
-    bt = min(BEAM_TILE, beams)
+    rows = beams if half is None else beams // 2
+    bt = min(BEAM_TILE, rows)
     tk = min(ELEM_TILE, elems)
+    tiles = rows // bt
+    if half is None:
+        half = jnp.zeros((1,), jnp.int32)
     return pl.pallas_call(
         complex_kernel,
-        out_shape=jax.ShapeDtypeStruct((2, beams, samples), jnp.float32),
-        grid=(beams // bt, elems // tk),
-        in_specs=[
-            pl.BlockSpec((2, bt, tk), lambda i, k: (0, i, k)),
-            pl.BlockSpec((2, tk, samples), lambda i, k: (0, k, 0)),
-        ],
-        out_specs=pl.BlockSpec((2, bt, samples), lambda i, k: (0, i, 0)),
+        out_shape=jax.ShapeDtypeStruct((2, rows, samples), jnp.float32),
+        grid_spec=pltpu.PrefetchScalarGridSpec(
+            num_scalar_prefetch=1,
+            grid=(tiles, elems // tk),
+            in_specs=[
+                pl.BlockSpec((2, bt, tk), lambda i, k, h: (0, h[0] * tiles + i, k)),
+                pl.BlockSpec((2, tk, samples), lambda i, k, h: (0, k, 0)),
+            ],
+            out_specs=pl.BlockSpec((2, bt, samples), lambda i, k, h: (0, i, 0)),
+        ),
         compiler_params=pltpu.CompilerParams(
             dimension_semantics=("arbitrary", "arbitrary"), vmem_limit_bytes=48 * 1024 * 1024
         ),
         cost_estimate=pl.CostEstimate(
-            flops=8 * beams * elems * samples,
+            flops=8 * rows * elems * samples,
             transcendentals=0,
-            bytes_accessed=4 * beams * elems + 4 * elems * samples * (beams // bt) + 8 * beams * samples,
-        ),
-    )(w, x)
-
-
-def line_scatter(part, n_elem):
+            bytes_accessed=4 * rows * elems + 4 * elems * samples * tiles + 8 * rows * samples,
+        ),
+    )(half, w, x)
+
+
+def line_scatter(signal, weights, n_elem):
     me = lax.axis_index("elem")
-    blocks = part.reshape(2, n_elem, part.shape[1] // n_elem, part.shape[2])
+    lower = me >= n_elem // 2
+    first_base = jnp.where(lower, 0, n_elem // 2)
+    second_base = n_elem // 2 - first_base
+    first = partials(signal, weights, (1 - lower.astype(jnp.int32)).reshape(1))
+    second = partials(signal, weights, lower.astype(jnp.int32).reshape(1))
+    count = n_elem // 2
+    first = first.reshape(2, count, first.shape[1] // count, first.shape[2])
+    second = second.reshape(2, count, second.shape[1] // count, second.shape[2])
+
+    def block(q, late):
+        from_first = lax.dynamic_index_in_dim(first, jnp.clip(q - first_base, 0, count - 1), 1, False)
+        if not late:
+            return from_first
+        from_second = lax.dynamic_index_in_dim(second, jnp.clip(q - second_base, 0, count - 1), 1, False)
+        in_first = (q >= first_base) & (q < first_base + count)
+        return jnp.where(in_first, from_first, from_second)
+
     got_right = None
     got_left = None
     for step in range(1, n_elem):
-        to_right = lax.dynamic_index_in_dim(blocks, jnp.clip(me + n_elem - step, 0, n_elem - 1), 1, False)
-        to_left = lax.dynamic_index_in_dim(blocks, jnp.clip(me - n_elem + step, 0, n_elem - 1), 1, False)
+        late = step > n_elem // 2
+        to_right = block(me + n_elem - step, late)
+        to_left = block(me - n_elem + step, late)
         if got_right is not None:
             to_right = to_right + got_right
             to_left = to_left + got_left
         got_right = lax.ppermute(to_right, "elem", [(c, c + 1) for c in range(step)])
         got_left = lax.ppermute(to_left, "elem", [(c, c - 1) for c in range(n_elem - step, n_elem)])
-    own = lax.dynamic_index_in_dim(blocks, me, 1, False)
-    if got_right is None:
-        return own
+    own = lax.dynamic_index_in_dim(second, jnp.clip(me - second_base, 0, count - 1), 1, False)
     return own + got_right + got_left
 
 
@@ -138,10 +160,10 @@
     samples = signal.shape[3]
     gates = samples // PULSES
     beams = weights.shape[2]
-    part = partials(signal, weights)
-    if n_elem <= 8:
-        summed = line_scatter(part, n_elem)
+    if 2 <= n_elem <= 8 and n_elem % 2 == 0:
+        summed = line_scatter(signal, weights, n_elem)
     else:
+        part = partials(signal, weights)
         summed = lax.psum_scatter(part, "elem", scatter_dimension=1, tiled=True)
     stats = beam_stats(summed, gates)
     padded = with_halo(stats, "gate", 2)

time: 131 us -> 120 us (0.916)
  waiting for transfers between devices: 55.1 us -> 44.3 us
  Pallas kernels: 22.9 us -> 24.7 us
    ppermute x3, waiting for transfers between devices: 43.3 us -> 32.4 us  [line_scatter(): lax.ppermute(to_right, 'elem', [(c, c + 1) for c in range(step)])]
    dynamic_slice x8 -> x7, local copies, waits for them, and re-layouts: 15 us -> 10.2 us  [the longest x5 8.1 us: block(): lax.dynamic_index_in_dim(first, jnp.clip(q - first_base, 0, count - 1), 1...]
    unnamed x0 -> x8, local copies, waits for them, and re-layouts: none -> 3.54 us
    pallas_call x1 -> x2, Pallas kernels: 22.9 us -> 24.7 us  [partials(): pl.pallas_call(complex_kernel, out_shape=jax.ShapeDtypeStruct((2, rows, s...]
  transfers between devices with their start and end apart: 8 -> 8, of which waited for: 6 -> 5; matrix products, arithmetic and copies ran while one was open for 16% -> 16% of each run, Pallas kernels for 0% -> 10%
where the time goes in v5:
time: 120 us
  waiting for transfers between devices  44.3 us (37%)
  Pallas kernels  24.7 us (21%)
  starting transfers between devices  22.2 us (18%)
  local copies, waits for them, and re-layouts  13.8 us (12%)
  other arithmetic  13.6 us (11%)
    ppermute x3, waiting for transfers between devices, line_scatter(): lax.ppermute(to_right, 'elem', [(c, c + 1) for c in range(step)])  32.4 us
    pallas_call x2, Pallas kernels, partials(): pl.pallas_call(complex_kernel, out_shape=jax.ShapeDtypeStruct((2, rows, s...  24.7 us
    ppermute x3, starting transfers between devices, line_scatter(): lax.ppermute(to_right, 'elem', [(c, c + 1) for c in range(step)])  16 us
    dynamic_slice x5, local copies, waits for them, and re-layouts, block(): lax.dynamic_index_in_dim(first, jnp.clip(q - first_base, 0, count - 1), 1...  8.1 us
    ppermute x3, waiting for transfers between devices, line_scatter(): lax.ppermute(to_left, 'elem', [(c, c - 1) for c in range(n_elem - step, n...  7.45 us
    add x2, other arithmetic, line_scatter(): to_right = to_right + got_right  5.1 us
    add x2, other arithmetic, line_scatter(): to_left = to_left + got_left  4.85 us
    ppermute x3, starting transfers between devices, line_scatter(): lax.ppermute(to_left, 'elem', [(c, c - 1) for c in range(n_elem - step, n...  4.56 us
  transfers between devices with their start and end apart: 8, of which 5 were waited for; matrix products, arithmetic and copies ran while one was open for 16% of the time, Pallas kernels for 10%

profile of v5, /device:TPU:0, one launch (start us, length us, event | category | flops | bytes accessed | tf_op | source)
XLA Modules:
  0.0 119.5 jit_solution(11832588115155610432)
XLA Ops:
  0.7 12.4 %shard_map.42 = f32[2,512,512]{2,1,0:T(8,128)S(1)} custom-call(s32[1]{0:T(128)} %bitcast.5.half_ref, bf16[2,1024,4096]{2,1,0:T(8,128)(2,1)} %bitcast.52, bf16[2,4096,512]{2,1,0:T(8,128)(2,1)} %bitcast.54), custom_call_target="tpu_custom_call" | custom-call | flops 8589934592 | bytes 18874368 | tf_op jit(solution)/shard_map/pallas_call | solution.py:101
  13.0 2.4 %constant_dynamic-slice_fusion.7 = (f32[2,1,256,512]{3,2,1,0:T(8,128)S(1)}, f32[2,1,256,512]{3,2,1,0:T(8,128)}, f32[2,1,256,512]{3,2,1,0:T(8,128)S(1)}, f32[2,1,...) fusion(f32[2,2,256,512]{3,2,1,0:T(8,128)S(1)} %bitcast.40, s32[]{:T(128)S(6)} %min.29, ...), kind=kLoop, calls=%fused_computation.50 | loop fusion | bytes 12582936 | tf_op jit(solution)/shard_map/jit(dynamic_index_in_dim)/dynamic_slice | solution.py:136
  15.4 2.5 %copy.10 = f32[2,1,256,512]{2,3,0,1:T(8,128)} copy(f32[2,1,256,512]{3,2,1,0:T(8,128)} %get-tuple-element.18) | data formatting | bytes 2097152 | tf_op jit(solution)/shard_map/jit(dynamic_index_in_dim)/dynamic_slice | solution.py:136
  17.9 6.0 %collective-permute-start = (f32[2,256,512]{1,2,0:T(8,128)}, f32[2,256,512]{1,2,0:T(8,128)}, u32[]{:S(2)}, u32[]{:S(2)}) collective-permute-start(f32[2,256,512]{1,2,0:T(8,128)} %bitcast.51), channel_id=1, source_target_pairs={{0,4},{1,5},{2,6},{3,7},{16,20},{17,21},{18,22},{19,23}} | collective-permute-start | bytes 3145736 | tf_op jit(solution)/shard_map/ppermute | solution.py:152
  23.9 1.3 %copy.14 = f32[2,1,256,512]{2,3,0,1:T(8,128)} copy(f32[2,1,256,512]{3,2,1,0:T(8,128)S(1)} %get-tuple-element.17) | data formatting | bytes 2097152 | tf_op jit(solution)/shard_map/jit(dynamic_index_in_dim)/dynamic_slice | solution.py:136
  25.2 1.6 %collective-permute-start.3 = (f32[2,256,512]{1,2,0:T(8,128)}, f32[2,256,512]{1,2,0:T(8,128)}, u32[]{:S(2)}, u32[]{:S(2)}) collective-permute-start(f32[2,256,512]{1,2,0:T(8,128)} %bitcast.50), channel_id=1, source_target_pairs={{12,8},{13,9},{14,10},{15,11},{28,24},{29,25},{30,26},{31,27}} | collective-permute-start | bytes 3145736 | tf_op jit(solution)/shard_map/ppermute | solution.py:153
  27.6 1.6 %copy.13 = f32[2,1,256,512]{2,3,0,1:T(8,128)S(1)} copy(f32[2,1,256,512]{3,2,1,0:T(8,128)} %get-tuple-element.16) | data formatting | bytes 2097152 | tf_op jit(solution)/shard_map/jit(dynamic_index_in_dim)/dynamic_slice | solution.py:136
  29.1 16.5 %collective-permute-done = f32[2,256,512]{1,2,0:T(8,128)} collective-permute-done((f32[2,256,512]{1,2,0:T(8,128)}, f32[2,256,512]{1,2,0:T(8,128)}, u32[]{:S(2)}, u32[]{:S(2)}) %collective-permute-start) | collective-permute-done | bytes 1048608 | tf_op jit(solution)/shard_map/ppermute | solution.py:152
  45.6 2.4 %bitcast_add_fusion.2 = f32[2,256,512]{1,2,0:T(8,128)} fusion(f32[2,256,512]{1,2,0:T(8,128)} %collective-permute-done, f32[2,1,256,512]{2,3,0,1:T(8,128)S(1)} %copy.9), kind=kLoop, calls=%fused_computation.3 | loop fusion | flops 262144 | bytes 3145728 | tf_op jit(solution)/shard_map/add | solution.py:150
  48.0 5.4 %collective-permute-start.1 = (f32[2,256,512]{1,2,0:T(8,128)}, f32[2,256,512]{1,2,0:T(8,128)}, u32[]{:S(2)}, u32[]{:S(2)}) collective-permute-start(f32[2,256,512]{1,2,0:T(8,128)} %bitcast_add_fusion.2), channel_id=1, source_target_pairs={{0,4},{4,8},{1,5},{5,9},{2,6},{6,10},{3,7},{7,11},{16,20},{20,24},... | collective-permute-start | bytes 3145736 | tf_op jit(solution)/shard_map/ppermute | solution.py:152
  53.4 2.4 %bitcast_add_fusion = f32[2,256,512]{1,2,0:T(8,128)} fusion(f32[2,256,512]{1,2,0:T(8,128)} %collective-permute-done.3, f32[2,1,256,512]{2,3,0,1:T(8,128)S(1)} %copy.13), kind=kLoop, calls=%fused_computation.1 | loop fusion | flops 262144 | bytes 3145728 | tf_op jit(solution)/shard_map/add | solution.py:151
  55.7 1.6 %collective-permute-start.4 = (f32[2,256,512]{1,2,0:T(8,128)}, f32[2,256,512]{1,2,0:T(8,128)}, u32[]{:S(2)}, u32[]{:S(2)}) collective-permute-start(f32[2,256,512]{1,2,0:T(8,128)} %bitcast_add_fusion), channel_id=1, source_target_pairs={{8,4},{12,8},{9,5},{13,9},{10,6},{14,10},{11,7},{15,11},{24,20},{2... | collective-permute-start | bytes 3145736 | tf_op jit(solution)/shard_map/ppermute | solution.py:153
  57.4 12.3 %shard_map.41 = f32[2,512,512]{2,1,0:T(8,128)S(1)} custom-call(s32[1]{0:T(128)} %bitcast.half_ref, bf16[2,1024,4096]{2,1,0:T(8,128)(2,1)} %bitcast.53, bf16[2,4096,512]{2,1,0:T(8,128)(2,1)} %bitcast.55), custom_call_target="tpu_custom_call" | custom-call | flops 8589934592 | bytes 18874368 | tf_op jit(solution)/shard_map/pallas_call | solution.py:101
  69.7 1.8 %constant_dynamic-slice_fusion.8 = (f32[2,1,256,512]{3,2,1,0:T(8,128)}, f32[2,1,256,512]{3,2,1,0:T(8,128)S(1)}, f32[2,1,256,512]{3,2,1,0:T(8,128)}) fusion(f32[2,2,256,512]{3,2,1,0:T(8,128)S(1)} %bitcast.41, s32[]{:T(128)S(6)} %min.28, s32[]{:T(128)S(6)} %min.30, s32[]{:T(128)S(6)} %min.34), kind=kLoop, calls=%fused_computation.51 | loop fusion | bytes 6291468 | tf_op jit(solution)/shard_map/jit(dynamic_index_in_dim)/dynamic_slice | solution.py:154
  73.2 1.6 %copy.18 = f32[2,1,256,512]{2,3,0,1:T(8,128)S(1)} copy(f32[2,1,256,512]{3,2,1,0:T(8,128)} %get-tuple-element.14) | data formatting | bytes 2097152
  74.8 2.7 %bitcast_add_fusion.3 = f32[2,256,512]{1,2,0:T(8,128)} fusion(f32[2,256,512]{1,2,0:T(8,128)} %collective-permute-done.1, f32[2,1,256,512]{2,3,0,1:T(8,128)S(1)} %copy.15, f32[2,1,256,512]{2,3,0,1:T(8,128)} %copy.16, pred[]{:T(512)S(6)} %and.9), kind=kLoop, calls=%fused_computation.4 | loop fusion | flops 524288 | bytes 4194305 | tf_op jit(solution)/shard_map/add | solution.py:150
  77.5 4.6 %collective-permute-start.2 = (f32[2,256,512]{1,2,0:T(8,128)}, f32[2,256,512]{1,2,0:T(8,128)}, u32[]{:S(2)}, u32[]{:S(2)}) collective-permute-start(f32[2,256,512]{1,2,0:T(8,128)} %bitcast_add_fusion.3), channel_id=1, source_target_pairs={{0,4},{4,8},{8,12},{1,5},{5,9},{9,13},{2,6},{6,10},{10,14},{3,7},{... | collective-permute-start | bytes 3145736 | tf_op jit(solution)/shard_map/ppermute | solution.py:152
  82.1 2.5 %bitcast_add_fusion.1 = f32[2,256,512]{1,2,0:T(8,128)} fusion(f32[2,256,512]{1,2,0:T(8,128)} %collective-permute-done.4, f32[2,1,256,512]{2,3,0,1:T(8,128)S(1)} %copy.17, f32[2,1,256,512]{2,3,0,1:T(8,128)S(1)} %copy.18, pred[]{:T(512)S(6)} %and.10), kind=kLoop, calls=%fused_computation.2 | loop fusion | flops 524288 | bytes 4194305 | tf_op jit(solution)/shard_map/add | solution.py:151
  86.2 15.9 %collective-permute-done.2 = f32[2,256,512]{1,2,0:T(8,128)} collective-permute-done((f32[2,256,512]{1,2,0:T(8,128)}, f32[2,256,512]{1,2,0:T(8,128)}, u32[]{:S(2)}, u32[]{:S(2)}) %collective-permute-start.2) | collective-permute-done | bytes 1048608 | tf_op jit(solution)/shard_map/ppermute | solution.py:152
  102.2 7.4 %collective-permute-done.5 = f32[2,256,512]{1,2,0:T(8,128)S(1)} collective-permute-done((f32[2,256,512]{1,2,0:T(8,128)}, f32[2,256,512]{1,2,0:T(8,128)S(1)}, u32[]{:S(2)}, u32[]{:S(2)}) %collective-permute-start.5) | collective-permute-done | bytes 1048608 | tf_op jit(solution)/shard_map/ppermute | solution.py:153
  109.6 1.4 %fusion = f32[2,256,512]{1,2,0:T(8,128)S(1)} fusion(f32[2,256,512]{1,2,0:T(8,128)S(1)} %collective-permute-done.5, f32[2,256,512]{1,2,0:T(8,128)} %collective-permute-done.2, f32[2,1,256,512]{2,3,0,1:T(8,128)S(1)} %copy.6), kind=kLoop, calls=%fused_computation.6 | loop fusion | flops 524288 | bytes 4194304 | tf_op jit(solution)/shard_map/add | solution.py:155
  111.7 2.3 %collective-permute-done.6 = f32[2,256,8,64]{1,3,2,0:T(8,128)S(1)} collective-permute-done((f32[2,256,8,64]{1,3,2,0:T(8,128)S(1)}, f32[2,256,8,64]{1,3,2,0:T(8,128)S(1)}, u32[]{:S(2)}, u32[]{:S(2)}) %collective-permute-start.6) | collective-permute-done | bytes 1048608 | tf_op jit(solution)/shard_map/ppermute | solution.py:16
  114.5 1.6 %collective-permute-start.7 = (f32[7,256,1]{1,2,0:T(1,128)S(1)}, f32[7,256,1]{1,2,0:T(1,128)S(1)}, u32[]{:S(2)}, u32[]{:S(2)}) collective-permute-start(f32[7,256,1]{1,2,0:T(1,128)S(1)} %broadcast_select_fusion.4), channel_id=1, source_target_pairs={{0,2},{2,0},{1,3},{3,1},{4,6},{6,4},{5,7},{7,5},{8,10},{10,8},{9,1... | collective-permute-start | bytes 21512 | tf_op jit(solution)/shard_map/ppermute | solution.py:26
  116.1 2.1 %collective-permute-done.7 = f32[7,256,1]{1,2,0:T(1,128)S(1)} collective-permute-done((f32[7,256,1]{1,2,0:T(1,128)S(1)}, f32[7,256,1]{1,2,0:T(1,128)S(1)}, u32[]{:S(2)}, u32[]{:S(2)}) %collective-permute-start.7) | collective-permute-done | bytes 7200 | tf_op jit(solution)/shard_map/ppermute | solution.py:26
  (33 shorter events, 6.3 us)
Async XLA Ops:
  17.9 27.7 %collective-permute-start = (f32[2,256,512]{1,2,0:T(8,128)}, f32[2,256,512]{1,2,0:T(8,128)}, u32[]{:S(2)}, u32[]{:S(2)}) collective-permute-start(f32[2,256,512]{1,2,0:T(8,128)} %bitcast.51), channel_id=1, source_target_pairs={{0,4},{1,5},{2,6},{3,7},{16,20},{17,21},{18,22},{19,23}} | collective-permute-start | bytes 3145736 | tf_op jit(solution)/shard_map/ppermute | solution.py:152
  25.2 28.1 %collective-permute-start.3 = (f32[2,256,512]{1,2,0:T(8,128)}, f32[2,256,512]{1,2,0:T(8,128)}, u32[]{:S(2)}, u32[]{:S(2)}) collective-permute-start(f32[2,256,512]{1,2,0:T(8,128)} %bitcast.50), channel_id=1, source_target_pairs={{12,8},{13,9},{14,10},{15,11},{28,24},{29,25},{30,26},{31,27}} | collective-permute-start | bytes 3145736 | tf_op jit(solution)/shard_map/ppermute | solution.py:153
  48.0 26.8 %collective-permute-start.1 = (f32[2,256,512]{1,2,0:T(8,128)}, f32[2,256,512]{1,2,0:T(8,128)}, u32[]{:S(2)}, u32[]{:S(2)}) collective-permute-start(f32[2,256,512]{1,2,0:T(8,128)} %bitcast_add_fusion.2), channel_id=1, source_target_pairs={{0,4},{4,8},{1,5},{5,9},{2,6},{6,10},{3,7},{7,11},{16,20},{20,24},... | collective-permute-start | bytes 3145736 | tf_op jit(solution)/shard_map/ppermute | solution.py:152
  55.7 26.4 %collective-permute-start.4 = (f32[2,256,512]{1,2,0:T(8,128)}, f32[2,256,512]{1,2,0:T(8,128)}, u32[]{:S(2)}, u32[]{:S(2)}) collective-permute-start(f32[2,256,512]{1,2,0:T(8,128)} %bitcast_add_fusion), channel_id=1, source_target_pairs={{8,4},{12,8},{9,5},{13,9},{10,6},{14,10},{11,7},{15,11},{24,20},{2... | collective-permute-start | bytes 3145736 | tf_op jit(solution)/shard_map/ppermute | solution.py:153
  71.5 1.3 %copy-start.1 = (f32[2,1,256,512]{3,2,1,0:T(8,128)S(1)}, f32[2,1,256,512]{3,2,1,0:T(8,128)}, u32[]{:S(2)}) copy-start(f32[2,1,256,512]{3,2,1,0:T(8,128)} %get-tuple-element.20) | copy-start | bytes 3145732
  77.5 8.4 %copy-start = (f32[2,1,256,512]{3,2,1,0:T(8,128)S(1)}, f32[2,1,256,512]{3,2,1,0:T(8,128)}, u32[]{:S(2)}) copy-start(f32[2,1,256,512]{3,2,1,0:T(8,128)} %get-tuple-element.12) | copy-start | bytes 3145732
  77.5 24.6 %collective-permute-start.2 = (f32[2,256,512]{1,2,0:T(8,128)}, f32[2,256,512]{1,2,0:T(8,128)}, u32[]{:S(2)}, u32[]{:S(2)}) collective-permute-start(f32[2,256,512]{1,2,0:T(8,128)} %bitcast_add_fusion.3), channel_id=1, source_target_pairs={{0,4},{4,8},{8,12},{1,5},{5,9},{9,13},{2,6},{6,10},{10,14},{3,7},{... | collective-permute-start | bytes 3145736 | tf_op jit(solution)/shard_map/ppermute | solution.py:152
  84.6 25.0 %collective-permute-start.5 = (f32[2,256,512]{1,2,0:T(8,128)}, f32[2,256,512]{1,2,0:T(8,128)S(1)}, u32[]{:S(2)}, u32[]{:S(2)}) collective-permute-start(f32[2,256,512]{1,2,0:T(8,128)} %bitcast_add_fusion.1), channel_id=1, source_target_pairs={{4,0},{8,4},{12,8},{5,1},{9,5},{13,9},{6,2},{10,6},{14,10},{7,3},{... | collective-permute-start | bytes 3145736 | tf_op jit(solution)/shard_map/ppermute | solution.py:153
  111.2 2.7 %collective-permute-start.6 = (f32[2,256,8,64]{1,3,2,0:T(8,128)S(1)}, f32[2,256,8,64]{1,3,2,0:T(8,128)S(1)}, u32[]{:S(2)}, u32[]{:S(2)}) collective-permute-start(f32[2,256,8,64]{1,3,2,0:T(8,128)S(1)} %pad_maximum_fusion), channel_id=1, source_target_pairs={{0,1},{1,0},{2,3},{3,2},{4,5},{5,4},{6,7},{7,6},{8,9},{9,8},{10,11... | collective-permute-start | bytes 3145736 | tf_op jit(solution)/shard_map/ppermute | solution.py:16
  114.5 3.7 %collective-permute-start.7 = (f32[7,256,1]{1,2,0:T(1,128)S(1)}, f32[7,256,1]{1,2,0:T(1,128)S(1)}, u32[]{:S(2)}, u32[]{:S(2)}) collective-permute-start(f32[7,256,1]{1,2,0:T(1,128)S(1)} %broadcast_select_fusion.4), channel_id=1, source_target_pairs={{0,2},{2,0},{1,3},{3,1},{4,6},{6,4},{5,7},{7,5},{8,10},{10,8},{9,1... | collective-permute-start | bytes 21512 | tf_op jit(solution)/shard_map/ppermute | solution.py:26

commit v6 on v5

--- a/solution.py
+++ b/solution.py
@@ -121,37 +121,96 @@
     )(half, w, x)
 
 
+def block_kernel(index_ref, w_ref, x_ref, o_ref, acc_ref):
+    bt = w_ref.shape[1]
+    rows = w_ref[...].reshape(2 * bt, w_ref.shape[2])
+    with_re = jnp.dot(rows, x_ref[0], preferred_element_type=jnp.float32)
+    with_im = jnp.dot(rows, x_ref[1], preferred_element_type=jnp.float32)
+    real = with_re[:bt] + with_im[bt:]
+    imag = with_im[:bt] - with_re[bt:]
+    step = pl.program_id(0)
+
+    @pl.when(step == 0)
+    def _():
+        acc_ref[0] = real
+        acc_ref[1] = imag
+
+    @pl.when(step > 0)
+    def _():
+        acc_ref[0] += real
+        acc_ref[1] += imag
+
+    @pl.when(step == pl.num_programs(0) - 1)
+    def _():
+        o_ref[0] = acc_ref[0].T
+        o_ref[1] = acc_ref[1].T
+
+
+def block_partial(signal, weights, index, count):
+    w = weights[:, 0]
+    x = signal[:, 0]
+    elems = w.shape[2]
+    samples = x.shape[2]
+    tk = min(ELEM_TILE, elems)
+    return pl.pallas_call(
+        block_kernel,
+        out_shape=jax.ShapeDtypeStruct((2, samples, count), jnp.float32),
+        grid_spec=pltpu.PrefetchScalarGridSpec(
+            num_scalar_prefetch=1,
+            grid=(elems // tk,),
+            in_specs=[
+                pl.BlockSpec((2, count, tk), lambda k, b: (0, b[0], k)),
+                pl.BlockSpec((2, tk, samples), lambda k, b: (0, k, 0)),
+            ],
+            out_specs=pl.BlockSpec((2, samples, count), lambda k, b: (0, 0, 0)),
+            scratch_shapes=[pltpu.VMEM((2, count, samples), jnp.float32)],
+        ),
+        compiler_params=pltpu.CompilerParams(
+            dimension_semantics=("arbitrary",), vmem_limit_bytes=48 * 1024 * 1024
+        ),
+        cost_estimate=pl.CostEstimate(
+            flops=8 * count * elems * samples,
+            transcendentals=0,
+            bytes_accessed=4 * count * elems + 4 * elems * samples + 8 * count * samples,
+        ),
+    )(index.reshape(1), w, x)
+
+
 def line_scatter(signal, weights, n_elem):
     me = lax.axis_index("elem")
-    lower = me >= n_elem // 2
-    first_base = jnp.where(lower, 0, n_elem // 2)
-    second_base = n_elem // 2 - first_base
-    first = partials(signal, weights, (1 - lower.astype(jnp.int32)).reshape(1))
-    second = partials(signal, weights, lower.astype(jnp.int32).reshape(1))
-    count = n_elem // 2
-    first = first.reshape(2, count, first.shape[1] // count, first.shape[2])
-    second = second.reshape(2, count, second.shape[1] // count, second.shape[2])
-
-    def block(q, late):
-        from_first = lax.dynamic_index_in_dim(first, jnp.clip(q - first_base, 0, count - 1), 1, False)
-        if not late:
-            return from_first
-        from_second = lax.dynamic_index_in_dim(second, jnp.clip(q - second_base, 0, count - 1), 1, False)
-        in_first = (q >= first_base) & (q < first_base + count)
-        return jnp.where(in_first, from_first, from_second)
+    near = me < n_elem // 2
+    local = weights.shape[2] // n_elem
+
+    def order(c, q):
+        return n_elem - 1 - q if c < n_elem // 2 else q
+
+    made = []
+    for k in range(n_elem):
+        index = jnp.where(near, n_elem - 1 - k, k).astype(jnp.int32)
+        made.append(jnp.swapaxes(block_partial(signal, weights, index, local), 1, 2))
+
+    def pick(q, needed):
+        at = jnp.where(near, n_elem - 1 - q, q)
+        picked = made[needed[0]]
+        for k in needed[1:]:
+            picked = jnp.where(at == k, made[k], picked)
+        return picked
 
     got_right = None
     got_left = None
     for step in range(1, n_elem):
-        late = step > n_elem // 2
-        to_right = block(me + n_elem - step, late)
-        to_left = block(me - n_elem + step, late)
+        senders_right = range(step)
+        senders_left = range(n_elem - step, n_elem)
+        need_right = sorted({order(c, c + n_elem - step) for c in senders_right})
+        need_left = sorted({order(c, c - n_elem + step) for c in senders_left})
+        to_right = pick(me + n_elem - step, need_right)
+        to_left = pick(me - n_elem + step, need_left)
         if got_right is not None:
             to_right = to_right + got_right
             to_left = to_left + got_left
-        got_right = lax.ppermute(to_right, "elem", [(c, c + 1) for c in range(step)])
-        got_left = lax.ppermute(to_left, "elem", [(c, c - 1) for c in range(n_elem - step, n_elem)])
-    own = lax.dynamic_index_in_dim(second, jnp.clip(me - second_base, 0, count - 1), 1, False)
+        got_right = lax.ppermute(to_right, "elem", [(c, c + 1) for c in senders_right])
+        got_left = lax.ppermute(to_left, "elem", [(c, c - 1) for c in senders_left])
+    own = pick(me, sorted({order(c, c) for c in range(n_elem)}))
     return own + got_right + got_left
 
 

time: 120 us -> 112 us (0.933)
  local copies, waits for them, and re-layouts: 13.8 us -> 0.07 us
  Pallas kernels: 24.7 us -> 33.5 us
  other arithmetic: 13.6 us -> 9.71 us
  starting transfers between devices: 22.2 us -> 25.2 us
  waiting for transfers between devices: 44.3 us -> 42.6 us
    dynamic_slice x7 -> x0, local copies, waits for them, and re-layouts: 10.2 us -> none  [the longest x5 8.1 us: block(): lax.dynamic_index_in_dim(first, jnp.clip(q - first_base, 0, count - 1), 1...]
    pallas_call x2 -> x4, Pallas kernels: 24.7 us -> 33.5 us  [block_partial(): pl.pallas_call(block_kernel, out_shape=jax.ShapeDtypeStruct((2, samples,...]
    add x2 -> x0, other arithmetic: 4.85 us -> none  [line_scatter(): to_left = to_left + got_left]
    unnamed x8 -> x0, local copies, waits for them, and re-layouts: 3.54 us -> none
    ppermute x6, starting transfers between devices: 20.5 us -> 23.5 us  [the longest x3 18.9 us: line_scatter(): lax.ppermute(to_right, 'elem', [(c, c + 1) for c in senders_right])]
    ppermute x6, waiting for transfers between devices: 39.9 us -> 38.2 us  [the longest x3 34 us: line_scatter(): lax.ppermute(to_right, 'elem', [(c, c + 1) for c in senders_right])]
  transfers between devices with their start and end apart: 8 -> 8, of which waited for: 5 -> 6; matrix products, arithmetic and copies ran while one was open for 16% -> 0% of each run, Pallas kernels for 10% -> 22%
where the time goes in v6:
time: 112 us
  waiting for transfers between devices  42.6 us (38%)
  Pallas kernels  33.5 us (30%)
  starting transfers between devices  25.2 us (22%)
  other arithmetic  9.71 us (9%)
    ppermute x3, waiting for transfers between devices, line_scatter(): lax.ppermute(to_right, 'elem', [(c, c + 1) for c in senders_right])  34 us
    pallas_call x4, Pallas kernels, block_partial(): pl.pallas_call(block_kernel, out_shape=jax.ShapeDtypeStruct((2, samples,...  33.5 us
    ppermute x3, starting transfers between devices, line_scatter(): lax.ppermute(to_right, 'elem', [(c, c + 1) for c in senders_right])  18.9 us
    add x2, other arithmetic, line_scatter(): to_right = to_right + got_right  5.97 us
    ppermute x3, starting transfers between devices, line_scatter(): got_left = lax.ppermute(to_left, 'elem', [(c, c - 1) for c in senders_left])  4.64 us
    ppermute x3, waiting for transfers between devices, line_scatter(): got_left = lax.ppermute(to_left, 'elem', [(c, c - 1) for c in senders_left])  4.19 us
    ppermute x1, waiting for transfers between devices, swapped(): return lax.ppermute(value, axis, pairs)  2.26 us
  transfers between devices with their start and end apart: 8, of which 6 were waited for; matrix products, arithmetic and copies ran while one was open for 0% of the time, Pallas kernels for 22%

profile of v6, /device:TPU:0, one launch (start us, length us, event | category | flops | bytes accessed | tf_op | source)
XLA Modules:
  0.0 111.9 jit_solution(1593280414790924091)
XLA Ops:
  0.6 8.4 %shard_map.44 = f32[2,512,256]{2,1,0:T(8,128)S(1)} custom-call(s32[1]{0:T(128)} %bitcast.8.index_ref, bf16[2,1024,4096]{2,1,0:T(8,128)(2,1)} %bitcast.60, bf16[2,4096,512]{2,1,0:T(8,128)(2,1)} %bitcast.64), custom_call_target="tpu_custom_call" | custom-call | flops 4294967296 | bytes 13631488 | tf_op jit(solution)/shard_map/pallas_call | solution.py:155
  9.0 5.0 %collective-permute-start = (f32[2,256,512]{1,2,0:T(8,128)S(1)}, f32[2,256,512]{1,2,0:T(8,128)S(1)}, u32[]{:S(2)}, u32[]{:S(2)}) collective-permute-start(f32[2,256,512]{1,2,0:T(8,128)S(1)} %bitcast.58), channel_id=1, source_target_pairs={{0,4},{1,5},{2,6},{3,7},{16,20},{17,21},{18,22},{19,23}} | collective-permute-start | bytes 3145736 | tf_op jit(solution)/shard_map/ppermute | solution.py:211
  14.1 1.7 %collective-permute-start.3 = (f32[2,256,512]{1,2,0:T(8,128)S(1)}, f32[2,256,512]{1,2,0:T(8,128)}, u32[]{:S(2)}, u32[]{:S(2)}) collective-permute-start(f32[2,256,512]{1,2,0:T(8,128)S(1)} %bitcast.59), channel_id=1, source_target_pairs={{12,8},{13,9},{14,10},{15,11},{28,24},{29,25},{30,26},{31,27}} | collective-permute-start | bytes 3145736 | tf_op jit(solution)/shard_map/ppermute | solution.py:212
  15.7 8.4 %shard_map.43 = f32[2,512,256]{2,1,0:T(8,128)S(1)} custom-call(s32[1]{0:T(128)} %bitcast.6.index_ref, bf16[2,1024,4096]{2,1,0:T(8,128)(2,1)} %bitcast.61, bf16[2,4096,512]{2,1,0:T(8,128)(2,1)} %bitcast.65), custom_call_target="tpu_custom_call" | custom-call | flops 4294967296 | bytes 13631488 | tf_op jit(solution)/shard_map/pallas_call | solution.py:155
  24.1 12.3 %collective-permute-done = f32[2,256,512]{1,2,0:T(8,128)S(1)} collective-permute-done((f32[2,256,512]{1,2,0:T(8,128)S(1)}, f32[2,256,512]{1,2,0:T(8,128)S(1)}, u32[]{:S(2)}, u32[]{:S(2)}) %collective-permute-start) | collective-permute-done | bytes 1048608 | tf_op jit(solution)/shard_map/ppermute | solution.py:211
  36.4 2.8 %fusion.2 = (f32[2,256,512]{1,2,0:T(8,128)}, f32[2,256,512]{1,2,0:T(8,128)}) fusion(f32[2,256,512]{1,2,0:T(8,128)S(1)} %collective-permute-done, f32[2,512,256]{2,1,0:T(8,128)S(1)} %shard_map.43, pred[]{:T(512)S(6)} %eq.35, f32[2,512,256]{2,1,0:T(8,128)S(1)} %shard_map.44, f32[2,256,512]{1,2,0:T(8,128)} %collective-permute-done.3, pred[]{:T(512)S(6)} %eq.38), kind=kLoop, calls=%fused_computation.7 | loop fusion | flops 1048576 | bytes 6291458 | tf_op jit(solution)/shard_map/add | solution.py:209
  39.2 5.4 %collective-permute-start.1 = (f32[2,256,512]{1,2,0:T(8,128)}, f32[2,256,512]{1,2,0:T(8,128)}, u32[]{:S(2)}, u32[]{:S(2)}) collective-permute-start(f32[2,256,512]{1,2,0:T(8,128)} %get-tuple-element.14), channel_id=1, source_target_pairs={{0,4},{4,8},{1,5},{5,9},{2,6},{6,10},{3,7},{7,11},{16,20},{20,24},... | collective-permute-start | bytes 3145736 | tf_op jit(solution)/shard_map/ppermute | solution.py:211
  44.6 1.7 %collective-permute-start.4 = (f32[2,256,512]{1,2,0:T(8,128)}, f32[2,256,512]{1,2,0:T(8,128)}, u32[]{:S(2)}, u32[]{:S(2)}) collective-permute-start(f32[2,256,512]{1,2,0:T(8,128)} %get-tuple-element.15), channel_id=1, source_target_pairs={{8,4},{12,8},{9,5},{13,9},{10,6},{14,10},{11,7},{15,11},{24,20},{2... | collective-permute-start | bytes 3145736 | tf_op jit(solution)/shard_map/ppermute | solution.py:212
  46.3 8.4 %shard_map.41 = f32[2,512,256]{2,1,0:T(8,128)S(1)} custom-call(s32[1]{0:T(128)} %bitcast.index_ref, bf16[2,1024,4096]{2,1,0:T(8,128)(2,1)} %bitcast.62, bf16[2,4096,512]{2,1,0:T(8,128)(2,1)} %bitcast.66), custom_call_target="tpu_custom_call" | custom-call | flops 4294967296 | bytes 13631488 | tf_op jit(solution)/shard_map/pallas_call | solution.py:155
  54.6 8.4 %shard_map.42 = f32[2,512,256]{2,1,0:T(8,128)S(1)} custom-call(s32[1]{0:T(128)} %bitcast.4.index_ref, bf16[2,1024,4096]{2,1,0:T(8,128)(2,1)} %bitcast.63, bf16[2,4096,512]{2,1,0:T(8,128)(2,1)} %bitcast.67), custom_call_target="tpu_custom_call" | custom-call | flops 4294967296 | bytes 13631488 | tf_op jit(solution)/shard_map/pallas_call | solution.py:155
  63.0 2.4 %collective-permute-done.1 = f32[2,256,512]{1,2,0:T(8,128)} collective-permute-done((f32[2,256,512]{1,2,0:T(8,128)}, f32[2,256,512]{1,2,0:T(8,128)}, u32[]{:S(2)}, u32[]{:S(2)}) %collective-permute-start.1) | collective-permute-done | bytes 1048608 | tf_op jit(solution)/shard_map/ppermute | solution.py:211
  65.4 3.2 %fusion.1 = (f32[2,256,512]{1,2,0:T(8,128)}, f32[2,256,512]{1,2,0:T(8,128)}) fusion(f32[2,256,512]{1,2,0:T(8,128)} %collective-permute-done.1, f32[2,512,256]{2,1,0:T(8,128)S(1)} %shard_map.43, f32[2,512,256]{2,1,0:T(8,128)S(1)} %shard_map.42, f32[2,512,256]{2,1,0:T(8,128)S(1)} %shard_map.41, pred[]{:T(512)S(6)} %eq.34, pred[]{:T(512)S(6)} %eq.33, ...), kind=kLoop, calls=%fused_computation.6 | loop fusion | flops 1572864 | bytes 7340036 | tf_op jit(solution)/shard_map/add | solution.py:209
  68.6 8.5 %collective-permute-start.2 = (f32[2,256,512]{1,2,0:T(8,128)}, f32[2,256,512]{1,2,0:T(8,128)S(1)}, u32[]{:S(2)}, u32[]{:S(2)}) collective-permute-start(f32[2,256,512]{1,2,0:T(8,128)} %get-tuple-element.10), channel_id=1, source_target_pairs={{0,4},{4,8},{8,12},{1,5},{5,9},{9,13},{2,6},{6,10},{10,14},{3,7},{... | collective-permute-start | bytes 3145736 | tf_op jit(solution)/shard_map/ppermute | solution.py:211
  77.1 1.3 %collective-permute-start.5 = (f32[2,256,512]{1,2,0:T(8,128)}, f32[2,256,512]{1,2,0:T(8,128)}, u32[]{:S(2)}, u32[]{:S(2)}) collective-permute-start(f32[2,256,512]{1,2,0:T(8,128)} %get-tuple-element.11), channel_id=1, source_target_pairs={{4,0},{8,4},{12,8},{5,1},{9,5},{13,9},{6,2},{10,6},{14,10},{7,3},{... | collective-permute-start | bytes 3145736 | tf_op jit(solution)/shard_map/ppermute | solution.py:212
  78.4 19.3 %collective-permute-done.2 = f32[2,256,512]{1,2,0:T(8,128)S(1)} collective-permute-done((f32[2,256,512]{1,2,0:T(8,128)}, f32[2,256,512]{1,2,0:T(8,128)S(1)}, u32[]{:S(2)}, u32[]{:S(2)}) %collective-permute-start.2) | collective-permute-done | bytes 1048608 | tf_op jit(solution)/shard_map/ppermute | solution.py:211
  97.8 4.2 %collective-permute-done.5 = f32[2,256,512]{1,2,0:T(8,128)} collective-permute-done((f32[2,256,512]{1,2,0:T(8,128)}, f32[2,256,512]{1,2,0:T(8,128)}, u32[]{:S(2)}, u32[]{:S(2)}) %collective-permute-start.5) | collective-permute-done | bytes 1048608 | tf_op jit(solution)/shard_map/ppermute | solution.py:212
  101.9 1.5 %fusion.7 = f32[2,256,512]{1,2,0:T(8,128)S(1)} fusion(f32[2,256,512]{1,2,0:T(8,128)} %collective-permute-done.5, f32[2,256,512]{1,2,0:T(8,128)S(1)} %collective-permute-done.2, f32[2,512,256]{2,1,0:T(8,128)S(1)} %shard_map.42, f32[2,512,256]{2,1,0:T(8,128)S(1)} %shard_map.41, pred[]{:T(512)S(6)} %eq.32), kind=kLoop, calls=%fused_computation.13 | loop fusion | flops 786432 | bytes 5242881 | tf_op jit(solution)/shard_map/add | solution.py:214
  103.8 0.2 subtract_reduce_fusion.1
  104.1 2.3 %collective-permute-done.6 = f32[2,256,8,64]{1,3,2,0:T(8,128)S(1)} collective-permute-done((f32[2,256,8,64]{1,3,2,0:T(8,128)S(1)}, f32[2,256,8,64]{1,3,2,0:T(8,128)S(1)}, u32[]{:S(2)}, u32[]{:S(2)}) %collective-permute-start.6) | collective-permute-done | bytes 1048608 | tf_op jit(solution)/shard_map/ppermute | solution.py:16
  106.5 0.3 subtract_reduce_fusion
  106.9 1.6 %collective-permute-start.7 = (f32[7,256,1]{1,2,0:T(1,128)S(1)}, f32[7,256,1]{1,2,0:T(1,128)S(1)}, u32[]{:S(2)}, u32[]{:S(2)}) collective-permute-start(f32[7,256,1]{1,2,0:T(1,128)S(1)} %broadcast_select_fusion.4), channel_id=1, source_target_pairs={{0,2},{2,0},{1,3},{3,1},{4,6},{6,4},{5,7},{7,5},{8,10},{10,8},{9,1... | collective-permute-start | bytes 21512 | tf_op jit(solution)/shard_map/ppermute | solution.py:26
  108.5 2.1 %collective-permute-done.7 = f32[7,256,1]{1,2,0:T(1,128)S(1)} collective-permute-done((f32[7,256,1]{1,2,0:T(1,128)S(1)}, f32[7,256,1]{1,2,0:T(1,128)S(1)}, u32[]{:S(2)}, u32[]{:S(2)}) %collective-permute-start.7) | collective-permute-done | bytes 7200 | tf_op jit(solution)/shard_map/ppermute | solution.py:26
  110.7 0.6 slice_divide_fusion
  111.3 0.6 maximum_bitcast_fusion
  (18 shorter events, 0.6 us)
Async XLA Ops:
  9.0 27.4 %collective-permute-start = (f32[2,256,512]{1,2,0:T(8,128)S(1)}, f32[2,256,512]{1,2,0:T(8,128)S(1)}, u32[]{:S(2)}, u32[]{:S(2)}) collective-permute-start(f32[2,256,512]{1,2,0:T(8,128)S(1)} %bitcast.58), channel_id=1, source_target_pairs={{0,4},{1,5},{2,6},{3,7},{16,20},{17,21},{18,22},{19,23}} | collective-permute-start | bytes 3145736 | tf_op jit(solution)/shard_map/ppermute | solution.py:211
  14.1 22.3 %collective-permute-start.3 = (f32[2,256,512]{1,2,0:T(8,128)S(1)}, f32[2,256,512]{1,2,0:T(8,128)}, u32[]{:S(2)}, u32[]{:S(2)}) collective-permute-start(f32[2,256,512]{1,2,0:T(8,128)S(1)} %bitcast.59), channel_id=1, source_target_pairs={{12,8},{13,9},{14,10},{15,11},{28,24},{29,25},{30,26},{31,27}} | collective-permute-start | bytes 3145736 | tf_op jit(solution)/shard_map/ppermute | solution.py:212
  39.2 26.2 %collective-permute-start.1 = (f32[2,256,512]{1,2,0:T(8,128)}, f32[2,256,512]{1,2,0:T(8,128)}, u32[]{:S(2)}, u32[]{:S(2)}) collective-permute-start(f32[2,256,512]{1,2,0:T(8,128)} %get-tuple-element.14), channel_id=1, source_target_pairs={{0,4},{4,8},{1,5},{5,9},{2,6},{6,10},{3,7},{7,11},{16,20},{20,24},... | collective-permute-start | bytes 3145736 | tf_op jit(solution)/shard_map/ppermute | solution.py:211
  44.6 20.9 %collective-permute-start.4 = (f32[2,256,512]{1,2,0:T(8,128)}, f32[2,256,512]{1,2,0:T(8,128)}, u32[]{:S(2)}, u32[]{:S(2)}) collective-permute-start(f32[2,256,512]{1,2,0:T(8,128)} %get-tuple-element.15), channel_id=1, source_target_pairs={{8,4},{12,8},{9,5},{13,9},{10,6},{14,10},{11,7},{15,11},{24,20},{2... | collective-permute-start | bytes 3145736 | tf_op jit(solution)/shard_map/ppermute | solution.py:212
  68.6 29.1 %collective-permute-start.2 = (f32[2,256,512]{1,2,0:T(8,128)}, f32[2,256,512]{1,2,0:T(8,128)S(1)}, u32[]{:S(2)}, u32[]{:S(2)}) collective-permute-start(f32[2,256,512]{1,2,0:T(8,128)} %get-tuple-element.10), channel_id=1, source_target_pairs={{0,4},{4,8},{8,12},{1,5},{5,9},{9,13},{2,6},{6,10},{10,14},{3,7},{... | collective-permute-start | bytes 3145736 | tf_op jit(solution)/shard_map/ppermute | solution.py:211
  77.1 24.8 %collective-permute-start.5 = (f32[2,256,512]{1,2,0:T(8,128)}, f32[2,256,512]{1,2,0:T(8,128)}, u32[]{:S(2)}, u32[]{:S(2)}) collective-permute-start(f32[2,256,512]{1,2,0:T(8,128)} %get-tuple-element.11), channel_id=1, source_target_pairs={{4,0},{8,4},{12,8},{5,1},{9,5},{13,9},{6,2},{10,6},{14,10},{7,3},{... | collective-permute-start | bytes 3145736 | tf_op jit(solution)/shard_map/ppermute | solution.py:212
  103.6 2.7 %collective-permute-start.6 = (f32[2,256,8,64]{1,3,2,0:T(8,128)S(1)}, f32[2,256,8,64]{1,3,2,0:T(8,128)S(1)}, u32[]{:S(2)}, u32[]{:S(2)}) collective-permute-start(f32[2,256,8,64]{1,3,2,0:T(8,128)S(1)} %pad_maximum_fusion), channel_id=1, source_target_pairs={{0,1},{1,0},{2,3},{3,2},{4,5},{5,4},{6,7},{7,6},{8,9},{9,8},{10,11... | collective-permute-start | bytes 3145736 | tf_op jit(solution)/shard_map/ppermute | solution.py:16
  106.9 3.7 %collective-permute-start.7 = (f32[7,256,1]{1,2,0:T(1,128)S(1)}, f32[7,256,1]{1,2,0:T(1,128)S(1)}, u32[]{:S(2)}, u32[]{:S(2)}) collective-permute-start(f32[7,256,1]{1,2,0:T(1,128)S(1)} %broadcast_select_fusion.4), channel_id=1, source_target_pairs={{0,2},{2,0},{1,3},{3,1},{4,6},{6,4},{5,7},{7,5},{8,10},{10,8},{9,1... | collective-permute-start | bytes 21512 | tf_op jit(solution)/shard_map/ppermute | solution.py:26

commit v7 on v6

--- a/solution.py
+++ b/solution.py
@@ -16,25 +16,6 @@
     return lax.ppermute(value, axis, pairs)
 
 
-def with_halo(block, axis, dim):
-    count = lax.axis_size(axis)
-    first = lax.slice_in_dim(block, 0, 1, axis=dim)
-    last = lax.slice_in_dim(block, block.shape[dim] - 1, None, axis=dim)
-    index = lax.axis_index(axis)
-    if count == 2:
-        sent = jnp.where(index == 0, last, first)
-        got = lax.ppermute(sent, axis, [(0, 1), (1, 0)])
-        zero = jnp.zeros_like(got)
-        low = jnp.where(index == 0, zero, got)
-        high = jnp.where(index == 0, got, zero)
-    else:
-        forward = [(i, i + 1) for i in range(count - 1)]
-        backward = [(target, source) for source, target in forward]
-        low = lax.ppermute(last, axis, forward)
-        high = lax.ppermute(first, axis, backward)
-    return jnp.concatenate([low, block, high], axis=dim)
-
-
 def lag_stats(real, imag):
     zero_lag = jnp.mean(real * real + imag * imag, axis=-1)
     lag_re = jnp.sum(real[..., :-1] * real[..., 1:] + imag[..., :-1] * imag[..., 1:], axis=-1) / (
@@ -56,15 +37,45 @@
 
 def beam_stats(summed, gates):
     count = summed.shape[1]
-    real = summed[0].reshape(count, gates, PULSES)
-    imag = summed[1].reshape(count, gates, PULSES)
-    zero_lag, lag_re, lag_im = lag_stats(real, imag)
-    series = jnp.stack([real, imag])
+    series = summed.reshape(2, count, gates, PULSES)
     pol_index = lax.axis_index("pol")
     other = swapped(series, "pol", 0)
-    first = jnp.where(pol_index == 0, series, other)
-    second = jnp.where(pol_index == 0, other, series)
-    pair = jnp.stack(pair_stats(first, second))
+    n_gate = lax.axis_size("gate")
+    n_pol = lax.axis_size("pol")
+    gate_index = lax.axis_index("gate")
+    first = series[:, :, :1]
+    last = series[:, :, gates - 1 :]
+    both = ("gate", "pol")
+
+    def across(g, p):
+        return g * n_pol + (n_pol - 1 - p)
+
+    if n_gate == 2:
+        sent = jnp.where(gate_index == 0, last, first)
+        got_own = lax.ppermute(sent, "gate", [(0, 1), (1, 0)])
+        got_other = lax.ppermute(sent, both, [(g * n_pol + p, across(1 - g, p)) for g in range(2) for p in range(n_pol)])
+        zero = jnp.zeros_like(got_own)
+        low_own = jnp.where(gate_index == 0, zero, got_own)
+        high_own = jnp.where(gate_index == 0, got_own, zero)
+        low_other = jnp.where(gate_index == 0, zero, got_other)
+        high_other = jnp.where(gate_index == 0, got_other, zero)
+    else:
+        forward = [(i, i + 1) for i in range(n_gate - 1)]
+        backward = [(i + 1, i) for i in range(n_gate - 1)]
+        low_own = lax.ppermute(last, "gate", forward)
+        high_own = lax.ppermute(first, "gate", backward)
+        low_other = lax.ppermute(
+            last, both, [(g * n_pol + p, across(g + 1, p)) for g in range(n_gate - 1) for p in range(n_pol)]
+        )
+        high_other = lax.ppermute(
+            first, both, [((g + 1) * n_pol + p, across(g, p)) for g in range(n_gate - 1) for p in range(n_pol)]
+        )
+    own = jnp.concatenate([low_own, series, high_own], axis=2)
+    partner = jnp.concatenate([low_other, other, high_other], axis=2)
+    zero_lag, lag_re, lag_im = lag_stats(own[0], own[1])
+    first_pol = jnp.where(pol_index == 0, own, partner)
+    second_pol = jnp.where(pol_index == 0, partner, own)
+    pair = jnp.stack(pair_stats(first_pol, second_pol))
     return jnp.concatenate([jnp.stack([zero_lag, lag_re, lag_im]), pair], axis=0)
 
 
@@ -225,7 +236,7 @@
         part = partials(signal, weights)
         summed = lax.psum_scatter(part, "elem", scatter_dimension=1, tiled=True)
     stats = beam_stats(summed, gates)
-    padded = with_halo(stats, "gate", 2)
+    padded = stats
     smoothed = (padded[..., :-2] + 2.0 * padded[..., 1:-1] + padded[..., 2:]) * 0.25
     power = smoothed[0]
     magnitude = jnp.sqrt(smoothed[1] * smoothed[1] + smoothed[2] * smoothed[2])

time: 112 us -> 115 us (1.027)
    ppermute x1 -> x2, waiting for transfers between devices: 2.14 us -> 6.35 us  [the longest x1 4.53 us: beam_stats(): got_own = lax.ppermute(sent, 'gate', [(0, 1), (1, 0)])]
    ppermute x1, waiting for transfers between devices: 2.26 us -> 0.01 us  [swapped(): return lax.ppermute(value, axis, pairs)]
  transfers between devices with their start and end apart: 8 -> 9, of which waited for: 6 -> 6; matrix products, arithmetic and copies ran while one was open for 0% -> 0% of each run, Pallas kernels for 22% -> 22%
where the time goes in v7:
time: 115 us
  waiting for transfers between devices  43.5 us (38%)
  Pallas kernels  33.5 us (29%)
  starting transfers between devices  25.5 us (22%)
  other arithmetic  10.4 us (9%)
    ppermute x3, waiting for transfers between devices, line_scatter(): lax.ppermute(to_right, 'elem', [(c, c + 1) for c in senders_right])  34 us
    pallas_call x4, Pallas kernels, block_partial(): pl.pallas_call(block_kernel, out_shape=jax.ShapeDtypeStruct((2, samples,...  33.5 us
    ppermute x3, starting transfers between devices, line_scatter(): lax.ppermute(to_right, 'elem', [(c, c + 1) for c in senders_right])  18.9 us
    add x2, other arithmetic, line_scatter(): to_right = to_right + got_right  5.97 us
    ppermute x3, starting transfers between devices, line_scatter(): got_left = lax.ppermute(to_left, 'elem', [(c, c - 1) for c in senders_left])  4.64 us
    ppermute x1, waiting for transfers between devices, beam_stats(): got_own = lax.ppermute(sent, 'gate', [(0, 1), (1, 0)])  4.53 us
    ppermute x3, waiting for transfers between devices, line_scatter(): got_left = lax.ppermute(to_left, 'elem', [(c, c - 1) for c in senders_left])  3.15 us
  transfers between devices with their start and end apart: 9, of which 6 were waited for; matrix products, arithmetic and copies ran while one was open for 0% of the time, Pallas kernels for 22%

profile of v7, /device:TPU:0, one launch (start us, length us, event | category | flops | bytes accessed | tf_op | source)
XLA Modules:
  0.0 115.0 jit_solution(3903171345372685067)
XLA Ops:
  0.6 8.4 %shard_map.44 = f32[2,512,256]{2,1,0:T(8,128)S(1)} custom-call(s32[1]{0:T(128)} %bitcast.8.index_ref, bf16[2,1024,4096]{2,1,0:T(8,128)(2,1)} %bitcast.65, bf16[2,4096,512]{2,1,0:T(8,128)(2,1)} %bitcast.69), custom_call_target="tpu_custom_call" | custom-call | flops 4294967296 | bytes 13631488 | tf_op jit(solution)/shard_map/pallas_call | solution.py:166
  9.0 5.0 %collective-permute-start = (f32[2,256,512]{1,2,0:T(8,128)S(1)}, f32[2,256,512]{1,2,0:T(8,128)S(1)}, u32[]{:S(2)}, u32[]{:S(2)}) collective-permute-start(f32[2,256,512]{1,2,0:T(8,128)S(1)} %bitcast.63), channel_id=1, source_target_pairs={{0,4},{1,5},{2,6},{3,7},{16,20},{17,21},{18,22},{19,23}} | collective-permute-start | bytes 3145736 | tf_op jit(solution)/shard_map/ppermute | solution.py:222
  14.1 1.7 %collective-permute-start.3 = (f32[2,256,512]{1,2,0:T(8,128)S(1)}, f32[2,256,512]{1,2,0:T(8,128)}, u32[]{:S(2)}, u32[]{:S(2)}) collective-permute-start(f32[2,256,512]{1,2,0:T(8,128)S(1)} %bitcast.64), channel_id=1, source_target_pairs={{12,8},{13,9},{14,10},{15,11},{28,24},{29,25},{30,26},{31,27}} | collective-permute-start | bytes 3145736 | tf_op jit(solution)/shard_map/ppermute | solution.py:223
  15.7 8.4 %shard_map.43 = f32[2,512,256]{2,1,0:T(8,128)S(1)} custom-call(s32[1]{0:T(128)} %bitcast.6.index_ref, bf16[2,1024,4096]{2,1,0:T(8,128)(2,1)} %bitcast.66, bf16[2,4096,512]{2,1,0:T(8,128)(2,1)} %bitcast.70), custom_call_target="tpu_custom_call" | custom-call | flops 4294967296 | bytes 13631488 | tf_op jit(solution)/shard_map/pallas_call | solution.py:166
  24.1 12.3 %collective-permute-done = f32[2,256,512]{1,2,0:T(8,128)S(1)} collective-permute-done((f32[2,256,512]{1,2,0:T(8,128)S(1)}, f32[2,256,512]{1,2,0:T(8,128)S(1)}, u32[]{:S(2)}, u32[]{:S(2)}) %collective-permute-start) | collective-permute-done | bytes 1048608 | tf_op jit(solution)/shard_map/ppermute | solution.py:222
  36.4 2.8 %fusion.2 = (f32[2,256,512]{1,2,0:T(8,128)}, f32[2,256,512]{1,2,0:T(8,128)}) fusion(f32[2,256,512]{1,2,0:T(8,128)S(1)} %collective-permute-done, f32[2,512,256]{2,1,0:T(8,128)S(1)} %shard_map.43, pred[]{:T(512)S(6)} %eq.37, f32[2,512,256]{2,1,0:T(8,128)S(1)} %shard_map.44, f32[2,256,512]{1,2,0:T(8,128)} %collective-permute-done.3, pred[]{:T(512)S(6)} %eq.40), kind=kLoop, calls=%fused_computation.8 | loop fusion | flops 1048576 | bytes 6291458 | tf_op jit(solution)/shard_map/add | solution.py:220
  39.2 5.4 %collective-permute-start.1 = (f32[2,256,512]{1,2,0:T(8,128)}, f32[2,256,512]{1,2,0:T(8,128)}, u32[]{:S(2)}, u32[]{:S(2)}) collective-permute-start(f32[2,256,512]{1,2,0:T(8,128)} %get-tuple-element.14), channel_id=1, source_target_pairs={{0,4},{4,8},{1,5},{5,9},{2,6},{6,10},{3,7},{7,11},{16,20},{20,24},... | collective-permute-start | bytes 3145736 | tf_op jit(solution)/shard_map/ppermute | solution.py:222
  44.6 1.7 %collective-permute-start.4 = (f32[2,256,512]{1,2,0:T(8,128)}, f32[2,256,512]{1,2,0:T(8,128)}, u32[]{:S(2)}, u32[]{:S(2)}) collective-permute-start(f32[2,256,512]{1,2,0:T(8,128)} %get-tuple-element.15), channel_id=1, source_target_pairs={{8,4},{12,8},{9,5},{13,9},{10,6},{14,10},{11,7},{15,11},{24,20},{2... | collective-permute-start | bytes 3145736 | tf_op jit(solution)/shard_map/ppermute | solution.py:223
  46.3 8.4 %shard_map.41 = f32[2,512,256]{2,1,0:T(8,128)S(1)} custom-call(s32[1]{0:T(128)} %bitcast.index_ref, bf16[2,1024,4096]{2,1,0:T(8,128)(2,1)} %bitcast.67, bf16[2,4096,512]{2,1,0:T(8,128)(2,1)} %bitcast.71), custom_call_target="tpu_custom_call" | custom-call | flops 4294967296 | bytes 13631488 | tf_op jit(solution)/shard_map/pallas_call | solution.py:166
  54.6 8.4 %shard_map.42 = f32[2,512,256]{2,1,0:T(8,128)S(1)} custom-call(s32[1]{0:T(128)} %bitcast.4.index_ref, bf16[2,1024,4096]{2,1,0:T(8,128)(2,1)} %bitcast.68, bf16[2,4096,512]{2,1,0:T(8,128)(2,1)} %bitcast.72), custom_call_target="tpu_custom_call" | custom-call | flops 4294967296 | bytes 13631488 | tf_op jit(solution)/shard_map/pallas_call | solution.py:166
  63.0 2.4 %collective-permute-done.1 = f32[2,256,512]{1,2,0:T(8,128)} collective-permute-done((f32[2,256,512]{1,2,0:T(8,128)}, f32[2,256,512]{1,2,0:T(8,128)}, u32[]{:S(2)}, u32[]{:S(2)}) %collective-permute-start.1) | collective-permute-done | bytes 1048608 | tf_op jit(solution)/shard_map/ppermute | solution.py:222
  65.4 3.2 %fusion.1 = (f32[2,256,512]{1,2,0:T(8,128)}, f32[2,256,512]{1,2,0:T(8,128)}) fusion(f32[2,256,512]{1,2,0:T(8,128)} %collective-permute-done.1, f32[2,512,256]{2,1,0:T(8,128)S(1)} %shard_map.43, f32[2,512,256]{2,1,0:T(8,128)S(1)} %shard_map.42, f32[2,512,256]{2,1,0:T(8,128)S(1)} %shard_map.41, pred[]{:T(512)S(6)} %eq.36, pred[]{:T(512)S(6)} %eq.35, ...), kind=kLoop, calls=%fused_computation.7 | loop fusion | flops 1572864 | bytes 7340036 | tf_op jit(solution)/shard_map/add | solution.py:220
  68.6 8.5 %collective-permute-start.2 = (f32[2,256,512]{1,2,0:T(8,128)}, f32[2,256,512]{1,2,0:T(8,128)S(1)}, u32[]{:S(2)}, u32[]{:S(2)}) collective-permute-start(f32[2,256,512]{1,2,0:T(8,128)} %get-tuple-element.10), channel_id=1, source_target_pairs={{0,4},{4,8},{8,12},{1,5},{5,9},{9,13},{2,6},{6,10},{10,14},{3,7},{... | collective-permute-start | bytes 3145736 | tf_op jit(solution)/shard_map/ppermute | solution.py:222
  77.1 1.3 %collective-permute-start.5 = (f32[2,256,512]{1,2,0:T(8,128)}, f32[2,256,512]{1,2,0:T(8,128)}, u32[]{:S(2)}, u32[]{:S(2)}) collective-permute-start(f32[2,256,512]{1,2,0:T(8,128)} %get-tuple-element.11), channel_id=1, source_target_pairs={{4,0},{8,4},{12,8},{5,1},{9,5},{13,9},{6,2},{10,6},{14,10},{7,3},{... | collective-permute-start | bytes 3145736 | tf_op jit(solution)/shard_map/ppermute | solution.py:223
  78.4 19.3 %collective-permute-done.2 = f32[2,256,512]{1,2,0:T(8,128)S(1)} collective-permute-done((f32[2,256,512]{1,2,0:T(8,128)}, f32[2,256,512]{1,2,0:T(8,128)S(1)}, u32[]{:S(2)}, u32[]{:S(2)}) %collective-permute-start.2) | collective-permute-done | bytes 1048608 | tf_op jit(solution)/shard_map/ppermute | solution.py:222
  97.8 1.0 copy-done
  98.8 3.1 %collective-permute-done.5 = f32[2,256,512]{1,2,0:T(8,128)} collective-permute-done((f32[2,256,512]{1,2,0:T(8,128)}, f32[2,256,512]{1,2,0:T(8,128)}, u32[]{:S(2)}, u32[]{:S(2)}) %collective-permute-start.5) | collective-permute-done | bytes 1048608 | tf_op jit(solution)/shard_map/ppermute | solution.py:223
  101.9 1.8 %fusion.7 = f32[2,256,512]{1,2,0:T(8,128)S(1)} fusion(f32[2,256,512]{1,2,0:T(8,128)} %collective-permute-done.5, f32[2,256,512]{1,2,0:T(8,128)} %copy-done, f32[2,512,256]{2,1,0:T(8,128)S(1)} %shard_map.42, f32[2,512,256]{2,1,0:T(8,128)S(1)} %shard_map.41, pred[]{:T(512)S(6)} %eq.34), kind=kLoop, calls=%fused_computation.14 | loop fusion | flops 786432 | bytes 5242881 | tf_op jit(solution)/shard_map/add | solution.py:225
  103.9 1.6 %collective-permute-start.6 = (f32[2,256,1,64]{1,3,2,0:T(8,128)S(1)}, f32[2,256,1,64]{1,3,2,0:T(8,128)S(1)}, u32[]{:S(2)}, u32[]{:S(2)}) collective-permute-start(f32[2,256,1,64]{1,3,2,0:T(8,128)S(1)} %slice_select_fusion), channel_id=1, source_target_pairs={{0,2},{2,0},{1,3},{3,1},{4,6},{6,4},{5,7},{7,5},{8,10},{10,8},{9,1... | collective-permute-start | bytes 393224 | tf_op jit(solution)/shard_map/ppermute | solution.py:55
  105.8 4.5 %collective-permute-done.6 = f32[2,256,1,64]{1,3,2,0:T(8,128)S(1)} collective-permute-done((f32[2,256,1,64]{1,3,2,0:T(8,128)S(1)}, f32[2,256,1,64]{1,3,2,0:T(8,128)S(1)}, u32[]{:S(2)}, u32[]{:S(2)}) %collective-permute-start.6) | collective-permute-done | bytes 131104 | tf_op jit(solution)/shard_map/ppermute | solution.py:55
  110.3 1.8 %collective-permute-done.7 = f32[2,256,1,64]{1,3,2,0:T(8,128)S(1)} collective-permute-done((f32[2,256,1,64]{1,3,2,0:T(8,128)S(1)}, f32[2,256,1,64]{1,3,2,0:T(8,128)S(1)}, u32[]{:S(2)}, u32[]{:S(2)}) %collective-permute-start.7) | collective-permute-done | bytes 131104 | tf_op jit(solution)/shard_map/ppermute | solution.py:56
  112.2 0.5 fusion.9
  113.7 0.6 slice_divide_fusion
  114.3 0.6 maximum_bitcast_fusion
  (22 shorter events, 1.4 us)
Async XLA Ops:
  9.0 27.4 %collective-permute-start = (f32[2,256,512]{1,2,0:T(8,128)S(1)}, f32[2,256,512]{1,2,0:T(8,128)S(1)}, u32[]{:S(2)}, u32[]{:S(2)}) collective-permute-start(f32[2,256,512]{1,2,0:T(8,128)S(1)} %bitcast.63), channel_id=1, source_target_pairs={{0,4},{1,5},{2,6},{3,7},{16,20},{17,21},{18,22},{19,23}} | collective-permute-start | bytes 3145736 | tf_op jit(solution)/shard_map/ppermute | solution.py:222
  14.1 22.3 %collective-permute-start.3 = (f32[2,256,512]{1,2,0:T(8,128)S(1)}, f32[2,256,512]{1,2,0:T(8,128)}, u32[]{:S(2)}, u32[]{:S(2)}) collective-permute-start(f32[2,256,512]{1,2,0:T(8,128)S(1)} %bitcast.64), channel_id=1, source_target_pairs={{12,8},{13,9},{14,10},{15,11},{28,24},{29,25},{30,26},{31,27}} | collective-permute-start | bytes 3145736 | tf_op jit(solution)/shard_map/ppermute | solution.py:223
  39.2 26.2 %collective-permute-start.1 = (f32[2,256,512]{1,2,0:T(8,128)}, f32[2,256,512]{1,2,0:T(8,128)}, u32[]{:S(2)}, u32[]{:S(2)}) collective-permute-start(f32[2,256,512]{1,2,0:T(8,128)} %get-tuple-element.14), channel_id=1, source_target_pairs={{0,4},{4,8},{1,5},{5,9},{2,6},{6,10},{3,7},{7,11},{16,20},{20,24},... | collective-permute-start | bytes 3145736 | tf_op jit(solution)/shard_map/ppermute | solution.py:222
  44.6 20.9 %collective-permute-start.4 = (f32[2,256,512]{1,2,0:T(8,128)}, f32[2,256,512]{1,2,0:T(8,128)}, u32[]{:S(2)}, u32[]{:S(2)}) collective-permute-start(f32[2,256,512]{1,2,0:T(8,128)} %get-tuple-element.15), channel_id=1, source_target_pairs={{8,4},{12,8},{9,5},{13,9},{10,6},{14,10},{11,7},{15,11},{24,20},{2... | collective-permute-start | bytes 3145736 | tf_op jit(solution)/shard_map/ppermute | solution.py:223
  68.6 29.1 %collective-permute-start.2 = (f32[2,256,512]{1,2,0:T(8,128)}, f32[2,256,512]{1,2,0:T(8,128)S(1)}, u32[]{:S(2)}, u32[]{:S(2)}) collective-permute-start(f32[2,256,512]{1,2,0:T(8,128)} %get-tuple-element.10), channel_id=1, source_target_pairs={{0,4},{4,8},{8,12},{1,5},{5,9},{9,13},{2,6},{6,10},{10,14},{3,7},{... | collective-permute-start | bytes 3145736 | tf_op jit(solution)/shard_map/ppermute | solution.py:222
  77.1 24.8 %collective-permute-start.5 = (f32[2,256,512]{1,2,0:T(8,128)}, f32[2,256,512]{1,2,0:T(8,128)}, u32[]{:S(2)}, u32[]{:S(2)}) collective-permute-start(f32[2,256,512]{1,2,0:T(8,128)} %get-tuple-element.11), channel_id=1, source_target_pairs={{4,0},{8,4},{12,8},{5,1},{9,5},{13,9},{6,2},{10,6},{14,10},{7,3},{... | collective-permute-start | bytes 3145736 | tf_op jit(solution)/shard_map/ppermute | solution.py:223
  97.8 1.0 copy-start
  103.8 8.4 %collective-permute-start.8 = (f32[2,256,8,64]{1,3,2,0:T(8,128)S(1)}, f32[2,256,8,64]{1,3,2,0:T(8,128)S(1)}, u32[]{:S(2)}, u32[]{:S(2)}) collective-permute-start(f32[2,256,8,64]{1,3,2,0:T(8,128)S(1)} %bitcast.73), channel_id=1, source_target_pairs={{0,1},{1,0},{2,3},{3,2},{4,5},{5,4},{6,7},{7,6},{8,9},{9,8},{10,11... | collective-permute-start | bytes 3145736 | tf_op jit(solution)/shard_map/ppermute | solution.py:16
  103.9 6.4 %collective-permute-start.6 = (f32[2,256,1,64]{1,3,2,0:T(8,128)S(1)}, f32[2,256,1,64]{1,3,2,0:T(8,128)S(1)}, u32[]{:S(2)}, u32[]{:S(2)}) collective-permute-start(f32[2,256,1,64]{1,3,2,0:T(8,128)S(1)} %slice_select_fusion), channel_id=1, source_target_pairs={{0,2},{2,0},{1,3},{3,1},{4,6},{6,4},{5,7},{7,5},{8,10},{10,8},{9,1... | collective-permute-start | bytes 393224 | tf_op jit(solution)/shard_map/ppermute | solution.py:55
  105.4 6.7 %collective-permute-start.7 = (f32[2,256,1,64]{1,3,2,0:T(8,128)S(1)}, f32[2,256,1,64]{1,3,2,0:T(8,128)S(1)}, u32[]{:S(2)}, u32[]{:S(2)}) collective-permute-start(f32[2,256,1,64]{1,3,2,0:T(8,128)S(1)} %slice_select_fusion), channel_id=1, source_target_pairs={{0,3},{1,2},{2,1},{3,0},{4,7},{5,6},{6,5},{7,4},{8,11},{9,10},{10,... | collective-permute-start | bytes 393224 | tf_op jit(solution)/shard_map/ppermute | solution.py:56

commit v8 on v6

--- a/solution.py
+++ b/solution.py
@@ -176,41 +176,56 @@
     )(index.reshape(1), w, x)
 
 
+def send_plan(n_elem):
+    plan = []
+    serves = []
+    for step in range(1, n_elem):
+        right = {c: c + n_elem - step for c in range(step)}
+        left = {c: c - n_elem + step for c in range(n_elem - step, n_elem)}
+        if set(right) & set(left):
+            plan += [right, left]
+            serves += [(step, "right"), (step, "left")]
+        else:
+            plan.append({**right, **left})
+            serves.append((step, "both"))
+    own_call = {}
+    for c in range(n_elem):
+        free = [k for k, row in enumerate(plan) if c not in row]
+        if free:
+            plan[free[0]][c] = c
+            own_call[c] = free[0]
+        else:
+            plan.append({c: c})
+            serves.append((None, "own"))
+            own_call[c] = len(plan) - 1
+    table = [[row.get(c, c) for c in range(n_elem)] for row in plan]
+    return table, serves, own_call
+
+
 def line_scatter(signal, weights, n_elem):
     me = lax.axis_index("elem")
-    near = me < n_elem // 2
     local = weights.shape[2] // n_elem
-
-    def order(c, q):
-        return n_elem - 1 - q if c < n_elem // 2 else q
-
+    table, serves, own_call = send_plan(n_elem)
     made = []
-    for k in range(n_elem):
-        index = jnp.where(near, n_elem - 1 - k, k).astype(jnp.int32)
+    for row in table:
+        index = jnp.asarray(row, jnp.int32)[me]
         made.append(jnp.swapaxes(block_partial(signal, weights, index, local), 1, 2))
-
-    def pick(q, needed):
-        at = jnp.where(near, n_elem - 1 - q, q)
-        picked = made[needed[0]]
-        for k in needed[1:]:
-            picked = jnp.where(at == k, made[k], picked)
-        return picked
-
     got_right = None
     got_left = None
     for step in range(1, n_elem):
-        senders_right = range(step)
-        senders_left = range(n_elem - step, n_elem)
-        need_right = sorted({order(c, c + n_elem - step) for c in senders_right})
-        need_left = sorted({order(c, c - n_elem + step) for c in senders_left})
-        to_right = pick(me + n_elem - step, need_right)
-        to_left = pick(me - n_elem + step, need_left)
+        calls = {way: k for k, (s, way) in enumerate(serves) if s == step}
+        to_right = made[calls.get("right", calls.get("both"))]
+        to_left = made[calls.get("left", calls.get("both"))]
         if got_right is not None:
             to_right = to_right + got_right
             to_left = to_left + got_left
-        got_right = lax.ppermute(to_right, "elem", [(c, c + 1) for c in senders_right])
-        got_left = lax.ppermute(to_left, "elem", [(c, c - 1) for c in senders_left])
-    own = pick(me, sorted({order(c, c) for c in range(n_elem)}))
+        got_right = lax.ppermute(to_right, "elem", [(c, c + 1) for c in range(step)])
+        got_left = lax.ppermute(to_left, "elem", [(c, c - 1) for c in range(n_elem - step, n_elem)])
+    own_at = jnp.asarray([own_call[c] for c in range(n_elem)], jnp.int32)[me]
+    used = sorted(set(own_call.values()))
+    own = made[used[0]]
+    for k in used[1:]:
+        own = jnp.where(own_at == k, made[k], own)
     return own + got_right + got_left
 
 
@@ -219,7 +234,7 @@
     samples = signal.shape[3]
     gates = samples // PULSES
     beams = weights.shape[2]
-    if 2 <= n_elem <= 8 and n_elem % 2 == 0:
+    if n_elem in (2, 4):
         summed = line_scatter(signal, weights, n_elem)
     else:
         part = partials(signal, weights)

time: 112 us -> 104 us (0.929)
  starting transfers between devices: 25.2 us -> 18.3 us
  other arithmetic: 9.71 us -> 3.07 us
  local copies, waits for them, and re-layouts: 0.07 us -> 3.69 us
  Pallas kernels: 33.5 us -> 36.1 us
  waiting for transfers between devices: 42.6 us -> 40.7 us
  between operations: 0.86 us -> 2.24 us
    ppermute x6, starting transfers between devices: 23.5 us -> 16.7 us  [the longest x3 13.9 us: line_scatter(): lax.ppermute(to_right, 'elem', [(c, c + 1) for c in range(step)])]
    add x2, other arithmetic: 5.97 us -> 0.34 us  [line_scatter(): to_right = to_right + got_right]
    dynamic_slice x0 -> x5, local copies, waits for them, and re-layouts: none -> 3.59 us  [the longest x4 3.01 us: line_scatter(): index = jnp.asarray(row, jnp.int32)[me]]
    pallas_call x4, Pallas kernels: 33.5 us -> 36.1 us  [block_partial(): pl.pallas_call(block_kernel, out_shape=jax.ShapeDtypeStruct((2, samples,...]
    ppermute x6, waiting for transfers between devices: 38.2 us -> 36.3 us  [the longest x3 30.7 us: line_scatter(): lax.ppermute(to_right, 'elem', [(c, c + 1) for c in range(step)])]
    add x1, other arithmetic: 1.49 us -> 0.34 us  [line_scatter(): return own + got_right + got_left]
  transfers between devices with their start and end apart: 8 -> 8, of which waited for: 6 -> 6; matrix products, arithmetic and copies ran while one was open for 0% -> 3% of each run, Pallas kernels for 22% -> 26%
where the time goes in v8:
time: 104 us
  waiting for transfers between devices  40.7 us (39%)
  Pallas kernels  36.1 us (35%)
  starting transfers between devices  18.3 us (18%)
  local copies, waits for them, and re-layouts  3.69 us (4%)
  other arithmetic  3.07 us (3%)
  between operations  2.24 us (2%)
    pallas_call x4, Pallas kernels, block_partial(): pl.pallas_call(block_kernel, out_shape=jax.ShapeDtypeStruct((2, samples,...  36.1 us
    ppermute x3, waiting for transfers between devices, line_scatter(): lax.ppermute(to_right, 'elem', [(c, c + 1) for c in range(step)])  30.7 us
    ppermute x3, starting transfers between devices, line_scatter(): lax.ppermute(to_right, 'elem', [(c, c + 1) for c in range(step)])  13.9 us
    ppermute x3, waiting for transfers between devices, line_scatter(): lax.ppermute(to_left, 'elem', [(c, c - 1) for c in range(n_elem - step, n...  5.59 us
    dynamic_slice x4, local copies, waits for them, and re-layouts, line_scatter(): index = jnp.asarray(row, jnp.int32)[me]  3.01 us
    ppermute x3, starting transfers between devices, line_scatter(): lax.ppermute(to_left, 'elem', [(c, c - 1) for c in range(n_elem - step, n...  2.74 us
    ppermute x1, waiting for transfers between devices, swapped(): return lax.ppermute(value, axis, pairs)  2.26 us
    ppermute x1, waiting for transfers between devices, with_halo(): got = lax.ppermute(sent, axis, [(0, 1), (1, 0)])  2.15 us
  transfers between devices with their start and end apart: 8, of which 6 were waited for; matrix products, arithmetic and copies ran while one was open for 3% of the time, Pallas kernels for 26%

profile of v8, /device:TPU:0, one launch (start us, length us, event | category | flops | bytes accessed | tf_op | source)
XLA Modules:
  0.0 104.1 jit_solution(13856506003794600976)
XLA Ops:
  0.6 1.2 %dynamic_slice.18.index_ref = s32[1]{0:T(128)} dynamic-slice(s32[4]{0:T(128)} %constant.57.clone, s32[]{:T(128)S(6)} %select_n.59), dynamic_slice_sizes={1} | dynamic-slice | bytes 12 | tf_op jit(solution)/shard_map/dynamic_slice | solution.py:211
  1.9 9.0 %shard_map.88 = f32[2,512,256]{2,1,0:T(8,128)S(1)} custom-call(s32[1]{0:T(128)} %dynamic_slice.18.index_ref, bf16[2,1024,4096]{2,1,0:T(8,128)(2,1)} %bitcast.43, bf16[2,4096,512]{2,1,0:T(8,128)(2,1)} %bitcast.47), custom_call_target="tpu_custom_call" | custom-call | flops 4294967296 | bytes 13631488 | tf_op jit(solution)/shard_map/pallas_call | solution.py:155
  11.0 5.0 %collective-permute-start = (f32[2,256,512]{1,2,0:T(8,128)S(1)}, f32[2,256,512]{1,2,0:T(8,128)S(1)}, u32[]{:S(2)}, u32[]{:S(2)}) collective-permute-start(f32[2,256,512]{1,2,0:T(8,128)S(1)} %bitcast.41), channel_id=1, source_target_pairs={{0,4},{1,5},{2,6},{3,7},{16,20},{17,21},{18,22},{19,23}} | collective-permute-start | bytes 3145736 | tf_op jit(solution)/shard_map/ppermute | solution.py:222
  16.0 0.7 collective-permute-start.3
  16.7 0.6 dynamic_slice.19.index_ref
  17.3 9.0 %shard_map.89 = f32[2,512,256]{2,1,0:T(8,128)S(1)} custom-call(s32[1]{0:T(128)} %dynamic_slice.19.index_ref, bf16[2,1024,4096]{2,1,0:T(8,128)(2,1)} %bitcast.44, bf16[2,4096,512]{2,1,0:T(8,128)(2,1)} %bitcast.48), custom_call_target="tpu_custom_call" | custom-call | flops 4294967296 | bytes 13631488 | tf_op jit(solution)/shard_map/pallas_call | solution.py:155
  26.4 12.0 %collective-permute-done = f32[2,256,512]{1,2,0:T(8,128)S(1)} collective-permute-done((f32[2,256,512]{1,2,0:T(8,128)S(1)}, f32[2,256,512]{1,2,0:T(8,128)S(1)}, u32[]{:S(2)}, u32[]{:S(2)}) %collective-permute-start) | collective-permute-done | bytes 1048608 | tf_op jit(solution)/shard_map/ppermute | solution.py:222
  38.5 4.5 %collective-permute-start.1 = (f32[2,256,512]{1,2,0:T(8,128)S(1)}, f32[2,256,512]{1,2,0:T(8,128)S(1)}, u32[]{:S(2)}, u32[]{:S(2)}) collective-permute-start(f32[2,256,512]{1,2,0:T(8,128)S(1)} %get-tuple-element.14), channel_id=1, source_target_pairs={{0,4},{4,8},{1,5},{5,9},{2,6},{6,10},{3,7},{7,11},{16,20},{20,24},... | collective-permute-start | bytes 3145736 | tf_op jit(solution)/shard_map/ppermute | solution.py:222
  43.0 0.6 dynamic_slice.17.index_ref
  43.6 0.6 dynamic_slice.16.index_ref
  44.2 0.7 collective-permute-start.4
  44.9 9.0 %shard_map.87 = f32[2,512,256]{2,1,0:T(8,128)S(1)} custom-call(s32[1]{0:T(128)} %dynamic_slice.17.index_ref, bf16[2,1024,4096]{2,1,0:T(8,128)(2,1)} %bitcast.45, bf16[2,4096,512]{2,1,0:T(8,128)(2,1)} %bitcast.49), custom_call_target="tpu_custom_call" | custom-call | flops 4294967296 | bytes 13631488 | tf_op jit(solution)/shard_map/pallas_call | solution.py:155
  54.0 9.0 %shard_map.86 = f32[2,512,256]{2,1,0:T(8,128)S(1)} custom-call(s32[1]{0:T(128)} %dynamic_slice.16.index_ref, bf16[2,1024,4096]{2,1,0:T(8,128)(2,1)} %bitcast.46, bf16[2,4096,512]{2,1,0:T(8,128)(2,1)} %bitcast.50), custom_call_target="tpu_custom_call" | custom-call | flops 4294967296 | bytes 13631488 | tf_op jit(solution)/shard_map/pallas_call | solution.py:155
  63.0 1.5 %collective-permute-done.1 = f32[2,256,512]{1,2,0:T(8,128)S(1)} collective-permute-done((f32[2,256,512]{1,2,0:T(8,128)S(1)}, f32[2,256,512]{1,2,0:T(8,128)S(1)}, u32[]{:S(2)}, u32[]{:S(2)}) %collective-permute-start.1) | collective-permute-done | bytes 1048608 | tf_op jit(solution)/shard_map/ppermute | solution.py:222
  64.6 4.5 %collective-permute-start.2 = (f32[2,256,512]{1,2,0:T(8,128)S(1)}, f32[2,256,512]{1,2,0:T(8,128)S(1)}, u32[]{:S(2)}, u32[]{:S(2)}) collective-permute-start(f32[2,256,512]{1,2,0:T(8,128)S(1)} %bitcast_add_fusion.2), channel_id=1, source_target_pairs={{0,4},{4,8},{8,12},{1,5},{5,9},{9,13},{2,6},{6,10},{10,14},{3,7},{... | collective-permute-start | bytes 3145736 | tf_op jit(solution)/shard_map/ppermute | solution.py:222
  69.2 1.3 %collective-permute-start.5 = (f32[2,256,512]{1,2,0:T(8,128)S(1)}, f32[2,256,512]{1,2,0:T(8,128)S(1)}, u32[]{:S(2)}, u32[]{:S(2)}) collective-permute-start(f32[2,256,512]{1,2,0:T(8,128)S(1)} %bitcast_add_fusion.3), channel_id=1, source_target_pairs={{4,0},{8,4},{12,8},{5,1},{9,5},{13,9},{6,2},{10,6},{14,10},{7,3},{... | collective-permute-start | bytes 3145736 | tf_op jit(solution)/shard_map/ppermute | solution.py:223
  70.5 0.6 dynamic_slice.15
  72.4 17.3 %collective-permute-done.2 = f32[2,256,512]{1,2,0:T(8,128)S(1)} collective-permute-done((f32[2,256,512]{1,2,0:T(8,128)S(1)}, f32[2,256,512]{1,2,0:T(8,128)S(1)}, u32[]{:S(2)}, u32[]{:S(2)}) %collective-permute-start.2) | collective-permute-done | bytes 1048608 | tf_op jit(solution)/shard_map/ppermute | solution.py:222
  89.7 5.6 %collective-permute-done.5 = f32[2,256,512]{1,2,0:T(8,128)S(1)} collective-permute-done((f32[2,256,512]{1,2,0:T(8,128)S(1)}, f32[2,256,512]{1,2,0:T(8,128)S(1)}, u32[]{:S(2)}, u32[]{:S(2)}) %collective-permute-start.5) | collective-permute-done | bytes 1048608 | tf_op jit(solution)/shard_map/ppermute | solution.py:223
  96.3 2.3 %collective-permute-done.6 = f32[2,256,8,64]{1,3,2,0:T(8,128)S(1)} collective-permute-done((f32[2,256,8,64]{1,3,2,0:T(8,128)S(1)}, f32[2,256,8,64]{1,3,2,0:T(8,128)S(1)}, u32[]{:S(2)}, u32[]{:S(2)}) %collective-permute-start.6) | collective-permute-done | bytes 1048608 | tf_op jit(solution)/shard_map/ppermute | solution.py:16
  99.1 1.6 %collective-permute-start.7 = (f32[7,256,1]{1,2,0:T(1,128)S(1)}, f32[7,256,1]{1,2,0:T(1,128)S(1)}, u32[]{:S(2)}, u32[]{:S(2)}) collective-permute-start(f32[7,256,1]{1,2,0:T(1,128)S(1)} %broadcast_select_fusion.4), channel_id=1, source_target_pairs={{0,2},{2,0},{1,3},{3,1},{4,6},{6,4},{5,7},{7,5},{8,10},{10,8},{9,1... | collective-permute-start | bytes 21512 | tf_op jit(solution)/shard_map/ppermute | solution.py:26
  100.6 2.1 %collective-permute-done.7 = f32[7,256,1]{1,2,0:T(1,128)S(1)} collective-permute-done((f32[7,256,1]{1,2,0:T(1,128)S(1)}, f32[7,256,1]{1,2,0:T(1,128)S(1)}, u32[]{:S(2)}, u32[]{:S(2)}) %collective-permute-start.7) | collective-permute-done | bytes 7200 | tf_op jit(solution)/shard_map/ppermute | solution.py:26
  102.9 0.6 slice_divide_fusion
  103.5 0.6 maximum_bitcast_fusion
  (32 shorter events, 2.0 us)
Async XLA Ops:
  0.6 16.1 %copy-start.3 = (s32[4]{0:T(128)S(1)}, s32[4]{0:T(128)}, u32[]{:S(2)}) copy-start(s32[4]{0:T(128)} %constant.58.clone) | copy-start | bytes 52
  10.9 32.1 %copy-start.2 = (s32[4]{0:T(128)S(1)}, s32[4]{0:T(128)}, u32[]{:S(2)}) copy-start(s32[4]{0:T(128)} %constant.59.clone) | copy-start | bytes 52
  10.9 32.6 %copy-start.1 = (s32[4]{0:T(128)S(1)}, s32[4]{0:T(128)}, u32[]{:S(2)}) copy-start(s32[4]{0:T(128)} %constant.60.clone) | copy-start | bytes 52
  11.0 27.4 %collective-permute-start = (f32[2,256,512]{1,2,0:T(8,128)S(1)}, f32[2,256,512]{1,2,0:T(8,128)S(1)}, u32[]{:S(2)}, u32[]{:S(2)}) collective-permute-start(f32[2,256,512]{1,2,0:T(8,128)S(1)} %bitcast.41), channel_id=1, source_target_pairs={{0,4},{1,5},{2,6},{3,7},{16,20},{17,21},{18,22},{19,23}} | collective-permute-start | bytes 3145736 | tf_op jit(solution)/shard_map/ppermute | solution.py:222
  16.0 22.3 %collective-permute-start.3 = (f32[2,256,512]{1,2,0:T(8,128)S(1)}, f32[2,256,512]{1,2,0:T(8,128)S(1)}, u32[]{:S(2)}, u32[]{:S(2)}) collective-permute-start(f32[2,256,512]{1,2,0:T(8,128)S(1)} %bitcast.42), channel_id=1, source_target_pairs={{12,8},{13,9},{14,10},{15,11},{28,24},{29,25},{30,26},{31,27}} | collective-permute-start | bytes 3145736 | tf_op jit(solution)/shard_map/ppermute | solution.py:223
  38.5 25.9 %collective-permute-start.1 = (f32[2,256,512]{1,2,0:T(8,128)S(1)}, f32[2,256,512]{1,2,0:T(8,128)S(1)}, u32[]{:S(2)}, u32[]{:S(2)}) collective-permute-start(f32[2,256,512]{1,2,0:T(8,128)S(1)} %get-tuple-element.14), channel_id=1, source_target_pairs={{0,4},{4,8},{1,5},{5,9},{2,6},{6,10},{3,7},{7,11},{16,20},{20,24},... | collective-permute-start | bytes 3145736 | tf_op jit(solution)/shard_map/ppermute | solution.py:222
  44.2 24.9 %collective-permute-start.4 = (f32[2,256,512]{1,2,0:T(8,128)S(1)}, f32[2,256,512]{1,2,0:T(8,128)S(1)}, u32[]{:S(2)}, u32[]{:S(2)}) collective-permute-start(f32[2,256,512]{1,2,0:T(8,128)S(1)} %get-tuple-element.15), channel_id=1, source_target_pairs={{8,4},{12,8},{9,5},{13,9},{10,6},{14,10},{11,7},{15,11},{24,20},{2... | collective-permute-start | bytes 3145736 | tf_op jit(solution)/shard_map/ppermute | solution.py:223
  53.9 16.6 %copy-start = (s32[4]{0:T(128)S(1)}, s32[4]{0:T(128)}, u32[]{:S(2)}) copy-start(s32[4]{0:T(128)} %constant.61.clone) | copy-start | bytes 52
  64.6 25.1 %collective-permute-start.2 = (f32[2,256,512]{1,2,0:T(8,128)S(1)}, f32[2,256,512]{1,2,0:T(8,128)S(1)}, u32[]{:S(2)}, u32[]{:S(2)}) collective-permute-start(f32[2,256,512]{1,2,0:T(8,128)S(1)} %bitcast_add_fusion.2), channel_id=1, source_target_pairs={{0,4},{4,8},{8,12},{1,5},{5,9},{9,13},{2,6},{6,10},{10,14},{3,7},{... | collective-permute-start | bytes 3145736 | tf_op jit(solution)/shard_map/ppermute | solution.py:222
  69.2 26.1 %collective-permute-start.5 = (f32[2,256,512]{1,2,0:T(8,128)S(1)}, f32[2,256,512]{1,2,0:T(8,128)S(1)}, u32[]{:S(2)}, u32[]{:S(2)}) collective-permute-start(f32[2,256,512]{1,2,0:T(8,128)S(1)} %bitcast_add_fusion.3), channel_id=1, source_target_pairs={{4,0},{8,4},{12,8},{5,1},{9,5},{13,9},{6,2},{10,6},{14,10},{7,3},{... | collective-permute-start | bytes 3145736 | tf_op jit(solution)/shard_map/ppermute | solution.py:223
  95.8 2.7 %collective-permute-start.6 = (f32[2,256,8,64]{1,3,2,0:T(8,128)S(1)}, f32[2,256,8,64]{1,3,2,0:T(8,128)S(1)}, u32[]{:S(2)}, u32[]{:S(2)}) collective-permute-start(f32[2,256,8,64]{1,3,2,0:T(8,128)S(1)} %pad_maximum_fusion), channel_id=1, source_target_pairs={{0,1},{1,0},{2,3},{3,2},{4,5},{5,4},{6,7},{7,6},{8,9},{9,8},{10,11... | collective-permute-start | bytes 3145736 | tf_op jit(solution)/shard_map/ppermute | solution.py:16
  99.1 3.7 %collective-permute-start.7 = (f32[7,256,1]{1,2,0:T(1,128)S(1)}, f32[7,256,1]{1,2,0:T(1,128)S(1)}, u32[]{:S(2)}, u32[]{:S(2)}) collective-permute-start(f32[7,256,1]{1,2,0:T(1,128)S(1)} %broadcast_select_fusion.4), channel_id=1, source_target_pairs={{0,2},{2,0},{1,3},{3,1},{4,6},{6,4},{5,7},{7,5},{8,10},{10,8},{9,1... | collective-permute-start | bytes 21512 | tf_op jit(solution)/shard_map/ppermute | solution.py:26

commit v9 on v8

--- a/solution.py
+++ b/solution.py
@@ -207,8 +207,14 @@
     local = weights.shape[2] // n_elem
     table, serves, own_call = send_plan(n_elem)
     made = []
+    def lookup(row):
+        value = jnp.int32(row[0])
+        for c in range(1, n_elem):
+            value = jnp.where(me == c, jnp.int32(row[c]), value)
+        return value
+
     for row in table:
-        index = jnp.asarray(row, jnp.int32)[me]
+        index = lookup(row)
         made.append(jnp.swapaxes(block_partial(signal, weights, index, local), 1, 2))
     got_right = None
     got_left = None
@@ -221,7 +227,7 @@
             to_left = to_left + got_left
         got_right = lax.ppermute(to_right, "elem", [(c, c + 1) for c in range(step)])
         got_left = lax.ppermute(to_left, "elem", [(c, c - 1) for c in range(n_elem - step, n_elem)])
-    own_at = jnp.asarray([own_call[c] for c in range(n_elem)], jnp.int32)[me]
+    own_at = lookup([own_call[c] for c in range(n_elem)])
     used = sorted(set(own_call.values()))
     own = made[used[0]]
     for k in used[1:]:

time: 104 us -> 109 us (1.048)
  other arithmetic: 3.07 us -> 9.22 us
  waiting for transfers between devices: 40.7 us -> 44.7 us
  local copies, waits for them, and re-layouts: 3.69 us -> 0.07 us
  Pallas kernels: 36.1 us -> 33.5 us
  starting transfers between devices: 18.3 us -> 20.1 us
  between operations: 2.24 us -> 0.9 us
    add x2, other arithmetic: 0.34 us -> 3.97 us  [line_scatter(): to_right = to_right + got_right]
    dynamic_slice x5 -> x0, local copies, waits for them, and re-layouts: 3.59 us -> none  [the longest x4 3.01 us: line_scatter(): index = jnp.asarray(row, jnp.int32)[me]]
    ppermute x3, waiting for transfers between devices: 30.7 us -> 34.1 us  [line_scatter(): lax.ppermute(to_right, 'elem', [(c, c + 1) for c in range(step)])]
    pallas_call x4, Pallas kernels: 36.1 us -> 33.5 us  [block_partial(): pl.pallas_call(block_kernel, out_shape=jax.ShapeDtypeStruct((2, samples,...]
    ppermute x3, starting transfers between devices: 13.9 us -> 15.8 us  [line_scatter(): lax.ppermute(to_right, 'elem', [(c, c + 1) for c in range(step)])]
    add x1, other arithmetic: 0.34 us -> 1.88 us  [line_scatter(): return own + got_right + got_left]
  transfers between devices with their start and end apart: 8 -> 8, of which waited for: 6 -> 6; matrix products, arithmetic and copies ran while one was open for 3% -> 4% of each run, Pallas kernels for 26% -> 23%
where the time goes in v9:
time: 109 us
  waiting for transfers between devices  44.7 us (41%)
  Pallas kernels  33.5 us (31%)
  starting transfers between devices  20.1 us (18%)
  other arithmetic  9.22 us (8%)
    ppermute x3, waiting for transfers between devices, line_scatter(): lax.ppermute(to_right, 'elem', [(c, c + 1) for c in range(step)])  34.1 us
    pallas_call x4, Pallas kernels, block_partial(): pl.pallas_call(block_kernel, out_shape=jax.ShapeDtypeStruct((2, samples,...  33.5 us
    ppermute x3, starting transfers between devices, line_scatter(): lax.ppermute(to_right, 'elem', [(c, c + 1) for c in range(step)])  15.8 us
    ppermute x3, waiting for transfers between devices, line_scatter(): lax.ppermute(to_left, 'elem', [(c, c - 1) for c in range(n_elem - step, n...  6.21 us
    add x2, other arithmetic, line_scatter(): to_right = to_right + got_right  3.97 us
    ppermute x3, starting transfers between devices, line_scatter(): lax.ppermute(to_left, 'elem', [(c, c - 1) for c in range(n_elem - step, n...  2.72 us
    ppermute x1, waiting for transfers between devices, swapped(): return lax.ppermute(value, axis, pairs)  2.26 us
  transfers between devices with their start and end apart: 8, of which 6 were waited for; matrix products, arithmetic and copies ran while one was open for 4% of the time, Pallas kernels for 23%

profile of v9, /device:TPU:0, one launch (start us, length us, event | category | flops | bytes accessed | tf_op | source)
XLA Modules:
  0.0 108.6 jit_solution(16536723037845181227)
XLA Ops:
  0.6 8.4 %shard_map.43 = f32[2,512,256]{2,1,0:T(8,128)S(1)} custom-call(s32[1]{0:T(128)} %bitcast.6.index_ref, bf16[2,1024,4096]{2,1,0:T(8,128)(2,1)} %bitcast.45, bf16[2,4096,512]{2,1,0:T(8,128)(2,1)} %bitcast.49), custom_call_target="tpu_custom_call" | custom-call | flops 4294967296 | bytes 13631488 | tf_op jit(solution)/shard_map/pallas_call | solution.py:155
  9.0 5.0 %collective-permute-start = (f32[2,256,512]{1,2,0:T(8,128)S(1)}, f32[2,256,512]{1,2,0:T(8,128)S(1)}, u32[]{:S(2)}, u32[]{:S(2)}) collective-permute-start(f32[2,256,512]{1,2,0:T(8,128)S(1)} %bitcast.43), channel_id=1, source_target_pairs={{0,4},{1,5},{2,6},{3,7},{16,20},{17,21},{18,22},{19,23}} | collective-permute-start | bytes 3145736 | tf_op jit(solution)/shard_map/ppermute | solution.py:228
  14.1 0.7 collective-permute-start.3
  14.8 8.4 %shard_map.44 = f32[2,512,256]{2,1,0:T(8,128)S(1)} custom-call(s32[1]{0:T(128)} %bitcast.8.index_ref, bf16[2,1024,4096]{2,1,0:T(8,128)(2,1)} %bitcast.46, bf16[2,4096,512]{2,1,0:T(8,128)(2,1)} %bitcast.50), custom_call_target="tpu_custom_call" | custom-call | flops 4294967296 | bytes 13631488 | tf_op jit(solution)/shard_map/pallas_call | solution.py:155
  23.2 13.2 %collective-permute-done = f32[2,256,512]{1,2,0:T(8,128)S(1)} collective-permute-done((f32[2,256,512]{1,2,0:T(8,128)S(1)}, f32[2,256,512]{1,2,0:T(8,128)S(1)}, u32[]{:S(2)}, u32[]{:S(2)}) %collective-permute-start) | collective-permute-done | bytes 1048608 | tf_op jit(solution)/shard_map/ppermute | solution.py:228
  36.4 1.6 %bitcast_add_fusion.1 = (f32[2,256,512]{1,2,0:T(8,128)}, f32[2,256,512]{1,2,0:T(8,128)}) fusion(f32[2,256,512]{1,2,0:T(8,128)S(1)} %collective-permute-done, f32[2,512,256]{2,1,0:T(8,128)S(1)} %shard_map.44, f32[2,256,512]{1,2,0:T(8,128)S(1)} %collective-permute-done.3), kind=kLoop, calls=%fused_computation.2 | loop fusion | flops 524288 | bytes 5242880 | tf_op jit(solution)/shard_map/add | solution.py:226
  38.0 5.4 %collective-permute-start.1 = (f32[2,256,512]{1,2,0:T(8,128)}, f32[2,256,512]{1,2,0:T(8,128)}, u32[]{:S(2)}, u32[]{:S(2)}) collective-permute-start(f32[2,256,512]{1,2,0:T(8,128)} %get-tuple-element.14), channel_id=1, source_target_pairs={{0,4},{4,8},{1,5},{5,9},{2,6},{6,10},{3,7},{7,11},{16,20},{20,24},... | collective-permute-start | bytes 3145736 | tf_op jit(solution)/shard_map/ppermute | solution.py:228
  43.4 0.7 collective-permute-start.4
  44.1 8.4 %shard_map.42 = f32[2,512,256]{2,1,0:T(8,128)S(1)} custom-call(s32[1]{0:T(128)} %bitcast.4.index_ref, bf16[2,1024,4096]{2,1,0:T(8,128)(2,1)} %bitcast.47, bf16[2,4096,512]{2,1,0:T(8,128)(2,1)} %bitcast.51), custom_call_target="tpu_custom_call" | custom-call | flops 4294967296 | bytes 13631488 | tf_op jit(solution)/shard_map/pallas_call | solution.py:155
  52.5 8.4 %shard_map.41 = f32[2,512,256]{2,1,0:T(8,128)S(1)} custom-call(s32[1]{0:T(128)} %bitcast.index_ref, bf16[2,1024,4096]{2,1,0:T(8,128)(2,1)} %bitcast.48, bf16[2,4096,512]{2,1,0:T(8,128)(2,1)} %bitcast.52), custom_call_target="tpu_custom_call" | custom-call | flops 4294967296 | bytes 13631488 | tf_op jit(solution)/shard_map/pallas_call | solution.py:155
  60.9 3.4 %collective-permute-done.1 = f32[2,256,512]{1,2,0:T(8,128)} collective-permute-done((f32[2,256,512]{1,2,0:T(8,128)}, f32[2,256,512]{1,2,0:T(8,128)}, u32[]{:S(2)}, u32[]{:S(2)}) %collective-permute-start.1) | collective-permute-done | bytes 1048608 | tf_op jit(solution)/shard_map/ppermute | solution.py:228
  64.2 2.4 %bitcast_add_fusion.2 = f32[2,256,512]{1,2,0:T(8,128)} fusion(f32[2,256,512]{1,2,0:T(8,128)} %collective-permute-done.1, f32[2,512,256]{2,1,0:T(8,128)S(1)} %shard_map.42), kind=kLoop, calls=%fused_computation.3 | loop fusion | flops 262144 | bytes 3145728 | tf_op jit(solution)/shard_map/add | solution.py:226
  66.6 5.4 %collective-permute-start.2 = (f32[2,256,512]{1,2,0:T(8,128)}, f32[2,256,512]{1,2,0:T(8,128)}, u32[]{:S(2)}, u32[]{:S(2)}) collective-permute-start(f32[2,256,512]{1,2,0:T(8,128)} %bitcast_add_fusion.2), channel_id=1, source_target_pairs={{0,4},{4,8},{8,12},{1,5},{5,9},{9,13},{2,6},{6,10},{10,14},{3,7},{... | collective-permute-start | bytes 3145736 | tf_op jit(solution)/shard_map/ppermute | solution.py:228
  72.0 1.1 %bitcast_add_fusion.3 = f32[2,256,512]{1,2,0:T(8,128)} fusion(f32[2,256,512]{1,2,0:T(8,128)S(1)} %collective-permute-done.4, f32[2,512,256]{2,1,0:T(8,128)S(1)} %shard_map.41), kind=kLoop, calls=%fused_computation.8 | loop fusion | flops 262144 | bytes 3145728 | tf_op jit(solution)/shard_map/add | solution.py:227
  73.1 1.3 %collective-permute-start.5 = (f32[2,256,512]{1,2,0:T(8,128)}, f32[2,256,512]{1,2,0:T(8,128)}, u32[]{:S(2)}, u32[]{:S(2)}) collective-permute-start(f32[2,256,512]{1,2,0:T(8,128)} %bitcast_add_fusion.3), channel_id=1, source_target_pairs={{4,0},{8,4},{12,8},{5,1},{9,5},{13,9},{6,2},{10,6},{14,10},{7,3},{... | collective-permute-start | bytes 3145736 | tf_op jit(solution)/shard_map/ppermute | solution.py:229
  74.4 17.6 %collective-permute-done.2 = f32[2,256,512]{1,2,0:T(8,128)} collective-permute-done((f32[2,256,512]{1,2,0:T(8,128)}, f32[2,256,512]{1,2,0:T(8,128)}, u32[]{:S(2)}, u32[]{:S(2)}) %collective-permute-start.2) | collective-permute-done | bytes 1048608 | tf_op jit(solution)/shard_map/ppermute | solution.py:228
  92.0 6.2 %collective-permute-done.5 = f32[2,256,512]{1,2,0:T(8,128)} collective-permute-done((f32[2,256,512]{1,2,0:T(8,128)}, f32[2,256,512]{1,2,0:T(8,128)}, u32[]{:S(2)}, u32[]{:S(2)}) %collective-permute-start.5) | collective-permute-done | bytes 1048608 | tf_op jit(solution)/shard_map/ppermute | solution.py:229
  98.2 1.9 %fusion.2 = f32[2,256,512]{1,2,0:T(8,128)S(1)} fusion(f32[2,256,512]{1,2,0:T(8,128)} %collective-permute-done.5, f32[2,256,512]{1,2,0:T(8,128)} %collective-permute-done.2, f32[2,512,256]{2,1,0:T(8,128)S(1)} %shard_map.42, f32[2,512,256]{2,1,0:T(8,128)S(1)} %shard_map.41, pred[]{:T(512)S(6)} %eq.19, pred[]{:T(512)S(6)} %eq.18, f32[2,512,256]{2,1,0:T(8,128)S(1)} %shard_map.43), kind=kLoop, calls=%fused_computation.7 | loop fusion | flops 1048576 | bytes 6291458 | tf_op jit(solution)/shard_map/add | solution.py:235
  100.7 2.3 %collective-permute-done.6 = f32[2,256,8,64]{1,3,2,0:T(8,128)S(1)} collective-permute-done((f32[2,256,8,64]{1,3,2,0:T(8,128)S(1)}, f32[2,256,8,64]{1,3,2,0:T(8,128)S(1)}, u32[]{:S(2)}, u32[]{:S(2)}) %collective-permute-start.6) | collective-permute-done | bytes 1048608 | tf_op jit(solution)/shard_map/ppermute | solution.py:16
  103.2 0.3 subtract_reduce_fusion
  103.6 1.6 %collective-permute-start.7 = (f32[7,256,1]{1,2,0:T(1,128)S(1)}, f32[7,256,1]{1,2,0:T(1,128)S(1)}, u32[]{:S(2)}, u32[]{:S(2)}) collective-permute-start(f32[7,256,1]{1,2,0:T(1,128)S(1)} %broadcast_select_fusion.4), channel_id=1, source_target_pairs={{0,2},{2,0},{1,3},{3,1},{4,6},{6,4},{5,7},{7,5},{8,10},{10,8},{9,1... | collective-permute-start | bytes 21512 | tf_op jit(solution)/shard_map/ppermute | solution.py:26
  105.1 2.1 %collective-permute-done.7 = f32[7,256,1]{1,2,0:T(1,128)S(1)} collective-permute-done((f32[7,256,1]{1,2,0:T(1,128)S(1)}, f32[7,256,1]{1,2,0:T(1,128)S(1)}, u32[]{:S(2)}, u32[]{:S(2)}) %collective-permute-start.7) | collective-permute-done | bytes 7200 | tf_op jit(solution)/shard_map/ppermute | solution.py:26
  107.4 0.6 slice_divide_fusion
  108.0 0.6 maximum_bitcast_fusion
  (19 shorter events, 0.8 us)
Async XLA Ops:
  9.0 27.4 %collective-permute-start = (f32[2,256,512]{1,2,0:T(8,128)S(1)}, f32[2,256,512]{1,2,0:T(8,128)S(1)}, u32[]{:S(2)}, u32[]{:S(2)}) collective-permute-start(f32[2,256,512]{1,2,0:T(8,128)S(1)} %bitcast.43), channel_id=1, source_target_pairs={{0,4},{1,5},{2,6},{3,7},{16,20},{17,21},{18,22},{19,23}} | collective-permute-start | bytes 3145736 | tf_op jit(solution)/shard_map/ppermute | solution.py:228
  14.1 22.3 %collective-permute-start.3 = (f32[2,256,512]{1,2,0:T(8,128)S(1)}, f32[2,256,512]{1,2,0:T(8,128)S(1)}, u32[]{:S(2)}, u32[]{:S(2)}) collective-permute-start(f32[2,256,512]{1,2,0:T(8,128)S(1)} %bitcast.44), channel_id=1, source_target_pairs={{12,8},{13,9},{14,10},{15,11},{28,24},{29,25},{30,26},{31,27}} | collective-permute-start | bytes 3145736 | tf_op jit(solution)/shard_map/ppermute | solution.py:229
  38.0 26.2 %collective-permute-start.1 = (f32[2,256,512]{1,2,0:T(8,128)}, f32[2,256,512]{1,2,0:T(8,128)}, u32[]{:S(2)}, u32[]{:S(2)}) collective-permute-start(f32[2,256,512]{1,2,0:T(8,128)} %get-tuple-element.14), channel_id=1, source_target_pairs={{0,4},{4,8},{1,5},{5,9},{2,6},{6,10},{3,7},{7,11},{16,20},{20,24},... | collective-permute-start | bytes 3145736 | tf_op jit(solution)/shard_map/ppermute | solution.py:228
  43.4 28.6 %collective-permute-start.4 = (f32[2,256,512]{1,2,0:T(8,128)}, f32[2,256,512]{1,2,0:T(8,128)S(1)}, u32[]{:S(2)}, u32[]{:S(2)}) collective-permute-start(f32[2,256,512]{1,2,0:T(8,128)} %get-tuple-element.15), channel_id=1, source_target_pairs={{8,4},{12,8},{9,5},{13,9},{10,6},{14,10},{11,7},{15,11},{24,20},{2... | collective-permute-start | bytes 3145736 | tf_op jit(solution)/shard_map/ppermute | solution.py:229
  66.6 25.4 %collective-permute-start.2 = (f32[2,256,512]{1,2,0:T(8,128)}, f32[2,256,512]{1,2,0:T(8,128)}, u32[]{:S(2)}, u32[]{:S(2)}) collective-permute-start(f32[2,256,512]{1,2,0:T(8,128)} %bitcast_add_fusion.2), channel_id=1, source_target_pairs={{0,4},{4,8},{8,12},{1,5},{5,9},{9,13},{2,6},{6,10},{10,14},{3,7},{... | collective-permute-start | bytes 3145736 | tf_op jit(solution)/shard_map/ppermute | solution.py:228
  73.1 25.1 %collective-permute-start.5 = (f32[2,256,512]{1,2,0:T(8,128)}, f32[2,256,512]{1,2,0:T(8,128)}, u32[]{:S(2)}, u32[]{:S(2)}) collective-permute-start(f32[2,256,512]{1,2,0:T(8,128)} %bitcast_add_fusion.3), channel_id=1, source_target_pairs={{4,0},{8,4},{12,8},{5,1},{9,5},{13,9},{6,2},{10,6},{14,10},{7,3},{... | collective-permute-start | bytes 3145736 | tf_op jit(solution)/shard_map/ppermute | solution.py:229
  100.3 2.7 %collective-permute-start.6 = (f32[2,256,8,64]{1,3,2,0:T(8,128)S(1)}, f32[2,256,8,64]{1,3,2,0:T(8,128)S(1)}, u32[]{:S(2)}, u32[]{:S(2)}) collective-permute-start(f32[2,256,8,64]{1,3,2,0:T(8,128)S(1)} %pad_maximum_fusion), channel_id=1, source_target_pairs={{0,1},{1,0},{2,3},{3,2},{4,5},{5,4},{6,7},{7,6},{8,9},{9,8},{10,11... | collective-permute-start | bytes 3145736 | tf_op jit(solution)/shard_map/ppermute | solution.py:16
  103.6 3.7 %collective-permute-start.7 = (f32[7,256,1]{1,2,0:T(1,128)S(1)}, f32[7,256,1]{1,2,0:T(1,128)S(1)}, u32[]{:S(2)}, u32[]{:S(2)}) collective-permute-start(f32[7,256,1]{1,2,0:T(1,128)S(1)} %broadcast_select_fusion.4), channel_id=1, source_target_pairs={{0,2},{2,0},{1,3},{3,1},{4,6},{6,4},{5,7},{7,5},{8,10},{10,8},{9,1... | collective-permute-start | bytes 21512 | tf_op jit(solution)/shard_map/ppermute | solution.py:26

commit v10 on v8

--- a/solution.py
+++ b/solution.py
@@ -207,8 +207,11 @@
     local = weights.shape[2] // n_elem
     table, serves, own_call = send_plan(n_elem)
     made = []
-    for row in table:
-        index = jnp.asarray(row, jnp.int32)[me]
+    for k, row in enumerate(table):
+        if k == 0 and row == [n_elem - 1] + list(range(1, n_elem - 1)) + [0]:
+            index = jnp.where(me == 0, n_elem - 1, jnp.where(me == n_elem - 1, 0, me)).astype(jnp.int32)
+        else:
+            index = jnp.asarray(row, jnp.int32)[me]
         made.append(jnp.swapaxes(block_partial(signal, weights, index, local), 1, 2))
     got_right = None
     got_left = None

time: 104 us -> 103 us (level)
  local copies, waits for them, and re-layouts: 3.69 us -> 2.45 us
    dynamic_slice x4 -> x3, local copies, waits for them, and re-layouts: 3.01 us -> 1.76 us  [line_scatter(): index = jnp.asarray(row, jnp.int32)[me]]
  transfers between devices with their start and end apart: 8 -> 8, of which waited for: 6 -> 6; matrix products, arithmetic and copies ran while one was open for 3% -> 3% of each run, Pallas kernels for 26% -> 27%
where the time goes in v10:
time: 103 us; the launch traced here: 102 us
  waiting for transfers between devices  40.7 us (40%)
  Pallas kernels  35.5 us (34%)
  starting transfers between devices  18.3 us (18%)
  other arithmetic  3.07 us (3%)
  local copies, waits for them, and re-layouts  2.45 us (2%)
  between operations  2.25 us (2%)
    pallas_call x4, Pallas kernels, block_partial(): pl.pallas_call(block_kernel, out_shape=jax.ShapeDtypeStruct((2, samples,...  35.5 us
    ppermute x3, waiting for transfers between devices, line_scatter(): lax.ppermute(to_right, 'elem', [(c, c + 1) for c in range(step)])  30.7 us
    ppermute x3, starting transfers between devices, line_scatter(): lax.ppermute(to_right, 'elem', [(c, c + 1) for c in range(step)])  13.9 us
    ppermute x3, waiting for transfers between devices, line_scatter(): lax.ppermute(to_left, 'elem', [(c, c - 1) for c in range(n_elem - step, n...  5.6 us
    ppermute x3, starting transfers between devices, line_scatter(): lax.ppermute(to_left, 'elem', [(c, c - 1) for c in range(n_elem - step, n...  2.74 us
    ppermute x1, waiting for transfers between devices, swapped(): return lax.ppermute(value, axis, pairs)  2.26 us
    ppermute x1, waiting for transfers between devices, with_halo(): got = lax.ppermute(sent, axis, [(0, 1), (1, 0)])  2.16 us
  transfers between devices with their start and end apart: 8, of which 6 were waited for; matrix products, arithmetic and copies ran while one was open for 3% of the time, Pallas kernels for 27%

profile of v10, /device:TPU:0, one launch (start us, length us, event | category | flops | bytes accessed | tf_op | source)
XLA Modules:
  0.0 102.2 jit_solution(5537646391121048412)
XLA Ops:
  0.7 8.4 %shard_map.79 = f32[2,512,256]{2,1,0:T(8,128)S(1)} custom-call(s32[1]{0:T(128)} %bitcast.6.index_ref, bf16[2,1024,4096]{2,1,0:T(8,128)(2,1)} %bitcast.44, bf16[2,4096,512]{2,1,0:T(8,128)(2,1)} %bitcast.48), custom_call_target="tpu_custom_call" | custom-call | flops 4294967296 | bytes 13631488 | tf_op jit(solution)/shard_map/pallas_call | solution.py:155
  9.1 5.0 %collective-permute-start = (f32[2,256,512]{1,2,0:T(8,128)S(1)}, f32[2,256,512]{1,2,0:T(8,128)S(1)}, u32[]{:S(2)}, u32[]{:S(2)}) collective-permute-start(f32[2,256,512]{1,2,0:T(8,128)S(1)} %bitcast.42), channel_id=1, source_target_pairs={{0,4},{1,5},{2,6},{3,7},{16,20},{17,21},{18,22},{19,23}} | collective-permute-start | bytes 3145736 | tf_op jit(solution)/shard_map/ppermute | solution.py:225
  14.1 0.7 collective-permute-start.3
  14.8 0.6 dynamic_slice.15.index_ref
  15.4 9.0 %shard_map.80 = f32[2,512,256]{2,1,0:T(8,128)S(1)} custom-call(s32[1]{0:T(128)} %dynamic_slice.15.index_ref, bf16[2,1024,4096]{2,1,0:T(8,128)(2,1)} %bitcast.45, bf16[2,4096,512]{2,1,0:T(8,128)(2,1)} %bitcast.49), custom_call_target="tpu_custom_call" | custom-call | flops 4294967296 | bytes 13631488 | tf_op jit(solution)/shard_map/pallas_call | solution.py:155
  24.5 12.0 %collective-permute-done = f32[2,256,512]{1,2,0:T(8,128)S(1)} collective-permute-done((f32[2,256,512]{1,2,0:T(8,128)S(1)}, f32[2,256,512]{1,2,0:T(8,128)S(1)}, u32[]{:S(2)}, u32[]{:S(2)}) %collective-permute-start) | collective-permute-done | bytes 1048608 | tf_op jit(solution)/shard_map/ppermute | solution.py:225
  36.7 4.5 %collective-permute-start.1 = (f32[2,256,512]{1,2,0:T(8,128)S(1)}, f32[2,256,512]{1,2,0:T(8,128)S(1)}, u32[]{:S(2)}, u32[]{:S(2)}) collective-permute-start(f32[2,256,512]{1,2,0:T(8,128)S(1)} %get-tuple-element.14), channel_id=1, source_target_pairs={{0,4},{4,8},{1,5},{5,9},{2,6},{6,10},{3,7},{7,11},{16,20},{20,24},... | collective-permute-start | bytes 3145736 | tf_op jit(solution)/shard_map/ppermute | solution.py:225
  41.1 0.6 dynamic_slice.14.index_ref
  41.7 0.6 dynamic_slice.13.index_ref
  42.3 0.7 collective-permute-start.4
  43.0 9.0 %shard_map.78 = f32[2,512,256]{2,1,0:T(8,128)S(1)} custom-call(s32[1]{0:T(128)} %dynamic_slice.14.index_ref, bf16[2,1024,4096]{2,1,0:T(8,128)(2,1)} %bitcast.46, bf16[2,4096,512]{2,1,0:T(8,128)(2,1)} %bitcast.50), custom_call_target="tpu_custom_call" | custom-call | flops 4294967296 | bytes 13631488 | tf_op jit(solution)/shard_map/pallas_call | solution.py:155
  52.1 9.0 %shard_map.77 = f32[2,512,256]{2,1,0:T(8,128)S(1)} custom-call(s32[1]{0:T(128)} %dynamic_slice.13.index_ref, bf16[2,1024,4096]{2,1,0:T(8,128)(2,1)} %bitcast.47, bf16[2,4096,512]{2,1,0:T(8,128)(2,1)} %bitcast.51), custom_call_target="tpu_custom_call" | custom-call | flops 4294967296 | bytes 13631488 | tf_op jit(solution)/shard_map/pallas_call | solution.py:155
  61.1 1.5 %collective-permute-done.1 = f32[2,256,512]{1,2,0:T(8,128)S(1)} collective-permute-done((f32[2,256,512]{1,2,0:T(8,128)S(1)}, f32[2,256,512]{1,2,0:T(8,128)S(1)}, u32[]{:S(2)}, u32[]{:S(2)}) %collective-permute-start.1) | collective-permute-done | bytes 1048608 | tf_op jit(solution)/shard_map/ppermute | solution.py:225
  62.7 4.5 %collective-permute-start.2 = (f32[2,256,512]{1,2,0:T(8,128)S(1)}, f32[2,256,512]{1,2,0:T(8,128)S(1)}, u32[]{:S(2)}, u32[]{:S(2)}) collective-permute-start(f32[2,256,512]{1,2,0:T(8,128)S(1)} %bitcast_add_fusion.2), channel_id=1, source_target_pairs={{0,4},{4,8},{8,12},{1,5},{5,9},{9,13},{2,6},{6,10},{10,14},{3,7},{... | collective-permute-start | bytes 3145736 | tf_op jit(solution)/shard_map/ppermute | solution.py:225
  67.3 1.3 %collective-permute-start.5 = (f32[2,256,512]{1,2,0:T(8,128)S(1)}, f32[2,256,512]{1,2,0:T(8,128)S(1)}, u32[]{:S(2)}, u32[]{:S(2)}) collective-permute-start(f32[2,256,512]{1,2,0:T(8,128)S(1)} %bitcast_add_fusion.3), channel_id=1, source_target_pairs={{4,0},{8,4},{12,8},{5,1},{9,5},{13,9},{6,2},{10,6},{14,10},{7,3},{... | collective-permute-start | bytes 3145736 | tf_op jit(solution)/shard_map/ppermute | solution.py:226
  68.6 0.6 dynamic_slice.12
  70.5 17.3 %collective-permute-done.2 = f32[2,256,512]{1,2,0:T(8,128)S(1)} collective-permute-done((f32[2,256,512]{1,2,0:T(8,128)S(1)}, f32[2,256,512]{1,2,0:T(8,128)S(1)}, u32[]{:S(2)}, u32[]{:S(2)}) %collective-permute-start.2) | collective-permute-done | bytes 1048608 | tf_op jit(solution)/shard_map/ppermute | solution.py:225
  87.8 5.6 %collective-permute-done.5 = f32[2,256,512]{1,2,0:T(8,128)S(1)} collective-permute-done((f32[2,256,512]{1,2,0:T(8,128)S(1)}, f32[2,256,512]{1,2,0:T(8,128)S(1)}, u32[]{:S(2)}, u32[]{:S(2)}) %collective-permute-start.5) | collective-permute-done | bytes 1048608 | tf_op jit(solution)/shard_map/ppermute | solution.py:226
  93.4 0.3 fusion.2
  94.4 2.3 %collective-permute-done.6 = f32[2,256,8,64]{1,3,2,0:T(8,128)S(1)} collective-permute-done((f32[2,256,8,64]{1,3,2,0:T(8,128)S(1)}, f32[2,256,8,64]{1,3,2,0:T(8,128)S(1)}, u32[]{:S(2)}, u32[]{:S(2)}) %collective-permute-start.6) | collective-permute-done | bytes 1048608 | tf_op jit(solution)/shard_map/ppermute | solution.py:16
  97.2 1.5 %collective-permute-start.7 = (f32[7,256,1]{1,2,0:T(1,128)S(1)}, f32[7,256,1]{1,2,0:T(1,128)S(1)}, u32[]{:S(2)}, u32[]{:S(2)}) collective-permute-start(f32[7,256,1]{1,2,0:T(1,128)S(1)} %broadcast_select_fusion.4), channel_id=1, source_target_pairs={{0,2},{2,0},{1,3},{3,1},{4,6},{6,4},{5,7},{7,5},{8,10},{10,8},{9,1... | collective-permute-start | bytes 21512 | tf_op jit(solution)/shard_map/ppermute | solution.py:26
  98.8 2.2 %collective-permute-done.7 = f32[7,256,1]{1,2,0:T(1,128)S(1)} collective-permute-done((f32[7,256,1]{1,2,0:T(1,128)S(1)}, f32[7,256,1]{1,2,0:T(1,128)S(1)}, u32[]{:S(2)}, u32[]{:S(2)}) %collective-permute-start.7) | collective-permute-done | bytes 7200 | tf_op jit(solution)/shard_map/ppermute | solution.py:26
  101.0 0.6 slice_divide_fusion
  101.6 0.6 maximum_bitcast_fusion
  (31 shorter events, 1.7 us)
Async XLA Ops:
  0.6 14.2 %copy-start.3 = (s32[4]{0:T(128)S(1)}, s32[4]{0:T(128)}, u32[]{:S(2)}) copy-start(s32[4]{0:T(128)} %constant.56.clone) | copy-start | bytes 52
  9.0 32.1 %copy-start.2 = (s32[4]{0:T(128)S(1)}, s32[4]{0:T(128)}, u32[]{:S(2)}) copy-start(s32[4]{0:T(128)} %constant.57.clone) | copy-start | bytes 52
  9.1 32.7 %copy-start.1 = (s32[4]{0:T(128)S(1)}, s32[4]{0:T(128)}, u32[]{:S(2)}) copy-start(s32[4]{0:T(128)} %constant.58.clone) | copy-start | bytes 52
  9.1 27.4 %collective-permute-start = (f32[2,256,512]{1,2,0:T(8,128)S(1)}, f32[2,256,512]{1,2,0:T(8,128)S(1)}, u32[]{:S(2)}, u32[]{:S(2)}) collective-permute-start(f32[2,256,512]{1,2,0:T(8,128)S(1)} %bitcast.42), channel_id=1, source_target_pairs={{0,4},{1,5},{2,6},{3,7},{16,20},{17,21},{18,22},{19,23}} | collective-permute-start | bytes 3145736 | tf_op jit(solution)/shard_map/ppermute | solution.py:225
  14.1 22.3 %collective-permute-start.3 = (f32[2,256,512]{1,2,0:T(8,128)S(1)}, f32[2,256,512]{1,2,0:T(8,128)S(1)}, u32[]{:S(2)}, u32[]{:S(2)}) collective-permute-start(f32[2,256,512]{1,2,0:T(8,128)S(1)} %bitcast.43), channel_id=1, source_target_pairs={{12,8},{13,9},{14,10},{15,11},{28,24},{29,25},{30,26},{31,27}} | collective-permute-start | bytes 3145736 | tf_op jit(solution)/shard_map/ppermute | solution.py:226
  36.7 25.9 %collective-permute-start.1 = (f32[2,256,512]{1,2,0:T(8,128)S(1)}, f32[2,256,512]{1,2,0:T(8,128)S(1)}, u32[]{:S(2)}, u32[]{:S(2)}) collective-permute-start(f32[2,256,512]{1,2,0:T(8,128)S(1)} %get-tuple-element.14), channel_id=1, source_target_pairs={{0,4},{4,8},{1,5},{5,9},{2,6},{6,10},{3,7},{7,11},{16,20},{20,24},... | collective-permute-start | bytes 3145736 | tf_op jit(solution)/shard_map/ppermute | solution.py:225
  42.3 24.9 %collective-permute-start.4 = (f32[2,256,512]{1,2,0:T(8,128)S(1)}, f32[2,256,512]{1,2,0:T(8,128)S(1)}, u32[]{:S(2)}, u32[]{:S(2)}) collective-permute-start(f32[2,256,512]{1,2,0:T(8,128)S(1)} %get-tuple-element.15), channel_id=1, source_target_pairs={{8,4},{12,8},{9,5},{13,9},{10,6},{14,10},{11,7},{15,11},{24,20},{2... | collective-permute-start | bytes 3145736 | tf_op jit(solution)/shard_map/ppermute | solution.py:226
  52.1 16.6 %copy-start = (s32[4]{0:T(128)S(1)}, s32[4]{0:T(128)}, u32[]{:S(2)}) copy-start(s32[4]{0:T(128)} %constant.59.clone) | copy-start | bytes 52
  62.7 25.1 %collective-permute-start.2 = (f32[2,256,512]{1,2,0:T(8,128)S(1)}, f32[2,256,512]{1,2,0:T(8,128)S(1)}, u32[]{:S(2)}, u32[]{:S(2)}) collective-permute-start(f32[2,256,512]{1,2,0:T(8,128)S(1)} %bitcast_add_fusion.2), channel_id=1, source_target_pairs={{0,4},{4,8},{8,12},{1,5},{5,9},{9,13},{2,6},{6,10},{10,14},{3,7},{... | collective-permute-start | bytes 3145736 | tf_op jit(solution)/shard_map/ppermute | solution.py:225
  67.3 26.1 %collective-permute-start.5 = (f32[2,256,512]{1,2,0:T(8,128)S(1)}, f32[2,256,512]{1,2,0:T(8,128)S(1)}, u32[]{:S(2)}, u32[]{:S(2)}) collective-permute-start(f32[2,256,512]{1,2,0:T(8,128)S(1)} %bitcast_add_fusion.3), channel_id=1, source_target_pairs={{4,0},{8,4},{12,8},{5,1},{9,5},{13,9},{6,2},{10,6},{14,10},{7,3},{... | collective-permute-start | bytes 3145736 | tf_op jit(solution)/shard_map/ppermute | solution.py:226
  93.9 2.7 %collective-permute-start.6 = (f32[2,256,8,64]{1,3,2,0:T(8,128)S(1)}, f32[2,256,8,64]{1,3,2,0:T(8,128)S(1)}, u32[]{:S(2)}, u32[]{:S(2)}) collective-permute-start(f32[2,256,8,64]{1,3,2,0:T(8,128)S(1)} %pad_maximum_fusion), channel_id=1, source_target_pairs={{0,1},{1,0},{2,3},{3,2},{4,5},{5,4},{6,7},{7,6},{8,9},{9,8},{10,11... | collective-permute-start | bytes 3145736 | tf_op jit(solution)/shard_map/ppermute | solution.py:16
  97.2 3.7 %collective-permute-start.7 = (f32[7,256,1]{1,2,0:T(1,128)S(1)}, f32[7,256,1]{1,2,0:T(1,128)S(1)}, u32[]{:S(2)}, u32[]{:S(2)}) collective-permute-start(f32[7,256,1]{1,2,0:T(1,128)S(1)} %broadcast_select_fusion.4), channel_id=1, source_target_pairs={{0,2},{2,0},{1,3},{3,1},{4,6},{6,4},{5,7},{7,5},{8,10},{10,8},{9,1... | collective-permute-start | bytes 21512 | tf_op jit(solution)/shard_map/ppermute | solution.py:26

commit v11 on v10

--- a/solution.py
+++ b/solution.py
@@ -207,11 +207,12 @@
     local = weights.shape[2] // n_elem
     table, serves, own_call = send_plan(n_elem)
     made = []
+    later = jnp.asarray(table, jnp.int32)[:, me]
     for k, row in enumerate(table):
         if k == 0 and row == [n_elem - 1] + list(range(1, n_elem - 1)) + [0]:
             index = jnp.where(me == 0, n_elem - 1, jnp.where(me == n_elem - 1, 0, me)).astype(jnp.int32)
         else:
-            index = jnp.asarray(row, jnp.int32)[me]
+            index = later[k]
         made.append(jnp.swapaxes(block_partial(signal, weights, index, local), 1, 2))
     got_right = None
     got_left = None
@@ -222,8 +223,14 @@
         if got_right is not None:
             to_right = to_right + got_right
             to_left = to_left + got_left
-        got_right = lax.ppermute(to_right, "elem", [(c, c + 1) for c in range(step)])
-        got_left = lax.ppermute(to_left, "elem", [(c, c - 1) for c in range(n_elem - step, n_elem)])
+        pairs_right = [(c, c + 1) for c in range(step)]
+        pairs_left = [(c, c - 1) for c in range(n_elem - step, n_elem)]
+        merged = pairs_right + pairs_left
+        if "both" in calls and got_right is None and len({t for _, t in merged}) == len(merged):
+            got_right = got_left = lax.ppermute(to_right, "elem", merged)
+        else:
+            got_right = lax.ppermute(to_right, "elem", pairs_right)
+            got_left = lax.ppermute(to_left, "elem", pairs_left)
     own_at = jnp.asarray([own_call[c] for c in range(n_elem)], jnp.int32)[me]
     used = sorted(set(own_call.values()))
     own = made[used[0]]

time: 103 us -> 101 us (0.981)
  local copies, waits for them, and re-layouts: 2.45 us -> 1.35 us
    dynamic_slice x3 -> x1, local copies, waits for them, and re-layouts: 1.76 us -> 0.08 us  [line_scatter(): later = jnp.asarray(table, jnp.int32)[:, me]]
    ppermute x6 -> x5, starting transfers between devices: 16.7 us -> 15.9 us  [the longest x2 8.9 us: line_scatter(): got_right = lax.ppermute(to_right, 'elem', pairs_right)]
    ppermute x6 -> x5, waiting for transfers between devices: 36.3 us -> 36.8 us  [the longest x2 19.9 us: line_scatter(): got_right = lax.ppermute(to_right, 'elem', pairs_right)]
  transfers between devices with their start and end apart: 8 -> 7, of which waited for: 6 -> 6; matrix products, arithmetic and copies ran while one was open for 3% -> 2% of each run, Pallas kernels for 27% -> 27%
where the time goes in v11:
time: 101 us
  waiting for transfers between devices  41.2 us (41%)
  Pallas kernels  35.5 us (35%)
  starting transfers between devices  17.6 us (17%)
  other arithmetic  3 us (3%)
  between operations  2.22 us (2%)
  local copies, waits for them, and re-layouts  1.35 us (1%)
    pallas_call x4, Pallas kernels, block_partial(): pl.pallas_call(block_kernel, out_shape=jax.ShapeDtypeStruct((2, samples,...  35.5 us
    ppermute x2, waiting for transfers between devices, line_scatter(): got_right = lax.ppermute(to_right, 'elem', pairs_right)  19.9 us
    ppermute x1, waiting for transfers between devices, line_scatter(): got_right = got_left = lax.ppermute(to_right, 'elem', merged)  12.6 us
    ppermute x2, starting transfers between devices, line_scatter(): got_right = lax.ppermute(to_right, 'elem', pairs_right)  8.9 us
    ppermute x1, starting transfers between devices, line_scatter(): got_right = got_left = lax.ppermute(to_right, 'elem', merged)  5.02 us
    ppermute x2, waiting for transfers between devices, line_scatter(): got_left = lax.ppermute(to_left, 'elem', pairs_left)  4.34 us
    ppermute x1, waiting for transfers between devices, swapped(): return lax.ppermute(value, axis, pairs)  2.26 us
    ppermute x1, waiting for transfers between devices, with_halo(): got = lax.ppermute(sent, axis, [(0, 1), (1, 0)])  2.15 us
  transfers between devices with their start and end apart: 7, of which 6 were waited for; matrix products, arithmetic and copies ran while one was open for 2% of the time, Pallas kernels for 27%

profile of v11, /device:TPU:0, one launch (start us, length us, event | category | flops | bytes accessed | tf_op | source)
XLA Modules:
  0.0 100.9 jit_solution(16487698475649515003)
XLA Ops:
  0.7 8.4 %shard_map.61 = f32[2,512,256]{2,1,0:T(8,128)S(1)} custom-call(s32[1]{0:T(128)} %bitcast.8.index_ref, bf16[2,1024,4096]{2,1,0:T(8,128)(2,1)} %bitcast.45, bf16[2,4096,512]{2,1,0:T(8,128)(2,1)} %bitcast.49), custom_call_target="tpu_custom_call" | custom-call | flops 4294967296 | bytes 13631488 | tf_op jit(solution)/shard_map/pallas_call | solution.py:155
  9.0 5.0 %collective-permute-start = (f32[2,256,512]{1,2,0:T(8,128)S(1)}, f32[2,256,512]{1,2,0:T(8,128)S(1)}, u32[]{:S(2)}, u32[]{:S(2)}) collective-permute-start(f32[2,256,512]{1,2,0:T(8,128)S(1)} %bitcast.44), channel_id=1, source_target_pairs={{0,4},{12,8},{1,5},{13,9},{2,6},{14,10},{3,7},{15,11},{16,20},{28,... | collective-permute-start | bytes 3145736 | tf_op jit(solution)/shard_map/ppermute | solution.py:230
  14.2 0.6 fusion.11
  14.8 9.0 %shard_map.62 = f32[2,512,256]{2,1,0:T(8,128)S(1)} custom-call(s32[1]{0:T(128)} %bitcast.10.index_ref, bf16[2,1024,4096]{2,1,0:T(8,128)(2,1)} %bitcast.46, bf16[2,4096,512]{2,1,0:T(8,128)(2,1)} %bitcast.50), custom_call_target="tpu_custom_call" | custom-call | flops 4294967296 | bytes 13631488 | tf_op jit(solution)/shard_map/pallas_call | solution.py:155
  23.8 12.6 %collective-permute-done = f32[2,256,512]{1,2,0:T(8,128)S(1)} collective-permute-done((f32[2,256,512]{1,2,0:T(8,128)S(1)}, f32[2,256,512]{1,2,0:T(8,128)S(1)}, u32[]{:S(2)}, u32[]{:S(2)}) %collective-permute-start) | collective-permute-done | bytes 1048608 | tf_op jit(solution)/shard_map/ppermute | solution.py:230
  36.6 4.5 %collective-permute-start.1 = (f32[2,256,512]{1,2,0:T(8,128)S(1)}, f32[2,256,512]{1,2,0:T(8,128)S(1)}, u32[]{:S(2)}, u32[]{:S(2)}) collective-permute-start(f32[2,256,512]{1,2,0:T(8,128)S(1)} %bitcast_add_fusion), channel_id=1, source_target_pairs={{0,4},{4,8},{1,5},{5,9},{2,6},{6,10},{3,7},{7,11},{16,20},{20,24},... | collective-permute-start | bytes 3145736 | tf_op jit(solution)/shard_map/ppermute | solution.py:232
  41.0 0.7 collective-permute-start.3
  41.7 9.0 %shard_map.60 = f32[2,512,256]{2,1,0:T(8,128)S(1)} custom-call(s32[1]{0:T(128)} %bitcast.6.index_ref, bf16[2,1024,4096]{2,1,0:T(8,128)(2,1)} %bitcast.47, bf16[2,4096,512]{2,1,0:T(8,128)(2,1)} %bitcast.51), custom_call_target="tpu_custom_call" | custom-call | flops 4294967296 | bytes 13631488 | tf_op jit(solution)/shard_map/pallas_call | solution.py:155
  50.8 9.1 %shard_map.59 = f32[2,512,256]{2,1,0:T(8,128)S(1)} custom-call(s32[1]{0:T(128)} %bitcast.1.index_ref, bf16[2,1024,4096]{2,1,0:T(8,128)(2,1)} %bitcast.48, bf16[2,4096,512]{2,1,0:T(8,128)(2,1)} %bitcast.52), custom_call_target="tpu_custom_call" | custom-call | flops 4294967296 | bytes 13631488 | tf_op jit(solution)/shard_map/pallas_call | solution.py:155
  59.9 2.6 %collective-permute-done.1 = f32[2,256,512]{1,2,0:T(8,128)S(1)} collective-permute-done((f32[2,256,512]{1,2,0:T(8,128)S(1)}, f32[2,256,512]{1,2,0:T(8,128)S(1)}, u32[]{:S(2)}, u32[]{:S(2)}) %collective-permute-start.1) | collective-permute-done | bytes 1048608 | tf_op jit(solution)/shard_map/ppermute | solution.py:232
  62.6 4.5 %collective-permute-start.2 = (f32[2,256,512]{1,2,0:T(8,128)S(1)}, f32[2,256,512]{1,2,0:T(8,128)S(1)}, u32[]{:S(2)}, u32[]{:S(2)}) collective-permute-start(f32[2,256,512]{1,2,0:T(8,128)S(1)} %bitcast_add_fusion.1), channel_id=1, source_target_pairs={{0,4},{4,8},{8,12},{1,5},{5,9},{9,13},{2,6},{6,10},{10,14},{3,7},{... | collective-permute-start | bytes 3145736 | tf_op jit(solution)/shard_map/ppermute | solution.py:232
  67.2 1.3 %collective-permute-start.4 = (f32[2,256,512]{1,2,0:T(8,128)S(1)}, f32[2,256,512]{1,2,0:T(8,128)S(1)}, u32[]{:S(2)}, u32[]{:S(2)}) collective-permute-start(f32[2,256,512]{1,2,0:T(8,128)S(1)} %bitcast_add_fusion.2), channel_id=1, source_target_pairs={{4,0},{8,4},{12,8},{5,1},{9,5},{13,9},{6,2},{10,6},{14,10},{7,3},{... | collective-permute-start | bytes 3145736 | tf_op jit(solution)/shard_map/ppermute | solution.py:233
  68.5 0.6 dynamic_slice.6
  70.4 17.3 %collective-permute-done.2 = f32[2,256,512]{1,2,0:T(8,128)S(1)} collective-permute-done((f32[2,256,512]{1,2,0:T(8,128)S(1)}, f32[2,256,512]{1,2,0:T(8,128)S(1)}, u32[]{:S(2)}, u32[]{:S(2)}) %collective-permute-start.2) | collective-permute-done | bytes 1048608 | tf_op jit(solution)/shard_map/ppermute | solution.py:232
  87.7 4.3 %collective-permute-done.4 = f32[2,256,512]{1,2,0:T(8,128)S(1)} collective-permute-done((f32[2,256,512]{1,2,0:T(8,128)S(1)}, f32[2,256,512]{1,2,0:T(8,128)S(1)}, u32[]{:S(2)}, u32[]{:S(2)}) %collective-permute-start.4) | collective-permute-done | bytes 1048608 | tf_op jit(solution)/shard_map/ppermute | solution.py:233
  92.0 0.3 fusion.2
  92.7 0.2 subtract_reduce_fusion.1
  93.0 2.3 %collective-permute-done.5 = f32[2,256,8,64]{1,3,2,0:T(8,128)S(1)} collective-permute-done((f32[2,256,8,64]{1,3,2,0:T(8,128)S(1)}, f32[2,256,8,64]{1,3,2,0:T(8,128)S(1)}, u32[]{:S(2)}, u32[]{:S(2)}) %collective-permute-start.5) | collective-permute-done | bytes 1048608 | tf_op jit(solution)/shard_map/ppermute | solution.py:16
  95.3 0.2 broadcast_select_fusion.1
  95.5 0.3 subtract_reduce_fusion
  95.9 1.6 %collective-permute-start.6 = (f32[7,256,1]{1,2,0:T(1,128)S(1)}, f32[7,256,1]{1,2,0:T(1,128)S(1)}, u32[]{:S(2)}, u32[]{:S(2)}) collective-permute-start(f32[7,256,1]{1,2,0:T(1,128)S(1)} %broadcast_select_fusion.4), channel_id=1, source_target_pairs={{0,2},{2,0},{1,3},{3,1},{4,6},{6,4},{5,7},{7,5},{8,10},{10,8},{9,1... | collective-permute-start | bytes 21512 | tf_op jit(solution)/shard_map/ppermute | solution.py:26
  97.4 2.1 %collective-permute-done.6 = f32[7,256,1]{1,2,0:T(1,128)S(1)} collective-permute-done((f32[7,256,1]{1,2,0:T(1,128)S(1)}, f32[7,256,1]{1,2,0:T(1,128)S(1)}, u32[]{:S(2)}, u32[]{:S(2)}) %collective-permute-start.6) | collective-permute-done | bytes 7200 | tf_op jit(solution)/shard_map/ppermute | solution.py:26
  99.6 0.6 slice_divide_fusion
  100.3 0.6 maximum_bitcast_fusion
  (24 shorter events, 0.9 us)
Async XLA Ops:
  0.6 13.5 %copy-start = (s32[4,4]{1,0:T(4,128)S(1)}, s32[4,4]{1,0:T(4,128)}, u32[]{:S(2)}) copy-start(s32[4,4]{1,0:T(4,128)} %constant.52.clone) | copy-start | bytes 196
  9.0 27.4 %collective-permute-start = (f32[2,256,512]{1,2,0:T(8,128)S(1)}, f32[2,256,512]{1,2,0:T(8,128)S(1)}, u32[]{:S(2)}, u32[]{:S(2)}) collective-permute-start(f32[2,256,512]{1,2,0:T(8,128)S(1)} %bitcast.44), channel_id=1, source_target_pairs={{0,4},{12,8},{1,5},{13,9},{2,6},{14,10},{3,7},{15,11},{16,20},{28,... | collective-permute-start | bytes 3145736 | tf_op jit(solution)/shard_map/ppermute | solution.py:230
  36.6 25.9 %collective-permute-start.1 = (f32[2,256,512]{1,2,0:T(8,128)S(1)}, f32[2,256,512]{1,2,0:T(8,128)S(1)}, u32[]{:S(2)}, u32[]{:S(2)}) collective-permute-start(f32[2,256,512]{1,2,0:T(8,128)S(1)} %bitcast_add_fusion), channel_id=1, source_target_pairs={{0,4},{4,8},{1,5},{5,9},{2,6},{6,10},{3,7},{7,11},{16,20},{20,24},... | collective-permute-start | bytes 3145736 | tf_op jit(solution)/shard_map/ppermute | solution.py:232
  41.0 26.1 %collective-permute-start.3 = (f32[2,256,512]{1,2,0:T(8,128)S(1)}, f32[2,256,512]{1,2,0:T(8,128)S(1)}, u32[]{:S(2)}, u32[]{:S(2)}) collective-permute-start(f32[2,256,512]{1,2,0:T(8,128)S(1)} %bitcast_add_fusion), channel_id=1, source_target_pairs={{8,4},{12,8},{9,5},{13,9},{10,6},{14,10},{11,7},{15,11},{24,20},{2... | collective-permute-start | bytes 3145736 | tf_op jit(solution)/shard_map/ppermute | solution.py:233
  50.8 17.8 %copy-start.1 = (s32[4]{0:T(128)S(1)}, s32[4]{0:T(128)}, u32[]{:S(2)}) copy-start(s32[4]{0:T(128)} %constant.53.clone) | copy-start | bytes 52
  62.6 25.1 %collective-permute-start.2 = (f32[2,256,512]{1,2,0:T(8,128)S(1)}, f32[2,256,512]{1,2,0:T(8,128)S(1)}, u32[]{:S(2)}, u32[]{:S(2)}) collective-permute-start(f32[2,256,512]{1,2,0:T(8,128)S(1)} %bitcast_add_fusion.1), channel_id=1, source_target_pairs={{0,4},{4,8},{8,12},{1,5},{5,9},{9,13},{2,6},{6,10},{10,14},{3,7},{... | collective-permute-start | bytes 3145736 | tf_op jit(solution)/shard_map/ppermute | solution.py:232
  67.2 24.8 %collective-permute-start.4 = (f32[2,256,512]{1,2,0:T(8,128)S(1)}, f32[2,256,512]{1,2,0:T(8,128)S(1)}, u32[]{:S(2)}, u32[]{:S(2)}) collective-permute-start(f32[2,256,512]{1,2,0:T(8,128)S(1)} %bitcast_add_fusion.2), channel_id=1, source_target_pairs={{4,0},{8,4},{12,8},{5,1},{9,5},{13,9},{6,2},{10,6},{14,10},{7,3},{... | collective-permute-start | bytes 3145736 | tf_op jit(solution)/shard_map/ppermute | solution.py:233
  92.6 2.7 %collective-permute-start.5 = (f32[2,256,8,64]{1,3,2,0:T(8,128)S(1)}, f32[2,256,8,64]{1,3,2,0:T(8,128)S(1)}, u32[]{:S(2)}, u32[]{:S(2)}) collective-permute-start(f32[2,256,8,64]{1,3,2,0:T(8,128)S(1)} %pad_maximum_fusion), channel_id=1, source_target_pairs={{0,1},{1,0},{2,3},{3,2},{4,5},{5,4},{6,7},{7,6},{8,9},{9,8},{10,11... | collective-permute-start | bytes 3145736 | tf_op jit(solution)/shard_map/ppermute | solution.py:16
  95.9 3.7 %collective-permute-start.6 = (f32[7,256,1]{1,2,0:T(1,128)S(1)}, f32[7,256,1]{1,2,0:T(1,128)S(1)}, u32[]{:S(2)}, u32[]{:S(2)}) collective-permute-start(f32[7,256,1]{1,2,0:T(1,128)S(1)} %broadcast_select_fusion.4), channel_id=1, source_target_pairs={{0,2},{2,0},{1,3},{3,1},{4,6},{6,4},{5,7},{7,5},{8,10},{10,8},{9,1... | collective-permute-start | bytes 21512 | tf_op jit(solution)/shard_map/ppermute | solution.py:26

commit v12 on v11

--- a/solution.py
+++ b/solution.py
@@ -216,6 +216,7 @@
         made.append(jnp.swapaxes(block_partial(signal, weights, index, local), 1, 2))
     got_right = None
     got_left = None
+    shared = False
     for step in range(1, n_elem):
         calls = {way: k for k, (s, way) in enumerate(serves) if s == step}
         to_right = made[calls.get("right", calls.get("both"))]
@@ -228,14 +229,18 @@
         merged = pairs_right + pairs_left
         if "both" in calls and got_right is None and len({t for _, t in merged}) == len(merged):
             got_right = got_left = lax.ppermute(to_right, "elem", merged)
+            shared = True
         else:
             got_right = lax.ppermute(to_right, "elem", pairs_right)
             got_left = lax.ppermute(to_left, "elem", pairs_left)
+            shared = False
     own_at = jnp.asarray([own_call[c] for c in range(n_elem)], jnp.int32)[me]
     used = sorted(set(own_call.values()))
     own = made[used[0]]
     for k in used[1:]:
         own = jnp.where(own_at == k, made[k], own)
+    if shared:
+        return own + got_right
     return own + got_right + got_left
 
 

time: 101 us -> 101 us (level)
  no operation moved by 1% of the time
where the time goes in v12:
time: 101 us
  waiting for transfers between devices  41.2 us (41%)
  Pallas kernels  35.5 us (35%)
  starting transfers between devices  17.6 us (17%)
  other arithmetic  3 us (3%)
  between operations  2.22 us (2%)
  local copies, waits for them, and re-layouts  1.35 us (1%)
    pallas_call x4, Pallas kernels, block_partial(): pl.pallas_call(block_kernel, out_shape=jax.ShapeDtypeStruct((2, samples,...  35.5 us
    ppermute x2, waiting for transfers between devices, line_scatter(): got_right = lax.ppermute(to_right, 'elem', pairs_right)  19.9 us
    ppermute x1, waiting for transfers between devices, line_scatter(): got_right = got_left = lax.ppermute(to_right, 'elem', merged)  12.6 us
    ppermute x2, starting transfers between devices, line_scatter(): got_right = lax.ppermute(to_right, 'elem', pairs_right)  8.9 us
    ppermute x1, starting transfers between devices, line_scatter(): got_right = got_left = lax.ppermute(to_right, 'elem', merged)  5.02 us
    ppermute x2, waiting for transfers between devices, line_scatter(): got_left = lax.ppermute(to_left, 'elem', pairs_left)  4.34 us
    ppermute x1, waiting for transfers between devices, swapped(): return lax.ppermute(value, axis, pairs)  2.26 us
    ppermute x1, waiting for transfers between devices, with_halo(): got = lax.ppermute(sent, axis, [(0, 1), (1, 0)])  2.15 us
  transfers between devices with their start and end apart: 7, of which 6 were waited for; matrix products, arithmetic and copies ran while one was open for 2% of the time, Pallas kernels for 27%

profile of v12, /device:TPU:0, one launch (start us, length us, event | category | flops | bytes accessed | tf_op | source)
XLA Modules:
  0.0 100.9 jit_solution(16487698475649515003)
XLA Ops:
  0.7 8.4 %shard_map.61 = f32[2,512,256]{2,1,0:T(8,128)S(1)} custom-call(s32[1]{0:T(128)} %bitcast.8.index_ref, bf16[2,1024,4096]{2,1,0:T(8,128)(2,1)} %bitcast.45, bf16[2,4096,512]{2,1,0:T(8,128)(2,1)} %bitcast.49), custom_call_target="tpu_custom_call" | custom-call | flops 4294967296 | bytes 13631488 | tf_op jit(solution)/shard_map/pallas_call | solution.py:155
  9.0 5.0 %collective-permute-start = (f32[2,256,512]{1,2,0:T(8,128)S(1)}, f32[2,256,512]{1,2,0:T(8,128)S(1)}, u32[]{:S(2)}, u32[]{:S(2)}) collective-permute-start(f32[2,256,512]{1,2,0:T(8,128)S(1)} %bitcast.44), channel_id=1, source_target_pairs={{0,4},{12,8},{1,5},{13,9},{2,6},{14,10},{3,7},{15,11},{16,20},{28,... | collective-permute-start | bytes 3145736 | tf_op jit(solution)/shard_map/ppermute | solution.py:231
  14.2 0.6 fusion.11
  14.8 9.0 %shard_map.62 = f32[2,512,256]{2,1,0:T(8,128)S(1)} custom-call(s32[1]{0:T(128)} %bitcast.10.index_ref, bf16[2,1024,4096]{2,1,0:T(8,128)(2,1)} %bitcast.46, bf16[2,4096,512]{2,1,0:T(8,128)(2,1)} %bitcast.50), custom_call_target="tpu_custom_call" | custom-call | flops 4294967296 | bytes 13631488 | tf_op jit(solution)/shard_map/pallas_call | solution.py:155
  23.8 12.6 %collective-permute-done = f32[2,256,512]{1,2,0:T(8,128)S(1)} collective-permute-done((f32[2,256,512]{1,2,0:T(8,128)S(1)}, f32[2,256,512]{1,2,0:T(8,128)S(1)}, u32[]{:S(2)}, u32[]{:S(2)}) %collective-permute-start) | collective-permute-done | bytes 1048608 | tf_op jit(solution)/shard_map/ppermute | solution.py:231
  36.6 4.5 %collective-permute-start.1 = (f32[2,256,512]{1,2,0:T(8,128)S(1)}, f32[2,256,512]{1,2,0:T(8,128)S(1)}, u32[]{:S(2)}, u32[]{:S(2)}) collective-permute-start(f32[2,256,512]{1,2,0:T(8,128)S(1)} %bitcast_add_fusion), channel_id=1, source_target_pairs={{0,4},{4,8},{1,5},{5,9},{2,6},{6,10},{3,7},{7,11},{16,20},{20,24},... | collective-permute-start | bytes 3145736 | tf_op jit(solution)/shard_map/ppermute | solution.py:234
  41.0 0.7 collective-permute-start.3
  41.7 9.0 %shard_map.60 = f32[2,512,256]{2,1,0:T(8,128)S(1)} custom-call(s32[1]{0:T(128)} %bitcast.6.index_ref, bf16[2,1024,4096]{2,1,0:T(8,128)(2,1)} %bitcast.47, bf16[2,4096,512]{2,1,0:T(8,128)(2,1)} %bitcast.51), custom_call_target="tpu_custom_call" | custom-call | flops 4294967296 | bytes 13631488 | tf_op jit(solution)/shard_map/pallas_call | solution.py:155
  50.8 9.1 %shard_map.59 = f32[2,512,256]{2,1,0:T(8,128)S(1)} custom-call(s32[1]{0:T(128)} %bitcast.1.index_ref, bf16[2,1024,4096]{2,1,0:T(8,128)(2,1)} %bitcast.48, bf16[2,4096,512]{2,1,0:T(8,128)(2,1)} %bitcast.52), custom_call_target="tpu_custom_call" | custom-call | flops 4294967296 | bytes 13631488 | tf_op jit(solution)/shard_map/pallas_call | solution.py:155
  59.9 2.6 %collective-permute-done.1 = f32[2,256,512]{1,2,0:T(8,128)S(1)} collective-permute-done((f32[2,256,512]{1,2,0:T(8,128)S(1)}, f32[2,256,512]{1,2,0:T(8,128)S(1)}, u32[]{:S(2)}, u32[]{:S(2)}) %collective-permute-start.1) | collective-permute-done | bytes 1048608 | tf_op jit(solution)/shard_map/ppermute | solution.py:234
  62.6 4.5 %collective-permute-start.2 = (f32[2,256,512]{1,2,0:T(8,128)S(1)}, f32[2,256,512]{1,2,0:T(8,128)S(1)}, u32[]{:S(2)}, u32[]{:S(2)}) collective-permute-start(f32[2,256,512]{1,2,0:T(8,128)S(1)} %bitcast_add_fusion.1), channel_id=1, source_target_pairs={{0,4},{4,8},{8,12},{1,5},{5,9},{9,13},{2,6},{6,10},{10,14},{3,7},{... | collective-permute-start | bytes 3145736 | tf_op jit(solution)/shard_map/ppermute | solution.py:234
  67.2 1.3 %collective-permute-start.4 = (f32[2,256,512]{1,2,0:T(8,128)S(1)}, f32[2,256,512]{1,2,0:T(8,128)S(1)}, u32[]{:S(2)}, u32[]{:S(2)}) collective-permute-start(f32[2,256,512]{1,2,0:T(8,128)S(1)} %bitcast_add_fusion.2), channel_id=1, source_target_pairs={{4,0},{8,4},{12,8},{5,1},{9,5},{13,9},{6,2},{10,6},{14,10},{7,3},{... | collective-permute-start | bytes 3145736 | tf_op jit(solution)/shard_map/ppermute | solution.py:235
  68.5 0.6 dynamic_slice.6
  70.4 17.3 %collective-permute-done.2 = f32[2,256,512]{1,2,0:T(8,128)S(1)} collective-permute-done((f32[2,256,512]{1,2,0:T(8,128)S(1)}, f32[2,256,512]{1,2,0:T(8,128)S(1)}, u32[]{:S(2)}, u32[]{:S(2)}) %collective-permute-start.2) | collective-permute-done | bytes 1048608 | tf_op jit(solution)/shard_map/ppermute | solution.py:234
  87.7 4.3 %collective-permute-done.4 = f32[2,256,512]{1,2,0:T(8,128)S(1)} collective-permute-done((f32[2,256,512]{1,2,0:T(8,128)S(1)}, f32[2,256,512]{1,2,0:T(8,128)S(1)}, u32[]{:S(2)}, u32[]{:S(2)}) %collective-permute-start.4) | collective-permute-done | bytes 1048608 | tf_op jit(solution)/shard_map/ppermute | solution.py:235
  92.0 0.3 fusion.2
  92.7 0.2 subtract_reduce_fusion.1
  93.0 2.3 %collective-permute-done.5 = f32[2,256,8,64]{1,3,2,0:T(8,128)S(1)} collective-permute-done((f32[2,256,8,64]{1,3,2,0:T(8,128)S(1)}, f32[2,256,8,64]{1,3,2,0:T(8,128)S(1)}, u32[]{:S(2)}, u32[]{:S(2)}) %collective-permute-start.5) | collective-permute-done | bytes 1048608 | tf_op jit(solution)/shard_map/ppermute | solution.py:16
  95.3 0.2 broadcast_select_fusion.1
  95.5 0.3 subtract_reduce_fusion
  95.9 1.6 %collective-permute-start.6 = (f32[7,256,1]{1,2,0:T(1,128)S(1)}, f32[7,256,1]{1,2,0:T(1,128)S(1)}, u32[]{:S(2)}, u32[]{:S(2)}) collective-permute-start(f32[7,256,1]{1,2,0:T(1,128)S(1)} %broadcast_select_fusion.4), channel_id=1, source_target_pairs={{0,2},{2,0},{1,3},{3,1},{4,6},{6,4},{5,7},{7,5},{8,10},{10,8},{9,1... | collective-permute-start | bytes 21512 | tf_op jit(solution)/shard_map/ppermute | solution.py:26
  97.4 2.1 %collective-permute-done.6 = f32[7,256,1]{1,2,0:T(1,128)S(1)} collective-permute-done((f32[7,256,1]{1,2,0:T(1,128)S(1)}, f32[7,256,1]{1,2,0:T(1,128)S(1)}, u32[]{:S(2)}, u32[]{:S(2)}) %collective-permute-start.6) | collective-permute-done | bytes 7200 | tf_op jit(solution)/shard_map/ppermute | solution.py:26
  99.6 0.6 slice_divide_fusion
  100.3 0.6 maximum_bitcast_fusion
  (24 shorter events, 0.9 us)
Async XLA Ops:
  0.6 13.5 %copy-start = (s32[4,4]{1,0:T(4,128)S(1)}, s32[4,4]{1,0:T(4,128)}, u32[]{:S(2)}) copy-start(s32[4,4]{1,0:T(4,128)} %constant.52.clone) | copy-start | bytes 196
  9.0 27.4 %collective-permute-start = (f32[2,256,512]{1,2,0:T(8,128)S(1)}, f32[2,256,512]{1,2,0:T(8,128)S(1)}, u32[]{:S(2)}, u32[]{:S(2)}) collective-permute-start(f32[2,256,512]{1,2,0:T(8,128)S(1)} %bitcast.44), channel_id=1, source_target_pairs={{0,4},{12,8},{1,5},{13,9},{2,6},{14,10},{3,7},{15,11},{16,20},{28,... | collective-permute-start | bytes 3145736 | tf_op jit(solution)/shard_map/ppermute | solution.py:231
  36.6 25.9 %collective-permute-start.1 = (f32[2,256,512]{1,2,0:T(8,128)S(1)}, f32[2,256,512]{1,2,0:T(8,128)S(1)}, u32[]{:S(2)}, u32[]{:S(2)}) collective-permute-start(f32[2,256,512]{1,2,0:T(8,128)S(1)} %bitcast_add_fusion), channel_id=1, source_target_pairs={{0,4},{4,8},{1,5},{5,9},{2,6},{6,10},{3,7},{7,11},{16,20},{20,24},... | collective-permute-start | bytes 3145736 | tf_op jit(solution)/shard_map/ppermute | solution.py:234
  41.0 26.1 %collective-permute-start.3 = (f32[2,256,512]{1,2,0:T(8,128)S(1)}, f32[2,256,512]{1,2,0:T(8,128)S(1)}, u32[]{:S(2)}, u32[]{:S(2)}) collective-permute-start(f32[2,256,512]{1,2,0:T(8,128)S(1)} %bitcast_add_fusion), channel_id=1, source_target_pairs={{8,4},{12,8},{9,5},{13,9},{10,6},{14,10},{11,7},{15,11},{24,20},{2... | collective-permute-start | bytes 3145736 | tf_op jit(solution)/shard_map/ppermute | solution.py:235
  50.8 17.8 %copy-start.1 = (s32[4]{0:T(128)S(1)}, s32[4]{0:T(128)}, u32[]{:S(2)}) copy-start(s32[4]{0:T(128)} %constant.53.clone) | copy-start | bytes 52
  62.6 25.1 %collective-permute-start.2 = (f32[2,256,512]{1,2,0:T(8,128)S(1)}, f32[2,256,512]{1,2,0:T(8,128)S(1)}, u32[]{:S(2)}, u32[]{:S(2)}) collective-permute-start(f32[2,256,512]{1,2,0:T(8,128)S(1)} %bitcast_add_fusion.1), channel_id=1, source_target_pairs={{0,4},{4,8},{8,12},{1,5},{5,9},{9,13},{2,6},{6,10},{10,14},{3,7},{... | collective-permute-start | bytes 3145736 | tf_op jit(solution)/shard_map/ppermute | solution.py:234
  67.2 24.8 %collective-permute-start.4 = (f32[2,256,512]{1,2,0:T(8,128)S(1)}, f32[2,256,512]{1,2,0:T(8,128)S(1)}, u32[]{:S(2)}, u32[]{:S(2)}) collective-permute-start(f32[2,256,512]{1,2,0:T(8,128)S(1)} %bitcast_add_fusion.2), channel_id=1, source_target_pairs={{4,0},{8,4},{12,8},{5,1},{9,5},{13,9},{6,2},{10,6},{14,10},{7,3},{... | collective-permute-start | bytes 3145736 | tf_op jit(solution)/shard_map/ppermute | solution.py:235
  92.6 2.7 %collective-permute-start.5 = (f32[2,256,8,64]{1,3,2,0:T(8,128)S(1)}, f32[2,256,8,64]{1,3,2,0:T(8,128)S(1)}, u32[]{:S(2)}, u32[]{:S(2)}) collective-permute-start(f32[2,256,8,64]{1,3,2,0:T(8,128)S(1)} %pad_maximum_fusion), channel_id=1, source_target_pairs={{0,1},{1,0},{2,3},{3,2},{4,5},{5,4},{6,7},{7,6},{8,9},{9,8},{10,11... | collective-permute-start | bytes 3145736 | tf_op jit(solution)/shard_map/ppermute | solution.py:16
  95.9 3.7 %collective-permute-start.6 = (f32[7,256,1]{1,2,0:T(1,128)S(1)}, f32[7,256,1]{1,2,0:T(1,128)S(1)}, u32[]{:S(2)}, u32[]{:S(2)}) collective-permute-start(f32[7,256,1]{1,2,0:T(1,128)S(1)} %broadcast_select_fusion.4), channel_id=1, source_target_pairs={{0,2},{2,0},{1,3},{3,1},{4,6},{6,4},{5,7},{7,5},{8,10},{10,8},{9,1... | collective-permute-start | bytes 21512 | tf_op jit(solution)/shard_map/ppermute | solution.py:26

commit v13 on v12

--- a/solution.py
+++ b/solution.py
@@ -8,6 +8,7 @@
 PULSES = 64
 BEAM_TILE = 512
 ELEM_TILE = 1024
+FIRST_TILE = 2048
 
 
 def swapped(value, axis, bit):
@@ -146,12 +147,12 @@
         o_ref[1] = acc_ref[1].T
 
 
-def block_partial(signal, weights, index, count):
+def block_partial(signal, weights, index, count, tile=ELEM_TILE):
     w = weights[:, 0]
     x = signal[:, 0]
     elems = w.shape[2]
     samples = x.shape[2]
-    tk = min(ELEM_TILE, elems)
+    tk = min(tile, elems)
     return pl.pallas_call(
         block_kernel,
         out_shape=jax.ShapeDtypeStruct((2, samples, count), jnp.float32),
@@ -213,7 +214,8 @@
             index = jnp.where(me == 0, n_elem - 1, jnp.where(me == n_elem - 1, 0, me)).astype(jnp.int32)
         else:
             index = later[k]
-        made.append(jnp.swapaxes(block_partial(signal, weights, index, local), 1, 2))
+        tile = FIRST_TILE if k == 0 else ELEM_TILE
+        made.append(jnp.swapaxes(block_partial(signal, weights, index, local, tile), 1, 2))
     got_right = None
     got_left = None
     shared = False

time: 101 us -> 101 us (level)
  no operation moved by 1% of the time
where the time goes in v13:
time: 101 us
  waiting for transfers between devices  41.2 us (41%)
  Pallas kernels  35.2 us (35%)
  starting transfers between devices  17.6 us (17%)
  other arithmetic  3 us (3%)
  between operations  2.22 us (2%)
  local copies, waits for them, and re-layouts  1.35 us (1%)
    pallas_call x4, Pallas kernels, block_partial(): pl.pallas_call(block_kernel, out_shape=jax.ShapeDtypeStruct((2, samples,...  35.2 us
    ppermute x2, waiting for transfers between devices, line_scatter(): got_right = lax.ppermute(to_right, 'elem', pairs_right)  19.9 us
    ppermute x1, waiting for transfers between devices, line_scatter(): got_right = got_left = lax.ppermute(to_right, 'elem', merged)  12.6 us
    ppermute x2, starting transfers between devices, line_scatter(): got_right = lax.ppermute(to_right, 'elem', pairs_right)  8.9 us
    ppermute x1, starting transfers between devices, line_scatter(): got_right = got_left = lax.ppermute(to_right, 'elem', merged)  5.02 us
    ppermute x2, waiting for transfers between devices, line_scatter(): got_left = lax.ppermute(to_left, 'elem', pairs_left)  4.34 us
    ppermute x1, waiting for transfers between devices, swapped(): return lax.ppermute(value, axis, pairs)  2.26 us
    ppermute x1, waiting for transfers between devices, with_halo(): got = lax.ppermute(sent, axis, [(0, 1), (1, 0)])  2.15 us
  transfers between devices with their start and end apart: 7, of which 6 were waited for; matrix products, arithmetic and copies ran while one was open for 2% of the time, Pallas kernels for 27%

profile of v13, /device:TPU:0, one launch (start us, length us, event | category | flops | bytes accessed | tf_op | source)
XLA Modules:
  0.0 100.5 jit_solution(12143496204394379685)
XLA Ops:
  0.7 8.0 %shard_map.61 = f32[2,512,256]{2,1,0:T(8,128)S(1)} custom-call(s32[1]{0:T(128)} %bitcast.8.index_ref, bf16[2,1024,4096]{2,1,0:T(8,128)(2,1)} %bitcast.45, bf16[2,4096,512]{2,1,0:T(8,128)(2,1)} %bitcast.49), custom_call_target="tpu_custom_call" | custom-call | flops 4294967296 | bytes 13631488 | tf_op jit(solution)/shard_map/pallas_call | solution.py:156
  8.7 5.0 %collective-permute-start = (f32[2,256,512]{1,2,0:T(8,128)S(1)}, f32[2,256,512]{1,2,0:T(8,128)S(1)}, u32[]{:S(2)}, u32[]{:S(2)}) collective-permute-start(f32[2,256,512]{1,2,0:T(8,128)S(1)} %bitcast.44), channel_id=1, source_target_pairs={{0,4},{12,8},{1,5},{13,9},{2,6},{14,10},{3,7},{15,11},{16,20},{28,... | collective-permute-start | bytes 3145736 | tf_op jit(solution)/shard_map/ppermute | solution.py:233
  13.8 0.6 fusion.11
  14.4 9.0 %shard_map.62 = f32[2,512,256]{2,1,0:T(8,128)S(1)} custom-call(s32[1]{0:T(128)} %bitcast.10.index_ref, bf16[2,1024,4096]{2,1,0:T(8,128)(2,1)} %bitcast.46, bf16[2,4096,512]{2,1,0:T(8,128)(2,1)} %bitcast.50), custom_call_target="tpu_custom_call" | custom-call | flops 4294967296 | bytes 13631488 | tf_op jit(solution)/shard_map/pallas_call | solution.py:156
  23.4 12.6 %collective-permute-done = f32[2,256,512]{1,2,0:T(8,128)S(1)} collective-permute-done((f32[2,256,512]{1,2,0:T(8,128)S(1)}, f32[2,256,512]{1,2,0:T(8,128)S(1)}, u32[]{:S(2)}, u32[]{:S(2)}) %collective-permute-start) | collective-permute-done | bytes 1048608 | tf_op jit(solution)/shard_map/ppermute | solution.py:233
  36.2 4.5 %collective-permute-start.1 = (f32[2,256,512]{1,2,0:T(8,128)S(1)}, f32[2,256,512]{1,2,0:T(8,128)S(1)}, u32[]{:S(2)}, u32[]{:S(2)}) collective-permute-start(f32[2,256,512]{1,2,0:T(8,128)S(1)} %bitcast_add_fusion), channel_id=1, source_target_pairs={{0,4},{4,8},{1,5},{5,9},{2,6},{6,10},{3,7},{7,11},{16,20},{20,24},... | collective-permute-start | bytes 3145736 | tf_op jit(solution)/shard_map/ppermute | solution.py:236
  40.7 0.7 collective-permute-start.3
  41.4 9.0 %shard_map.60 = f32[2,512,256]{2,1,0:T(8,128)S(1)} custom-call(s32[1]{0:T(128)} %bitcast.6.index_ref, bf16[2,1024,4096]{2,1,0:T(8,128)(2,1)} %bitcast.47, bf16[2,4096,512]{2,1,0:T(8,128)(2,1)} %bitcast.51), custom_call_target="tpu_custom_call" | custom-call | flops 4294967296 | bytes 13631488 | tf_op jit(solution)/shard_map/pallas_call | solution.py:156
  50.4 9.1 %shard_map.59 = f32[2,512,256]{2,1,0:T(8,128)S(1)} custom-call(s32[1]{0:T(128)} %bitcast.1.index_ref, bf16[2,1024,4096]{2,1,0:T(8,128)(2,1)} %bitcast.48, bf16[2,4096,512]{2,1,0:T(8,128)(2,1)} %bitcast.52), custom_call_target="tpu_custom_call" | custom-call | flops 4294967296 | bytes 13631488 | tf_op jit(solution)/shard_map/pallas_call | solution.py:156
  59.5 2.6 %collective-permute-done.1 = f32[2,256,512]{1,2,0:T(8,128)S(1)} collective-permute-done((f32[2,256,512]{1,2,0:T(8,128)S(1)}, f32[2,256,512]{1,2,0:T(8,128)S(1)}, u32[]{:S(2)}, u32[]{:S(2)}) %collective-permute-start.1) | collective-permute-done | bytes 1048608 | tf_op jit(solution)/shard_map/ppermute | solution.py:236
  62.3 4.5 %collective-permute-start.2 = (f32[2,256,512]{1,2,0:T(8,128)S(1)}, f32[2,256,512]{1,2,0:T(8,128)S(1)}, u32[]{:S(2)}, u32[]{:S(2)}) collective-permute-start(f32[2,256,512]{1,2,0:T(8,128)S(1)} %bitcast_add_fusion.1), channel_id=1, source_target_pairs={{0,4},{4,8},{8,12},{1,5},{5,9},{9,13},{2,6},{6,10},{10,14},{3,7},{... | collective-permute-start | bytes 3145736 | tf_op jit(solution)/shard_map/ppermute | solution.py:236
  66.9 1.3 %collective-permute-start.4 = (f32[2,256,512]{1,2,0:T(8,128)S(1)}, f32[2,256,512]{1,2,0:T(8,128)S(1)}, u32[]{:S(2)}, u32[]{:S(2)}) collective-permute-start(f32[2,256,512]{1,2,0:T(8,128)S(1)} %bitcast_add_fusion.2), channel_id=1, source_target_pairs={{4,0},{8,4},{12,8},{5,1},{9,5},{13,9},{6,2},{10,6},{14,10},{7,3},{... | collective-permute-start | bytes 3145736 | tf_op jit(solution)/shard_map/ppermute | solution.py:237
  68.2 0.6 dynamic_slice.6
  70.1 17.3 %collective-permute-done.2 = f32[2,256,512]{1,2,0:T(8,128)S(1)} collective-permute-done((f32[2,256,512]{1,2,0:T(8,128)S(1)}, f32[2,256,512]{1,2,0:T(8,128)S(1)}, u32[]{:S(2)}, u32[]{:S(2)}) %collective-permute-start.2) | collective-permute-done | bytes 1048608 | tf_op jit(solution)/shard_map/ppermute | solution.py:236
  87.3 4.3 %collective-permute-done.4 = f32[2,256,512]{1,2,0:T(8,128)S(1)} collective-permute-done((f32[2,256,512]{1,2,0:T(8,128)S(1)}, f32[2,256,512]{1,2,0:T(8,128)S(1)}, u32[]{:S(2)}, u32[]{:S(2)}) %collective-permute-start.4) | collective-permute-done | bytes 1048608 | tf_op jit(solution)/shard_map/ppermute | solution.py:237
  91.7 0.3 fusion.2
  92.4 0.2 subtract_reduce_fusion.1
  92.7 2.3 %collective-permute-done.5 = f32[2,256,8,64]{1,3,2,0:T(8,128)S(1)} collective-permute-done((f32[2,256,8,64]{1,3,2,0:T(8,128)S(1)}, f32[2,256,8,64]{1,3,2,0:T(8,128)S(1)}, u32[]{:S(2)}, u32[]{:S(2)}) %collective-permute-start.5) | collective-permute-done | bytes 1048608 | tf_op jit(solution)/shard_map/ppermute | solution.py:17
  94.9 0.2 broadcast_select_fusion.1
  95.1 0.3 subtract_reduce_fusion
  95.5 1.6 %collective-permute-start.6 = (f32[7,256,1]{1,2,0:T(1,128)S(1)}, f32[7,256,1]{1,2,0:T(1,128)S(1)}, u32[]{:S(2)}, u32[]{:S(2)}) collective-permute-start(f32[7,256,1]{1,2,0:T(1,128)S(1)} %broadcast_select_fusion.4), channel_id=1, source_target_pairs={{0,2},{2,0},{1,3},{3,1},{4,6},{6,4},{5,7},{7,5},{8,10},{10,8},{9,1... | collective-permute-start | bytes 21512 | tf_op jit(solution)/shard_map/ppermute | solution.py:27
  97.1 2.1 %collective-permute-done.6 = f32[7,256,1]{1,2,0:T(1,128)S(1)} collective-permute-done((f32[7,256,1]{1,2,0:T(1,128)S(1)}, f32[7,256,1]{1,2,0:T(1,128)S(1)}, u32[]{:S(2)}, u32[]{:S(2)}) %collective-permute-start.6) | collective-permute-done | bytes 7200 | tf_op jit(solution)/shard_map/ppermute | solution.py:27
  99.3 0.6 slice_divide_fusion
  99.9 0.6 maximum_bitcast_fusion
  (24 shorter events, 0.9 us)
Async XLA Ops:
  0.6 13.1 %copy-start = (s32[4,4]{1,0:T(4,128)S(1)}, s32[4,4]{1,0:T(4,128)}, u32[]{:S(2)}) copy-start(s32[4,4]{1,0:T(4,128)} %constant.52.clone) | copy-start | bytes 196
  8.7 27.4 %collective-permute-start = (f32[2,256,512]{1,2,0:T(8,128)S(1)}, f32[2,256,512]{1,2,0:T(8,128)S(1)}, u32[]{:S(2)}, u32[]{:S(2)}) collective-permute-start(f32[2,256,512]{1,2,0:T(8,128)S(1)} %bitcast.44), channel_id=1, source_target_pairs={{0,4},{12,8},{1,5},{13,9},{2,6},{14,10},{3,7},{15,11},{16,20},{28,... | collective-permute-start | bytes 3145736 | tf_op jit(solution)/shard_map/ppermute | solution.py:233
  36.2 25.9 %collective-permute-start.1 = (f32[2,256,512]{1,2,0:T(8,128)S(1)}, f32[2,256,512]{1,2,0:T(8,128)S(1)}, u32[]{:S(2)}, u32[]{:S(2)}) collective-permute-start(f32[2,256,512]{1,2,0:T(8,128)S(1)} %bitcast_add_fusion), channel_id=1, source_target_pairs={{0,4},{4,8},{1,5},{5,9},{2,6},{6,10},{3,7},{7,11},{16,20},{20,24},... | collective-permute-start | bytes 3145736 | tf_op jit(solution)/shard_map/ppermute | solution.py:236
  40.7 26.1 %collective-permute-start.3 = (f32[2,256,512]{1,2,0:T(8,128)S(1)}, f32[2,256,512]{1,2,0:T(8,128)S(1)}, u32[]{:S(2)}, u32[]{:S(2)}) collective-permute-start(f32[2,256,512]{1,2,0:T(8,128)S(1)} %bitcast_add_fusion), channel_id=1, source_target_pairs={{8,4},{12,8},{9,5},{13,9},{10,6},{14,10},{11,7},{15,11},{24,20},{2... | collective-permute-start | bytes 3145736 | tf_op jit(solution)/shard_map/ppermute | solution.py:237
  50.4 17.8 %copy-start.1 = (s32[4]{0:T(128)S(1)}, s32[4]{0:T(128)}, u32[]{:S(2)}) copy-start(s32[4]{0:T(128)} %constant.53.clone) | copy-start | bytes 52
  62.3 25.1 %collective-permute-start.2 = (f32[2,256,512]{1,2,0:T(8,128)S(1)}, f32[2,256,512]{1,2,0:T(8,128)S(1)}, u32[]{:S(2)}, u32[]{:S(2)}) collective-permute-start(f32[2,256,512]{1,2,0:T(8,128)S(1)} %bitcast_add_fusion.1), channel_id=1, source_target_pairs={{0,4},{4,8},{8,12},{1,5},{5,9},{9,13},{2,6},{6,10},{10,14},{3,7},{... | collective-permute-start | bytes 3145736 | tf_op jit(solution)/shard_map/ppermute | solution.py:236
  66.9 24.8 %collective-permute-start.4 = (f32[2,256,512]{1,2,0:T(8,128)S(1)}, f32[2,256,512]{1,2,0:T(8,128)S(1)}, u32[]{:S(2)}, u32[]{:S(2)}) collective-permute-start(f32[2,256,512]{1,2,0:T(8,128)S(1)} %bitcast_add_fusion.2), channel_id=1, source_target_pairs={{4,0},{8,4},{12,8},{5,1},{9,5},{13,9},{6,2},{10,6},{14,10},{7,3},{... | collective-permute-start | bytes 3145736 | tf_op jit(solution)/shard_map/ppermute | solution.py:237
  92.2 2.7 %collective-permute-start.5 = (f32[2,256,8,64]{1,3,2,0:T(8,128)S(1)}, f32[2,256,8,64]{1,3,2,0:T(8,128)S(1)}, u32[]{:S(2)}, u32[]{:S(2)}) collective-permute-start(f32[2,256,8,64]{1,3,2,0:T(8,128)S(1)} %pad_maximum_fusion), channel_id=1, source_target_pairs={{0,1},{1,0},{2,3},{3,2},{4,5},{5,4},{6,7},{7,6},{8,9},{9,8},{10,11... | collective-permute-start | bytes 3145736 | tf_op jit(solution)/shard_map/ppermute | solution.py:17
  95.5 3.7 %collective-permute-start.6 = (f32[7,256,1]{1,2,0:T(1,128)S(1)}, f32[7,256,1]{1,2,0:T(1,128)S(1)}, u32[]{:S(2)}, u32[]{:S(2)}) collective-permute-start(f32[7,256,1]{1,2,0:T(1,128)S(1)} %broadcast_select_fusion.4), channel_id=1, source_target_pairs={{0,2},{2,0},{1,3},{3,1},{4,6},{6,4},{5,7},{7,5},{8,10},{10,8},{9,1... | collective-permute-start | bytes 21512 | tf_op jit(solution)/shard_map/ppermute | solution.py:27

commit v14 on v13

--- a/solution.py
+++ b/solution.py
@@ -7,7 +7,7 @@
 
 PULSES = 64
 BEAM_TILE = 512
-ELEM_TILE = 1024
+ELEM_TILE = 2048
 FIRST_TILE = 2048
 
 

time: 101 us -> 101 us (level)
  Pallas kernels: 35.2 us -> 34.1 us
  waiting for transfers between devices: 41.2 us -> 42.3 us
    pallas_call x4, Pallas kernels: 35.2 us -> 34.1 us  [block_partial(): pl.pallas_call(block_kernel, out_shape=jax.ShapeDtypeStruct((2, samples,...]
  transfers between devices with their start and end apart: 7 -> 7, of which waited for: 6 -> 6; matrix products, arithmetic and copies ran while one was open for 2% -> 2% of each run, Pallas kernels for 27% -> 26%
where the time goes in v14:
time: 101 us
  waiting for transfers between devices  42.3 us (42%)
  Pallas kernels  34.1 us (34%)
  starting transfers between devices  17.6 us (17%)
  other arithmetic  3 us (3%)
  between operations  2.22 us (2%)
  local copies, waits for them, and re-layouts  1.35 us (1%)
    pallas_call x4, Pallas kernels, block_partial(): pl.pallas_call(block_kernel, out_shape=jax.ShapeDtypeStruct((2, samples,...  34.1 us
    ppermute x2, waiting for transfers between devices, line_scatter(): got_right = lax.ppermute(to_right, 'elem', pairs_right)  20.6 us
    ppermute x1, waiting for transfers between devices, line_scatter(): got_right = got_left = lax.ppermute(to_right, 'elem', merged)  13 us
    ppermute x2, starting transfers between devices, line_scatter(): got_right = lax.ppermute(to_right, 'elem', pairs_right)  8.9 us
    ppermute x1, starting transfers between devices, line_scatter(): got_right = got_left = lax.ppermute(to_right, 'elem', merged)  5.02 us
    ppermute x2, waiting for transfers between devices, line_scatter(): got_left = lax.ppermute(to_left, 'elem', pairs_left)  4.34 us
    ppermute x1, waiting for transfers between devices, swapped(): return lax.ppermute(value, axis, pairs)  2.26 us
    ppermute x1, waiting for transfers between devices, with_halo(): got = lax.ppermute(sent, axis, [(0, 1), (1, 0)])  2.15 us
  transfers between devices with their start and end apart: 7, of which 6 were waited for; matrix products, arithmetic and copies ran while one was open for 2% of the time, Pallas kernels for 26%

profile of v14, /device:TPU:0, one launch (start us, length us, event | category | flops | bytes accessed | tf_op | source)
XLA Modules:
  0.0 100.5 jit_solution(1270597082629117557)
XLA Ops:
  0.7 8.0 %shard_map.61 = f32[2,512,256]{2,1,0:T(8,128)S(1)} custom-call(s32[1]{0:T(128)} %bitcast.8.index_ref, bf16[2,1024,4096]{2,1,0:T(8,128)(2,1)} %bitcast.45, bf16[2,4096,512]{2,1,0:T(8,128)(2,1)} %bitcast.49), custom_call_target="tpu_custom_call" | custom-call | flops 4294967296 | bytes 13631488 | tf_op jit(solution)/shard_map/pallas_call | solution.py:156
  8.7 5.0 %collective-permute-start = (f32[2,256,512]{1,2,0:T(8,128)S(1)}, f32[2,256,512]{1,2,0:T(8,128)S(1)}, u32[]{:S(2)}, u32[]{:S(2)}) collective-permute-start(f32[2,256,512]{1,2,0:T(8,128)S(1)} %bitcast.44), channel_id=1, source_target_pairs={{0,4},{12,8},{1,5},{13,9},{2,6},{14,10},{3,7},{15,11},{16,20},{28,... | collective-permute-start | bytes 3145736 | tf_op jit(solution)/shard_map/ppermute | solution.py:233
  13.8 0.6 fusion.11
  14.4 8.7 %shard_map.62 = f32[2,512,256]{2,1,0:T(8,128)S(1)} custom-call(s32[1]{0:T(128)} %bitcast.10.index_ref, bf16[2,1024,4096]{2,1,0:T(8,128)(2,1)} %bitcast.46, bf16[2,4096,512]{2,1,0:T(8,128)(2,1)} %bitcast.50), custom_call_target="tpu_custom_call" | custom-call | flops 4294967296 | bytes 13631488 | tf_op jit(solution)/shard_map/pallas_call | solution.py:156
  23.1 13.0 %collective-permute-done = f32[2,256,512]{1,2,0:T(8,128)S(1)} collective-permute-done((f32[2,256,512]{1,2,0:T(8,128)S(1)}, f32[2,256,512]{1,2,0:T(8,128)S(1)}, u32[]{:S(2)}, u32[]{:S(2)}) %collective-permute-start) | collective-permute-done | bytes 1048608 | tf_op jit(solution)/shard_map/ppermute | solution.py:233
  36.2 4.5 %collective-permute-start.1 = (f32[2,256,512]{1,2,0:T(8,128)S(1)}, f32[2,256,512]{1,2,0:T(8,128)S(1)}, u32[]{:S(2)}, u32[]{:S(2)}) collective-permute-start(f32[2,256,512]{1,2,0:T(8,128)S(1)} %bitcast_add_fusion), channel_id=1, source_target_pairs={{0,4},{4,8},{1,5},{5,9},{2,6},{6,10},{3,7},{7,11},{16,20},{20,24},... | collective-permute-start | bytes 3145736 | tf_op jit(solution)/shard_map/ppermute | solution.py:236
  40.7 0.7 collective-permute-start.3
  41.4 8.7 %shard_map.60 = f32[2,512,256]{2,1,0:T(8,128)S(1)} custom-call(s32[1]{0:T(128)} %bitcast.6.index_ref, bf16[2,1024,4096]{2,1,0:T(8,128)(2,1)} %bitcast.47, bf16[2,4096,512]{2,1,0:T(8,128)(2,1)} %bitcast.51), custom_call_target="tpu_custom_call" | custom-call | flops 4294967296 | bytes 13631488 | tf_op jit(solution)/shard_map/pallas_call | solution.py:156
  50.1 8.7 %shard_map.59 = f32[2,512,256]{2,1,0:T(8,128)S(1)} custom-call(s32[1]{0:T(128)} %bitcast.1.index_ref, bf16[2,1024,4096]{2,1,0:T(8,128)(2,1)} %bitcast.48, bf16[2,4096,512]{2,1,0:T(8,128)(2,1)} %bitcast.52), custom_call_target="tpu_custom_call" | custom-call | flops 4294967296 | bytes 13631488 | tf_op jit(solution)/shard_map/pallas_call | solution.py:156
  58.8 3.3 %collective-permute-done.1 = f32[2,256,512]{1,2,0:T(8,128)S(1)} collective-permute-done((f32[2,256,512]{1,2,0:T(8,128)S(1)}, f32[2,256,512]{1,2,0:T(8,128)S(1)}, u32[]{:S(2)}, u32[]{:S(2)}) %collective-permute-start.1) | collective-permute-done | bytes 1048608 | tf_op jit(solution)/shard_map/ppermute | solution.py:236
  62.3 4.5 %collective-permute-start.2 = (f32[2,256,512]{1,2,0:T(8,128)S(1)}, f32[2,256,512]{1,2,0:T(8,128)S(1)}, u32[]{:S(2)}, u32[]{:S(2)}) collective-permute-start(f32[2,256,512]{1,2,0:T(8,128)S(1)} %bitcast_add_fusion.1), channel_id=1, source_target_pairs={{0,4},{4,8},{8,12},{1,5},{5,9},{9,13},{2,6},{6,10},{10,14},{3,7},{... | collective-permute-start | bytes 3145736 | tf_op jit(solution)/shard_map/ppermute | solution.py:236
  66.9 1.3 %collective-permute-start.4 = (f32[2,256,512]{1,2,0:T(8,128)S(1)}, f32[2,256,512]{1,2,0:T(8,128)S(1)}, u32[]{:S(2)}, u32[]{:S(2)}) collective-permute-start(f32[2,256,512]{1,2,0:T(8,128)S(1)} %bitcast_add_fusion.2), channel_id=1, source_target_pairs={{4,0},{8,4},{12,8},{5,1},{9,5},{13,9},{6,2},{10,6},{14,10},{7,3},{... | collective-permute-start | bytes 3145736 | tf_op jit(solution)/shard_map/ppermute | solution.py:237
  68.2 0.6 dynamic_slice.6
  70.1 17.3 %collective-permute-done.2 = f32[2,256,512]{1,2,0:T(8,128)S(1)} collective-permute-done((f32[2,256,512]{1,2,0:T(8,128)S(1)}, f32[2,256,512]{1,2,0:T(8,128)S(1)}, u32[]{:S(2)}, u32[]{:S(2)}) %collective-permute-start.2) | collective-permute-done | bytes 1048608 | tf_op jit(solution)/shard_map/ppermute | solution.py:236
  87.3 4.3 %collective-permute-done.4 = f32[2,256,512]{1,2,0:T(8,128)S(1)} collective-permute-done((f32[2,256,512]{1,2,0:T(8,128)S(1)}, f32[2,256,512]{1,2,0:T(8,128)S(1)}, u32[]{:S(2)}, u32[]{:S(2)}) %collective-permute-start.4) | collective-permute-done | bytes 1048608 | tf_op jit(solution)/shard_map/ppermute | solution.py:237
  91.7 0.3 fusion.2
  92.4 0.2 subtract_reduce_fusion.1
  92.7 2.3 %collective-permute-done.5 = f32[2,256,8,64]{1,3,2,0:T(8,128)S(1)} collective-permute-done((f32[2,256,8,64]{1,3,2,0:T(8,128)S(1)}, f32[2,256,8,64]{1,3,2,0:T(8,128)S(1)}, u32[]{:S(2)}, u32[]{:S(2)}) %collective-permute-start.5) | collective-permute-done | bytes 1048608 | tf_op jit(solution)/shard_map/ppermute | solution.py:17
  94.9 0.2 broadcast_select_fusion.1
  95.1 0.3 subtract_reduce_fusion
  95.5 1.6 %collective-permute-start.6 = (f32[7,256,1]{1,2,0:T(1,128)S(1)}, f32[7,256,1]{1,2,0:T(1,128)S(1)}, u32[]{:S(2)}, u32[]{:S(2)}) collective-permute-start(f32[7,256,1]{1,2,0:T(1,128)S(1)} %broadcast_select_fusion.4), channel_id=1, source_target_pairs={{0,2},{2,0},{1,3},{3,1},{4,6},{6,4},{5,7},{7,5},{8,10},{10,8},{9,1... | collective-permute-start | bytes 21512 | tf_op jit(solution)/shard_map/ppermute | solution.py:27
  97.1 2.1 %collective-permute-done.6 = f32[7,256,1]{1,2,0:T(1,128)S(1)} collective-permute-done((f32[7,256,1]{1,2,0:T(1,128)S(1)}, f32[7,256,1]{1,2,0:T(1,128)S(1)}, u32[]{:S(2)}, u32[]{:S(2)}) %collective-permute-start.6) | collective-permute-done | bytes 7200 | tf_op jit(solution)/shard_map/ppermute | solution.py:27
  99.3 0.6 slice_divide_fusion
  99.9 0.6 maximum_bitcast_fusion
  (24 shorter events, 0.9 us)
Async XLA Ops:
  0.6 13.1 %copy-start = (s32[4,4]{1,0:T(4,128)S(1)}, s32[4,4]{1,0:T(4,128)}, u32[]{:S(2)}) copy-start(s32[4,4]{1,0:T(4,128)} %constant.52.clone) | copy-start | bytes 196
  8.7 27.4 %collective-permute-start = (f32[2,256,512]{1,2,0:T(8,128)S(1)}, f32[2,256,512]{1,2,0:T(8,128)S(1)}, u32[]{:S(2)}, u32[]{:S(2)}) collective-permute-start(f32[2,256,512]{1,2,0:T(8,128)S(1)} %bitcast.44), channel_id=1, source_target_pairs={{0,4},{12,8},{1,5},{13,9},{2,6},{14,10},{3,7},{15,11},{16,20},{28,... | collective-permute-start | bytes 3145736 | tf_op jit(solution)/shard_map/ppermute | solution.py:233
  36.2 25.9 %collective-permute-start.1 = (f32[2,256,512]{1,2,0:T(8,128)S(1)}, f32[2,256,512]{1,2,0:T(8,128)S(1)}, u32[]{:S(2)}, u32[]{:S(2)}) collective-permute-start(f32[2,256,512]{1,2,0:T(8,128)S(1)} %bitcast_add_fusion), channel_id=1, source_target_pairs={{0,4},{4,8},{1,5},{5,9},{2,6},{6,10},{3,7},{7,11},{16,20},{20,24},... | collective-permute-start | bytes 3145736 | tf_op jit(solution)/shard_map/ppermute | solution.py:236
  40.7 26.1 %collective-permute-start.3 = (f32[2,256,512]{1,2,0:T(8,128)S(1)}, f32[2,256,512]{1,2,0:T(8,128)S(1)}, u32[]{:S(2)}, u32[]{:S(2)}) collective-permute-start(f32[2,256,512]{1,2,0:T(8,128)S(1)} %bitcast_add_fusion), channel_id=1, source_target_pairs={{8,4},{12,8},{9,5},{13,9},{10,6},{14,10},{11,7},{15,11},{24,20},{2... | collective-permute-start | bytes 3145736 | tf_op jit(solution)/shard_map/ppermute | solution.py:237
  50.1 18.1 %copy-start.1 = (s32[4]{0:T(128)S(1)}, s32[4]{0:T(128)}, u32[]{:S(2)}) copy-start(s32[4]{0:T(128)} %constant.53.clone) | copy-start | bytes 52
  62.3 25.1 %collective-permute-start.2 = (f32[2,256,512]{1,2,0:T(8,128)S(1)}, f32[2,256,512]{1,2,0:T(8,128)S(1)}, u32[]{:S(2)}, u32[]{:S(2)}) collective-permute-start(f32[2,256,512]{1,2,0:T(8,128)S(1)} %bitcast_add_fusion.1), channel_id=1, source_target_pairs={{0,4},{4,8},{8,12},{1,5},{5,9},{9,13},{2,6},{6,10},{10,14},{3,7},{... | collective-permute-start | bytes 3145736 | tf_op jit(solution)/shard_map/ppermute | solution.py:236
  66.9 24.8 %collective-permute-start.4 = (f32[2,256,512]{1,2,0:T(8,128)S(1)}, f32[2,256,512]{1,2,0:T(8,128)S(1)}, u32[]{:S(2)}, u32[]{:S(2)}) collective-permute-start(f32[2,256,512]{1,2,0:T(8,128)S(1)} %bitcast_add_fusion.2), channel_id=1, source_target_pairs={{4,0},{8,4},{12,8},{5,1},{9,5},{13,9},{6,2},{10,6},{14,10},{7,3},{... | collective-permute-start | bytes 3145736 | tf_op jit(solution)/shard_map/ppermute | solution.py:237
  92.2 2.7 %collective-permute-start.5 = (f32[2,256,8,64]{1,3,2,0:T(8,128)S(1)}, f32[2,256,8,64]{1,3,2,0:T(8,128)S(1)}, u32[]{:S(2)}, u32[]{:S(2)}) collective-permute-start(f32[2,256,8,64]{1,3,2,0:T(8,128)S(1)} %pad_maximum_fusion), channel_id=1, source_target_pairs={{0,1},{1,0},{2,3},{3,2},{4,5},{5,4},{6,7},{7,6},{8,9},{9,8},{10,11... | collective-permute-start | bytes 3145736 | tf_op jit(solution)/shard_map/ppermute | solution.py:17
  95.5 3.7 %collective-permute-start.6 = (f32[7,256,1]{1,2,0:T(1,128)S(1)}, f32[7,256,1]{1,2,0:T(1,128)S(1)}, u32[]{:S(2)}, u32[]{:S(2)}) collective-permute-start(f32[7,256,1]{1,2,0:T(1,128)S(1)} %broadcast_select_fusion.4), channel_id=1, source_target_pairs={{0,2},{2,0},{1,3},{3,1},{4,6},{6,4},{5,7},{7,5},{8,10},{10,8},{9,1... | collective-permute-start | bytes 21512 | tf_op jit(solution)/shard_map/ppermute | solution.py:27
